TPU v7x, 128 devices: a whole 4x4x4 slice. The times are simulated.
128 devices in a mesh: grp: 4 (over z), shard: 32 (over y, x, core).
Axes of the slice: x: 4, y: 4, z: 4, core: 2. Of those that a mesh axis runs over, the one named last changes fastest.
Arguments:
- users: float32 [65536, 128], P(('grp', 'shard')), may hold values from -2 to 2
- user_accum: float32 [65536, 128], P(('grp', 'shard')), may hold values from 100 to 3000
- positives: int32 [65536, 16], P(('grp', 'shard')), may hold values from 0 to 32767
- hot_table: float32 [32768, 128], P('shard'), may hold values from -2 to 2
- hot_accum: float32 [32768, 128], P('shard'), may hold values from 100 to 3000
- cold_table: float32 [131072, 128], P(('grp', 'shard')), may hold values from -2 to 2
- cold_accum: float32 [131072, 128], P(('grp', 'shard')), may hold values from 4 to 100
- cold_requests: int32 [128, 128, 128], P(('grp', 'shard')), may hold values from 0 to 1023
- cold_counts: int32 [128, 128], P(('grp', 'shard')), may hold values from 1 to 128, as said below
Outputs:
- new_users: float32 [65536, 128], P(('grp', 'shard'))
- new_user_accum: float32 [65536, 128], P(('grp', 'shard'))
- new_hot: float32 [32768, 128], P('shard')
- new_hot_accum: float32 [32768, 128], P('shard')
- new_cold: float32 [131072, 128], P(('grp', 'shard'))
- new_cold_accum: float32 [131072, 128], P(('grp', 'shard'))
Inputs may be any that keep to these rules, and one draw needn't show every extreme that they name: Slots s < cold_counts[d, o] of block (d, o) are live, the rest are padding. Every device has an owner of which it asks 128 live rows, and in every draw one owner receives 128 live rows from every device.
All inputs are finite; a program needn't handle non-finite values.
Results may differ from a plain program's by a relative error of at most 0.0089.
Values may be sent and summed in bfloat16 or wider, within the bound.
No kernel may reach another device: no remote copies, remote signals or barrier semaphores. Data moves between devices by JAX's collectives and lax.ppermute only.
A program may use at most 192 MiB of HBM per device.

v0:
```python
import jax
import jax.numpy as jnp
from jax import lax
from jax.sharding import PartitionSpec as P

POSITIVE_WEIGHT = 32.0
LEARN_RATE = 0.5


def hot_terms(user_rows, pos_rows, item_rows, item_first):
    item_ids = item_first + lax.iota(jnp.int32, item_rows.shape[0])
    matches = jnp.sum((pos_rows[:, :, None] == item_ids[None, None, :]).astype(jnp.float32), axis=1)
    scores = jnp.einsum("uk,ik->ui", user_rows, item_rows, preferred_element_type=jnp.float32)
    weights = (
        (1.0 + POSITIVE_WEIGHT * matches) * jax.nn.sigmoid(scores) - POSITIVE_WEIGHT * matches
    ).astype(jnp.bfloat16)
    user_part = jnp.dot(weights, item_rows, preferred_element_type=jnp.float32)
    item_part = jnp.einsum("ui,uk->ik", weights, user_rows, preferred_element_type=jnp.float32)
    return (user_part, item_part)


def adagrad(current, history, gradient):
    updated = history + gradient * gradient
    return (current - LEARN_RATE * gradient / jnp.sqrt(updated), updated)


def body(
    users,
    user_accum,
    positives,
    hot_table,
    hot_accum,
    cold_table,
    cold_accum,
    cold_requests,
    cold_counts,
):
    user_half = users.astype(jnp.bfloat16)
    hot_half = hot_table.astype(jnp.bfloat16)
    cold_half = cold_table.astype(jnp.bfloat16)
    feature_count = users.shape[1]
    local_users = users.shape[0]
    hot_all = lax.all_gather(hot_half, "shard", axis=0, tiled=True)
    item_total = hot_all.shape[0]
    block_rows = 4096
    turns = item_total // block_rows
    stacked = hot_all.reshape(turns, block_rows, feature_count)

    def item_step(running, inputs):
        item_rows, position = inputs
        user_part, item_part = hot_terms(user_half, positives, item_rows, position * block_rows)
        return (running + user_part, item_part)

    user_hot, item_parts = lax.scan(
        item_step,
        jnp.zeros((local_users, feature_count), jnp.float32),
        (stacked, lax.iota(jnp.int32, turns)),
    )
    item_grad = lax.psum_scatter(
        item_parts.reshape(item_total, feature_count), "shard", scatter_dimension=0, tiled=True
    )
    hot_grad = lax.psum(item_grad, "grp")
    devices = cold_requests.shape[1]
    slot_count = cold_requests.shape[2]
    requests = cold_requests.reshape(devices, slot_count)
    live_slots = lax.iota(jnp.int32, slot_count)[None, :] < cold_counts.reshape(devices, 1)
    asked_rows = lax.all_to_all(requests, ("grp", "shard"), split_axis=0, concat_axis=0, tiled=True)
    found = jnp.take(cold_half, asked_rows, axis=0)
    fetched, asked_rows = (
        lax.all_to_all(found, ("grp", "shard"), split_axis=0, concat_axis=0, tiled=True),
        asked_rows,
    )
    flat_rows = fetched.reshape(devices * slot_count, feature_count)
    scores = jnp.einsum("uk,rk->ur", user_half, flat_rows, preferred_element_type=jnp.float32)
    weights = (jax.nn.sigmoid(scores) * live_slots.reshape(1, -1).astype(jnp.float32)).astype(
        jnp.bfloat16
    )
    user_cold = jnp.dot(weights, flat_rows, preferred_element_type=jnp.float32)
    row_terms = jnp.einsum(
        "ur,uk->rk", weights, user_half, preferred_element_type=jnp.float32
    ).astype(jnp.bfloat16)
    row_terms = row_terms.reshape(devices, slot_count, feature_count)
    returned = lax.all_to_all(row_terms, ("grp", "shard"), split_axis=0, concat_axis=0, tiled=True)
    cold_grad = (
        jnp.zeros(cold_table.shape, jnp.float32)
        .at[asked_rows.reshape(-1)]
        .add(returned.reshape(devices * slot_count, feature_count).astype(jnp.float32))
    )
    user_grad = user_hot + user_cold
    new_users, new_user_accum = adagrad(users, user_accum, user_grad)
    new_hot, new_hot_accum = adagrad(hot_table, hot_accum, hot_grad)
    new_cold, new_cold_accum = adagrad(cold_table, cold_accum, cold_grad)
    return (new_users, new_user_accum, new_hot, new_hot_accum, new_cold, new_cold_accum)


def solution(mesh):
    return jax.shard_map(
        body,
        mesh=mesh,
        in_specs=(
            P(("grp", "shard"), None),
            P(("grp", "shard"), None),
            P(("grp", "shard"), None),
            P("shard", None),
            P("shard", None),
            P(("grp", "shard"), None),
            P(("grp", "shard"), None),
            P(("grp", "shard"), None, None),
            P(("grp", "shard"), None),
        ),
        out_specs=(
            P(("grp", "shard"), None),
            P(("grp", "shard"), None),
            P("shard", None),
            P("shard", None),
            P(("grp", "shard"), None),
            P(("grp", "shard"), None),
        ),
        check_vma=False,
    )
```

profile of v0, /device:TPU:0, one launch (start us, length us, event | category | flops | bytes accessed | tf_op | source)
XLA Modules:
  0.0 894.0 jit_solution(7626240216614543341)
XLA Ops:
  7.2 1.8 convert_element_type.38
  9.1 0.9 copy.19
  10.0 1.0 convert_element_type.39
  10.9 55.0 %all-gather.2.cloned.1.call-done = bf16[32768,128]{1,0:T(8,128)(2,1)} async-done(((bf16[1024,128]{1,0:T(8,128)(2,1)}), bf16[32768,128]{1,0:T(8,128)(2,1)}) %all-gather.2.cloned.1.call-update) | async-done | bytes 8388624 | tf_op jit(solution)/shard_map/all_gather | solution.py:43
  66.0 465.3 %while.13 = (s32[]{:T(128)}, f32[512,128]{1,0:T(8,128)S(1)}, f32[8,4096,128]{2,1,0:T(8,128)}, s32[512,16]{1,0:T(8,128)S(1)}, s32[8]{0:T(128)S(1)}, /*index=5*/bf...) while((s32[]{:T(128)}, f32[512,128]{1,0:T(8,128)S(1)}, ...), condition=%wide.region_2.3_spmd.clone, body=%wide.region_0.2_spmd.clone.sunk | while | flops 1726091264 | bytes 51183772 | solution.py:54
  66.0 0.6 dynamic_slice.23
  67.2 32.5 %convert_reduce_fusion.2 = f32[512,4096]{1,0:T(8,128)} fusion(s32[4096]{0:T(1024)S(1)} %iota_add_fusion.2, s32[512,16]{1,0:T(8,128)S(1)} %get-tuple-element.163), kind=kLoop, calls=%fused_computation.2.clone.1 | loop fusion | flops 98566144 | bytes 8437760 | tf_op jit(solution)/shard_map/while/body/eval_jaxpr/reduce_sum | solution.py:12
  99.7 9.0 %copy.21 = f32[512,4096]{0,1:T(8,128)} copy(f32[512,4096]{1,0:T(8,128)} %convert_reduce_fusion.2) | data formatting | bytes 16777216 | tf_op jit(solution)/shard_map/while/body/eval_jaxpr/reduce_sum | solution.py:12
  108.7 6.8 fusion.38
  115.5 3.8 convolution_add_fusion.3
  119.4 4.8 fusion.39
  124.1 0.6 dynamic_slice.23
  125.4 32.5 %convert_reduce_fusion.2 = f32[512,4096]{1,0:T(8,128)} fusion(s32[4096]{0:T(1024)S(1)} %iota_add_fusion.2, s32[512,16]{1,0:T(8,128)S(1)} %get-tuple-element.163), kind=kLoop, calls=%fused_computation.2.clone.1 | loop fusion | flops 98566144 | bytes 8437760 | tf_op jit(solution)/shard_map/while/body/eval_jaxpr/reduce_sum | solution.py:12
  157.9 9.0 %copy.21 = f32[512,4096]{0,1:T(8,128)} copy(f32[512,4096]{1,0:T(8,128)} %convert_reduce_fusion.2) | data formatting | bytes 16777216 | tf_op jit(solution)/shard_map/while/body/eval_jaxpr/reduce_sum | solution.py:12
  166.9 6.8 fusion.38
  173.7 3.8 convolution_add_fusion.3
  177.5 4.8 fusion.39
  183.5 32.5 %convert_reduce_fusion.2 = f32[512,4096]{1,0:T(8,128)} fusion(s32[4096]{0:T(1024)S(1)} %iota_add_fusion.2, s32[512,16]{1,0:T(8,128)S(1)} %get-tuple-element.163), kind=kLoop, calls=%fused_computation.2.clone.1 | loop fusion | flops 98566144 | bytes 8437760 | tf_op jit(solution)/shard_map/while/body/eval_jaxpr/reduce_sum | solution.py:12
  216.0 9.0 %copy.21 = f32[512,4096]{0,1:T(8,128)} copy(f32[512,4096]{1,0:T(8,128)} %convert_reduce_fusion.2) | data formatting | bytes 16777216 | tf_op jit(solution)/shard_map/while/body/eval_jaxpr/reduce_sum | solution.py:12
  225.0 6.8 fusion.38
  231.8 3.8 convolution_add_fusion.3
  235.7 4.8 fusion.39
  241.7 32.5 %convert_reduce_fusion.2 = f32[512,4096]{1,0:T(8,128)} fusion(s32[4096]{0:T(1024)S(1)} %iota_add_fusion.2, s32[512,16]{1,0:T(8,128)S(1)} %get-tuple-element.163), kind=kLoop, calls=%fused_computation.2.clone.1 | loop fusion | flops 98566144 | bytes 8437760 | tf_op jit(solution)/shard_map/while/body/eval_jaxpr/reduce_sum | solution.py:12
  274.2 9.0 %copy.21 = f32[512,4096]{0,1:T(8,128)} copy(f32[512,4096]{1,0:T(8,128)} %convert_reduce_fusion.2) | data formatting | bytes 16777216 | tf_op jit(solution)/shard_map/while/body/eval_jaxpr/reduce_sum | solution.py:12
  283.2 6.8 fusion.38
  290.0 3.8 convolution_add_fusion.3
  293.8 4.8 fusion.39
  298.6 0.6 dynamic_slice.23
  299.8 32.5 %convert_reduce_fusion.2 = f32[512,4096]{1,0:T(8,128)} fusion(s32[4096]{0:T(1024)S(1)} %iota_add_fusion.2, s32[512,16]{1,0:T(8,128)S(1)} %get-tuple-element.163), kind=kLoop, calls=%fused_computation.2.clone.1 | loop fusion | flops 98566144 | bytes 8437760 | tf_op jit(solution)/shard_map/while/body/eval_jaxpr/reduce_sum | solution.py:12
  332.4 9.0 %copy.21 = f32[512,4096]{0,1:T(8,128)} copy(f32[512,4096]{1,0:T(8,128)} %convert_reduce_fusion.2) | data formatting | bytes 16777216 | tf_op jit(solution)/shard_map/while/body/eval_jaxpr/reduce_sum | solution.py:12
  341.4 6.8 fusion.38
  348.2 3.8 convolution_add_fusion.3
  352.0 4.8 fusion.39
  358.1 32.5 %convert_reduce_fusion.2 = f32[512,4096]{1,0:T(8,128)} fusion(s32[4096]{0:T(1024)S(1)} %iota_add_fusion.2, s32[512,16]{1,0:T(8,128)S(1)} %get-tuple-element.163), kind=kLoop, calls=%fused_computation.2.clone.1 | loop fusion | flops 98566144 | bytes 8437760 | tf_op jit(solution)/shard_map/while/body/eval_jaxpr/reduce_sum | solution.py:12
  390.6 9.0 %copy.21 = f32[512,4096]{0,1:T(8,128)} copy(f32[512,4096]{1,0:T(8,128)} %convert_reduce_fusion.2) | data formatting | bytes 16777216 | tf_op jit(solution)/shard_map/while/body/eval_jaxpr/reduce_sum | solution.py:12
  399.6 6.8 fusion.38
  406.4 3.8 convolution_add_fusion.3
  410.2 4.8 fusion.39
  416.2 32.5 %convert_reduce_fusion.2 = f32[512,4096]{1,0:T(8,128)} fusion(s32[4096]{0:T(1024)S(1)} %iota_add_fusion.2, s32[512,16]{1,0:T(8,128)S(1)} %get-tuple-element.163), kind=kLoop, calls=%fused_computation.2.clone.1 | loop fusion | flops 98566144 | bytes 8437760 | tf_op jit(solution)/shard_map/while/body/eval_jaxpr/reduce_sum | solution.py:12
  448.7 9.0 %copy.21 = f32[512,4096]{0,1:T(8,128)} copy(f32[512,4096]{1,0:T(8,128)} %convert_reduce_fusion.2) | data formatting | bytes 16777216 | tf_op jit(solution)/shard_map/while/body/eval_jaxpr/reduce_sum | solution.py:12
  457.7 6.8 fusion.38
  464.5 3.8 convolution_add_fusion.3
  468.4 4.8 fusion.39
  473.1 0.6 dynamic_slice.23
  474.4 32.5 %convert_reduce_fusion.2 = f32[512,4096]{1,0:T(8,128)} fusion(s32[4096]{0:T(1024)S(1)} %iota_add_fusion.2, s32[512,16]{1,0:T(8,128)S(1)} %get-tuple-element.163), kind=kLoop, calls=%fused_computation.2.clone.1 | loop fusion | flops 98566144 | bytes 8437760 | tf_op jit(solution)/shard_map/while/body/eval_jaxpr/reduce_sum | solution.py:12
  506.9 9.0 %copy.21 = f32[512,4096]{0,1:T(8,128)} copy(f32[512,4096]{1,0:T(8,128)} %convert_reduce_fusion.2) | data formatting | bytes 16777216 | tf_op jit(solution)/shard_map/while/body/eval_jaxpr/reduce_sum | solution.py:12
  515.9 6.8 fusion.38
  522.7 3.8 convolution_add_fusion.3
  526.5 4.7 fusion.39
  531.3 8.3 all-to-all-start
  539.7 9.2 %all-to-all-done = s32[128,1,128]{2,1,0:T(1,128)S(1)} async-done(((s32[128,1,128]{2,1,0:T(1,128)}), s32[128,1,128]{2,1,0:T(1,128)S(1)}, u32[]{:S(2)}, u32[]{:S(2)}) %all-to-all-start) | async-done | bytes 65568 | tf_op jit(solution)/shard_map/all_to_all | solution.py:67
  548.9 57.4 %gather_fusion = bf16[16384,128]{1,0:T(8,128)(2,1)} fusion(bf16[1024,128]{1,0:T(8,128)(2,1)S(1)} %convert_element_type.40, s32[16384]{0:T(1024)S(1)} %fusion.13), kind=kCustom, calls=%fused_computation | custom fusion | bytes 8454144 | tf_op jit(solution)/shard_map/jit(_take)/gather | solution.py:68
  606.3 7.7 broadcast_select_fusion
  614.0 6.0 all-to-all-start.1
  620.2 60.5 %all-to-all-done.1 = bf16[128,128,128]{2,1,0:T(8,128)(2,1)} async-done(((bf16[128,128,128]{2,1,0:T(8,128)(2,1)}), bf16[128,128,128]{2,1,0:T(8,128)(2,1)}, u32[]{:S(2)}, u32[]{:S(2)}) %all-to-all-start.1) | async-done | bytes 4194336 | tf_op jit(solution)/shard_map/all_to_all | solution.py:70
  680.7 10.9 %multiply_convert_fusion = bf16[16384,512]{1,0:T(8,128)(2,1)S(1)} fusion(bf16[16384,128]{1,0:T(8,128)(2,1)} %bitcast.6, bf16[512,128]{1,0:T(8,128)(2,1)S(1)} %get-tuple-element.179, f32[16384]{0:T(1024)S(1)} %convert_bitcast_fusion), kind=kOutput, calls=%fused_computation.16 | convolution fusion | flops 2189426688 | bytes 21168128 | tf_op jit(solution)/shard_map/uk,rk->ur/dot_general | solution.py:74
  691.6 6.8 convolution_convert_fusion
  698.6 6.0 all-to-all-start.2
  704.7 52.3 %all-to-all-done.2 = bf16[128,128,128]{2,1,0:T(8,128)(2,1)} async-done(((bf16[128,128,128]{2,1,0:T(8,128)(2,1)}), bf16[128,128,128]{2,1,0:T(8,128)(2,1)}, u32[]{:S(2)}, u32[]{:S(2)}) %all-to-all-start.2) | async-done | bytes 4194336 | tf_op jit(solution)/shard_map/all_to_all | solution.py:83
  757.0 88.5 %scatter_custom_fusion = f32[1024,128]{1,0:T(8,128)S(1)} fusion(s32[16384]{0:T(1024)S(1)} %bitcast.70, bf16[16384,128]{1,0:T(8,128)(2,1)} %bitcast.18, f32[]{:T(128)} %constant.25.clone.1), kind=kCustom, calls=%fused_computation.18 | custom fusion | flops 4194304 | bytes 4718596 | tf_op jit(solution)/shard_map/scatter-add | solution.py:87
  845.5 1.1 multiply_subtract_fusion
  846.6 12.5 %multiply_subtract_fusion.2 = (f32[512,128]{1,0:T(8,128)}, f32[512,128]{1,0:T(8,128)}) fusion(f32[512,128]{1,0:T(8,128)S(1)} %copy-done.5, f32[512,128]{1,0:T(8,128)S(1)} %copy-done.7, f32[512,128]{1,0:T(8,128)S(1)} %get-tuple-element.44, bf16[16384,512]{1,0:T(8,128)(2,1)} %copy-done, bf16[16384,128]{1,0:T(8,128)(2,1)} %bitcast.6), kind=kOutput, calls=%fused_computation.28 | convolution fusion | flops 2147876864 | bytes 22282240 | tf_op jit(solution)/shard_map/dot_general | solution.py:78
  859.1 26.2 %all-reduce.2.cloned.1.call-done = f32[1024,128]{1,0:T(8,128)} async-done(((f32[1024,128]{1,0:T(8,128)}), f32[1024,128]{1,0:T(8,128)}) %all-reduce.2.cloned.1.call-update) | async-done | bytes 524304 | tf_op jit(solution)/shard_map/psum | solution.py:62
  885.4 2.1 multiply_subtract_fusion.1
  (43 shorter events, 3.0 us)
Async XLA Ops:
  7.2 58.8 %all-gather.2.cloned.1.call-start = ((), (), s32[]{:S(2)}) async-start(), calls=%async_computation.4 | async-start | bytes 8650752 | tf_op jit(solution)/shard_map/all_gather | solution.py:43
  9.0 837.5 %reduce-scatter.2.cloned.1.call-start = ((), (), s32[]{:S(2)}) async-start(), calls=%async_computation.5 | async-start | bytes 17301504 | tf_op jit(solution)/shard_map/reduce_scatter | solution.py:59
  531.3 8.3 copy-start.1
  531.3 17.6 %all-to-all-start = ((s32[128,1,128]{2,1,0:T(1,128)}), s32[128,1,128]{2,1,0:T(1,128)S(1)}, u32[]{:S(2)}, u32[]{:S(2)}) async-start(s32[128,1,128]{2,1,0:T(1,128)} %bitcast.1), calls=%async_computation | async-start | bytes 131072 | tf_op jit(solution)/shard_map/all_to_all | solution.py:67
  606.3 13.7 %copy-start.6 = (s32[1,128]{1,0:T(1,128)S(1)}, s32[1,128]{1,0:T(1,128)}, u32[]{:S(2)}) copy-start(s32[1,128]{1,0:T(1,128)} %param.19) | copy-start | bytes 1540
  614.0 66.7 %all-to-all-start.1 = ((bf16[128,128,128]{2,1,0:T(8,128)(2,1)}), bf16[128,128,128]{2,1,0:T(8,128)(2,1)}, u32[]{:S(2)}, u32[]{:S(2)}) async-start(bf16[128,128,128]{2,1,0:T(8,128)(2,1)} %broadcast_select_fusion), calls=%async_computation.1 | async-start | bytes 8388608 | tf_op jit(solution)/shard_map/all_to_all | solution.py:70
  691.6 7.0 copy-start
  698.6 146.9 %copy-start.3 = (f32[1024,128]{1,0:T(8,128)S(1)}, f32[1024,128]{1,0:T(8,128)}, u32[]{:S(2)}) copy-start(f32[1024,128]{1,0:T(8,128)} %param.17) | copy-start | bytes 1572868
  698.6 148.0 %copy-start.5 = (f32[512,128]{1,0:T(8,128)S(1)}, f32[512,128]{1,0:T(8,128)}, u32[]{:S(2)}) copy-start(f32[512,128]{1,0:T(8,128)} %param.11) | copy-start | bytes 786436
  698.6 148.0 %copy-start.7 = (f32[512,128]{1,0:T(8,128)S(1)}, f32[512,128]{1,0:T(8,128)}, u32[]{:S(2)}) copy-start(f32[512,128]{1,0:T(8,128)} %param.12) | copy-start | bytes 786436
  698.6 58.4 %all-to-all-start.2 = ((bf16[128,128,128]{2,1,0:T(8,128)(2,1)}), bf16[128,128,128]{2,1,0:T(8,128)(2,1)}, u32[]{:S(2)}, u32[]{:S(2)}) async-start(bf16[128,128,128]{2,1,0:T(8,128)(2,1)} %bitcast.64), calls=%async_computation.3 | async-start | bytes 8388608 | tf_op jit(solution)/shard_map/all_to_all | solution.py:83
  704.5 180.8 %all-reduce.2.cloned.1.call-start = ((), (), s32[]{:S(2)}) async-start(), calls=%async_computation.6 | async-start | bytes 1048576 | tf_op jit(solution)/shard_map/psum | solution.py:62
  846.6 38.8 %copy-start.2 = (f32[1024,128]{1,0:T(8,128)S(1)}, f32[1024,128]{1,0:T(8,128)}, u32[]{:S(2)}) copy-start(f32[1024,128]{1,0:T(8,128)} %param.14) | copy-start | bytes 1572868
  846.6 38.8 %copy-start.4 = (f32[1024,128]{1,0:T(8,128)S(1)}, f32[1024,128]{1,0:T(8,128)}, u32[]{:S(2)}) copy-start(f32[1024,128]{1,0:T(8,128)} %param.15) | copy-start | bytes 1572868
Sparse Core Ops, SparseCore 0:
  10.8 55.1 all-gather.1
  531.4 141.6 reduce-scatter.1
  846.7 38.6 all-reduce.1
where the time goes:
time: 897 us; the launch traced here: 894 us
  other arithmetic  363 us (40%)
  waiting for transfers between devices  203 us (23%)
  matrix products  153 us (17%)
  local copies, waits for them, and re-layouts  135 us (15%)
  starting transfers between devices  20.4 us (2%)
  between operations  13.9 us (2%)
    reduce_sum x8, other arithmetic, hot_terms(): jnp.sum((pos_rows[:, :, None] == item_ids[None, None, :]).astype(jnp.floa...  260 us
    scatter-add x1, other arithmetic, body(): cold_grad = jnp.zeros(cold_table.shape, jnp.float32).at[asked_rows.reshap...  88.5 us
    reduce_sum x8, local copies, waits for them, and re-layouts, hot_terms(): jnp.sum((pos_rows[:, :, None] == item_ids[None, None, :]).astype(jnp.floa...  72 us
    all_to_all x1, waiting for transfers between devices, body(): lax.all_to_all(found, ('grp', 'shard'), split_axis=0, concat_axis=0, tile...  60.5 us
    gather x1, local copies, waits for them, and re-layouts, body(): found = jnp.take(cold_half, asked_rows, axis=0)  57.4 us
    all_gather x1, waiting for transfers between devices, body(): hot_all = lax.all_gather(hot_half, 'shard', axis=0, tiled=True)  55 us
    dot_general x8, matrix products, hot_terms(): jnp.einsum('uk,ik->ui', user_rows, item_rows, preferred_element_type=jnp....  54.4 us
    all_to_all x1, waiting for transfers between devices, body(): lax.all_to_all(row_terms, ('grp', 'shard'), split_axis=0, concat_axis=0,...  52.3 us
  transfers between devices with their start and end apart: 6, of which 5 were waited for; matrix products, arithmetic and copies ran while one was open for 21% of the time, Pallas kernels for 0%

commit v1 on v0

v1 whole, which is shorter than its diff:
```python
import functools

import jax
import jax.numpy as jnp
from jax import lax
from jax.experimental import pallas as pl
from jax.experimental.pallas import tpu as pltpu
from jax.sharding import PartitionSpec as P

POSITIVE_WEIGHT = 32.0
LEARN_RATE = 0.5
LANES = 128
SUB = 8


def _nt(a, b):
    return lax.dot_general(a, b, (((1,), (1,)), ((), ())), preferred_element_type=jnp.float32)


def _tn(a, b):
    return lax.dot_general(a, b, (((0,), (0,)), ((), ())), preferred_element_type=jnp.float32)


def _hot_kernel(u_ref, h_ref, ph_ref, ol_ref, up_ref, ip_ref, m_ref):
    j = pl.program_id(0)
    block = h_ref.shape[0]
    nh = block // LANES
    subtiles = ph_ref.shape[0]
    per = LANES // SUB
    r = lax.broadcasted_iota(jnp.int32, (nh * SUB, LANES), 0)
    c = lax.broadcasted_iota(jnp.int32, (nh * SUB, LANES), 1)
    diag = (r % SUB) == (c // per)
    hrow = r // SUB + j * nh

    def sub(s, carry):
        ph = ph_ref[pl.ds(s, 1), :]
        lhs = jnp.where(diag & (ph == hrow), 1.0, 0.0).astype(jnp.bfloat16)
        out = _nt(lhs, ol_ref[s])
        base = pl.multiple_of(s * SUB, SUB)
        for h in range(nh):
            m_ref[pl.ds(base, SUB), pl.ds(h * LANES, LANES)] = out[h * SUB:(h + 1) * SUB, :]
        return carry

    lax.fori_loop(0, subtiles, sub, 0)
    u = u_ref[...]
    hj = h_ref[...]
    scores = _nt(u, hj)
    m = m_ref[...]
    w = ((1.0 + POSITIVE_WEIGHT * m) * jax.nn.sigmoid(scores) - POSITIVE_WEIGHT * m).astype(
        jnp.bfloat16
    )

    @pl.when(j == 0)
    def _():
        up_ref[...] = jnp.zeros_like(up_ref)

    up_ref[...] += jnp.dot(w, hj, preferred_element_type=jnp.float32)
    ip_ref[...] = _tn(w, u)


def hot_terms(user_half, positives, hot_all, block=2048):
    users, k = user_half.shape
    items = hot_all.shape[0]
    pos_count = positives.shape[1]
    subtiles = users // SUB
    assert SUB * pos_count == LANES
    pos_hi = (positives // LANES).reshape(subtiles, LANES)
    pos_lo = (positives % LANES).reshape(subtiles, 1, LANES)
    onehot_lo = (pos_lo == lax.broadcasted_iota(jnp.int32, (1, LANES, 1), 1)).astype(jnp.bfloat16)
    return pl.pallas_call(
        _hot_kernel,
        grid=(items // block,),
        in_specs=[
            pl.BlockSpec((users, k), lambda j: (0, 0)),
            pl.BlockSpec((block, k), lambda j: (j, 0)),
            pl.BlockSpec((subtiles, LANES), lambda j: (0, 0)),
            pl.BlockSpec((subtiles, LANES, LANES), lambda j: (0, 0, 0)),
        ],
        out_specs=[
            pl.BlockSpec((users, k), lambda j: (0, 0)),
            pl.BlockSpec((block, k), lambda j: (j, 0)),
        ],
        out_shape=[
            jax.ShapeDtypeStruct((users, k), jnp.float32),
            jax.ShapeDtypeStruct((items, k), jnp.float32),
        ],
        scratch_shapes=[pltpu.VMEM((users, block), jnp.float32)],
        compiler_params=pltpu.CompilerParams(dimension_semantics=("arbitrary",)),
    )(user_half, hot_all, pos_hi, onehot_lo)


def _gather_kernel(idx_ref, table_ref, out_ref):
    rows = table_ref.shape[0]
    onehot = (idx_ref[...] == lax.broadcasted_iota(jnp.int32, (1, rows), 1)).astype(jnp.bfloat16)
    out_ref[...] = jnp.dot(onehot, table_ref[...], preferred_element_type=jnp.float32).astype(
        out_ref.dtype
    )


def onehot_gather(table, idx, chunk=1024):
    rows, k = table.shape
    n = idx.shape[0]
    return pl.pallas_call(
        _gather_kernel,
        grid=(n // chunk,),
        in_specs=[
            pl.BlockSpec((chunk, 1), lambda i: (i, 0)),
            pl.BlockSpec((rows, k), lambda i: (0, 0)),
        ],
        out_specs=pl.BlockSpec((chunk, k), lambda i: (i, 0)),
        out_shape=jax.ShapeDtypeStruct((n, k), table.dtype),
    )(idx.reshape(n, 1), table)


def _scatter_kernel(idx_ref, val_ref, out_ref):
    i = pl.program_id(0)
    rows = out_ref.shape[0]
    chunk = idx_ref.shape[1]
    onehot = (idx_ref[...] == lax.broadcasted_iota(jnp.int32, (rows, chunk), 0)).astype(
        jnp.bfloat16
    )

    @pl.when(i == 0)
    def _():
        out_ref[...] = jnp.zeros_like(out_ref)

    out_ref[...] += jnp.dot(onehot, val_ref[...], preferred_element_type=jnp.float32)


def onehot_scatter_add(idx, values, rows, chunk=1024):
    n, k = values.shape
    return pl.pallas_call(
        _scatter_kernel,
        grid=(n // chunk,),
        in_specs=[
            pl.BlockSpec((1, chunk), lambda i: (0, i)),
            pl.BlockSpec((chunk, k), lambda i: (i, 0)),
        ],
        out_specs=pl.BlockSpec((rows, k), lambda i: (0, 0)),
        out_shape=jax.ShapeDtypeStruct((rows, k), jnp.float32),
        compiler_params=pltpu.CompilerParams(dimension_semantics=("arbitrary",)),
    )(idx.reshape(1, n), values)


def adagrad(current, history, gradient):
    updated = history + gradient * gradient
    return (current - LEARN_RATE * gradient / jnp.sqrt(updated), updated)


def body(
    users,
    user_accum,
    positives,
    hot_table,
    hot_accum,
    cold_table,
    cold_accum,
    cold_requests,
    cold_counts,
):
    user_half = users.astype(jnp.bfloat16)
    hot_half = hot_table.astype(jnp.bfloat16)
    cold_half = cold_table.astype(jnp.bfloat16)
    feature_count = users.shape[1]
    hot_all = lax.all_gather(hot_half, "shard", axis=0, tiled=True)
    item_total = hot_all.shape[0]
    user_hot, item_parts = hot_terms(user_half, positives, hot_all)
    item_grad = lax.psum_scatter(item_parts, "shard", scatter_dimension=0, tiled=True)
    hot_grad = lax.psum(item_grad, "grp")
    devices = cold_requests.shape[1]
    slot_count = cold_requests.shape[2]
    requests = cold_requests.reshape(devices, slot_count)
    live_slots = lax.iota(jnp.int32, slot_count)[None, :] < cold_counts.reshape(devices, 1)
    asked_rows = lax.all_to_all(requests, ("grp", "shard"), split_axis=0, concat_axis=0, tiled=True)
    found = onehot_gather(cold_half, asked_rows.reshape(-1))
    fetched = lax.all_to_all(
        found.reshape(devices, slot_count, feature_count),
        ("grp", "shard"),
        split_axis=0,
        concat_axis=0,
        tiled=True,
    )
    flat_rows = fetched.reshape(devices * slot_count, feature_count)
    scores = jnp.einsum("uk,rk->ur", user_half, flat_rows, preferred_element_type=jnp.float32)
    weights = (jax.nn.sigmoid(scores) * live_slots.reshape(1, -1).astype(jnp.float32)).astype(
        jnp.bfloat16
    )
    user_cold = jnp.dot(weights, flat_rows, preferred_element_type=jnp.float32)
    row_terms = jnp.einsum(
        "ur,uk->rk", weights, user_half, preferred_element_type=jnp.float32
    ).astype(jnp.bfloat16)
    row_terms = row_terms.reshape(devices, slot_count, feature_count)
    returned = lax.all_to_all(row_terms, ("grp", "shard"), split_axis=0, concat_axis=0, tiled=True)
    cold_grad = onehot_scatter_add(
        asked_rows.reshape(-1),
        returned.reshape(devices * slot_count, feature_count),
        cold_table.shape[0],
    )
    user_grad = user_hot + user_cold
    new_users, new_user_accum = adagrad(users, user_accum, user_grad)
    new_hot, new_hot_accum = adagrad(hot_table, hot_accum, hot_grad)
    new_cold, new_cold_accum = adagrad(cold_table, cold_accum, cold_grad)
    return (new_users, new_user_accum, new_hot, new_hot_accum, new_cold, new_cold_accum)


def solution(mesh):
    return jax.shard_map(
        body,
        mesh=mesh,
        in_specs=(
            P(("grp", "shard"), None),
            P(("grp", "shard"), None),
            P(("grp", "shard"), None),
            P("shard", None),
            P("shard", None),
            P(("grp", "shard"), None),
            P(("grp", "shard"), None),
            P(("grp", "shard"), None, None),
            P(("grp", "shard"), None),
        ),
        out_specs=(
            P(("grp", "shard"), None),
            P(("grp", "shard"), None),
            P("shard", None),
            P("shard", None),
            P(("grp", "shard"), None),
            P(("grp", "shard"), None),
        ),
        check_vma=False,
    )
```

time: 897 us -> 536 us (0.60)
  other arithmetic: 363 us -> 11.3 us
  Pallas kernels: 0 us -> 238 us
  local copies, waits for them, and re-layouts: 135 us -> 7.05 us
  matrix products: 153 us -> 28.2 us
  blocking collectives: 0 us -> 62.8 us
  waiting for transfers between devices: 203 us -> 160 us
    reduce_sum x8 -> x0, other arithmetic: 260 us -> none  [hot_terms(): jnp.sum((pos_rows[:, :, None] == item_ids[None, None, :]).astype(jnp.floa...]
    pallas_call x0 -> x3, Pallas kernels: none -> 238 us  [the longest x1 199 us: hot_terms(): pl.pallas_call(_hot_kernel, grid=(items // block,), in_specs=[pl.BlockSpe...]
    dot_general x24 -> x0, matrix products: 123 us -> none  [the longest x8 54.4 us: hot_terms(): jnp.einsum('uk,ik->ui', user_rows, item_rows, preferred_element_type=jnp....]
    scatter-add x1 -> x0, other arithmetic: 88.5 us -> none  [body(): cold_grad = jnp.zeros(cold_table.shape, jnp.float32).at[asked_rows.reshap...]
    reduce_sum x8 -> x0, local copies, waits for them, and re-layouts: 72 us -> none  [hot_terms(): jnp.sum((pos_rows[:, :, None] == item_ids[None, None, :]).astype(jnp.floa...]
    all_to_all x0 -> x1, blocking collectives: none -> 62.8 us  [body(): lax.all_to_all(row_terms, ('grp', 'shard'), split_axis=0, concat_axis=0,...]
    gather x1 -> x0, local copies, waits for them, and re-layouts: 57.4 us -> none  [body(): found = jnp.take(cold_half, asked_rows, axis=0)]
    all_to_all x2 -> x1, waiting for transfers between devices: 113 us -> 73.2 us  [body(): lax.all_to_all(found.reshape(devices, slot_count, feature_count), ('grp',...]
  transfers between devices with their start and end apart: 6 -> 5, of which waited for: 5 -> 4; matrix products, arithmetic and copies ran while one was open for 21% -> 8% of each run, Pallas kernels for 0% -> 7%
where the time goes in v1:
time: 536 us; the launch traced here: 535 us
  Pallas kernels  238 us (44%)
  waiting for transfers between devices  160 us (30%)
  blocking collectives  62.8 us (12%)
  matrix products  28.2 us (5%)
  starting transfers between devices  14.3 us (3%)
  between operations  13.9 us (3%)
  other arithmetic  11.3 us (2%)
  local copies, waits for them, and re-layouts  7.05 us (1%)
    pallas_call x1, Pallas kernels, hot_terms(): pl.pallas_call(_hot_kernel, grid=(items // block,), in_specs=[pl.BlockSpe...  199 us
    all_to_all x1, waiting for transfers between devices, body(): lax.all_to_all(found.reshape(devices, slot_count, feature_count), ('grp',...  73.2 us
    all_to_all x1, blocking collectives, body(): lax.all_to_all(row_terms, ('grp', 'shard'), split_axis=0, concat_axis=0,...  62.8 us
    all_gather x1, waiting for transfers between devices, body(): hot_all = lax.all_gather(hot_half, 'shard', axis=0, tiled=True)  51.3 us
    psum x1, waiting for transfers between devices, body(): hot_grad = lax.psum(item_grad, 'grp')  26.7 us
    pallas_call x1, Pallas kernels, onehot_scatter_add(): pl.pallas_call(_scatter_kernel, grid=(n // chunk,), in_specs=[pl.BlockSpe...  22.1 us
    pallas_call x1, Pallas kernels, onehot_gather(): pl.pallas_call(_gather_kernel, grid=(n // chunk,), in_specs=[pl.BlockSpec...  17.5 us
    dot_general x1, matrix products, body(): user_cold = jnp.dot(weights, flat_rows, preferred_element_type=jnp.float32)  12.6 us
  transfers between devices with their start and end apart: 5, of which 4 were waited for; matrix products, arithmetic and copies ran while one was open for 8% of the time, Pallas kernels for 7%

profile of v1, /device:TPU:0, one launch (start us, length us, event | category | flops | bytes accessed | tf_op | source)
XLA Modules:
  0.0 535.4 jit_solution(14841338104221823832)
XLA Ops:
  7.2 0.0 all-gather.2.cloned.1.call-start
  7.2 1.8 convert_element_type.30
  9.0 0.0 all-gather.2.cloned.1.call-update
  9.0 0.0 reduce-scatter.2.cloned.1.call-start
  9.1 1.6 convert_element_type.29.u_ref
  10.7 0.8 add_select_fusion
  11.5 0.1 copy.20
  11.6 0.1 eq.17
  11.7 0.1 copy.19
  11.9 0.8 reshape.55.ph_ref
  12.6 2.1 fusion.ol_ref
  14.7 51.3 %all-gather.2.cloned.1.call-done.h_ref = bf16[32768,128]{1,0:T(8,128)(2,1)} async-done(((bf16[1024,128]{1,0:T(8,128)(2,1)}), bf16[32768,128]{1,0:T(8,128)(2,1)}) %all-gather.2.cloned.1.call-update) | async-done | bytes 8388624 | tf_op jit(solution)/shard_map/all_gather | solution.py:165
  66.0 198.6 %shard_map.136 = (f32[512,128]{1,0:T(8,128)}, f32[32768,128]{1,0:T(8,128)}) custom-call(bf16[512,128]{1,0:T(8,128)(2,1)} %convert_element_type.29.u_ref, bf16[32768,128]{1,0:T(8,128)(2,1)} %all-gather.2.cloned.1.call-done.h_ref, s32[64,128]{1,0:T(8,128)} %reshape.55.ph_ref, bf16[64,128,128]{2,1,0:T(8,128)(2,1)} %fusion.ol_ref), custom_call_target="tpu_custom_call" | custom-call | tf_op jit(solution)/shard_map/pallas_call | solution.py:70
  264.5 0.0 copy-start.1
  264.5 0.0 reduce-scatter.2.cloned.1.call-update
  264.6 8.3 %all-to-all-start = ((s32[128,1,128]{2,1,0:T(1,128)}), s32[128,1,128]{2,1,0:T(1,128)S(1)}, u32[]{:S(2)}, u32[]{:S(2)}) async-start(s32[128,1,128]{2,1,0:T(1,128)} %bitcast), calls=%async_computation | async-start | bytes 131072 | tf_op jit(solution)/shard_map/all_to_all | solution.py:174
  272.9 0.0 copy-done.1
  272.9 0.7 convert_element_type.32.table_ref
  273.6 8.5 %all-to-all-done = s32[128,1,128]{2,1,0:T(1,128)S(1)} async-done(((s32[128,1,128]{2,1,0:T(1,128)}), s32[128,1,128]{2,1,0:T(1,128)S(1)}, u32[]{:S(2)}, u32[]{:S(2)}) %all-to-all-start) | async-done | bytes 65568 | tf_op jit(solution)/shard_map/all_to_all | solution.py:174
  282.1 0.0 copy-start.4
  282.1 4.9 copy.21.idx_ref
  287.0 0.0 copy-start.8
  287.0 0.0 copy-start.3
  287.0 17.5 %shard_map.137 = bf16[16384,128]{1,0:T(8,128)(2,1)} custom-call(s32[16384,1]{1,0:T(8,128)} %copy.21.idx_ref, bf16[1024,128]{1,0:T(8,128)(2,1)} %convert_element_type.32.table_ref), custom_call_target="tpu_custom_call" | custom-call | tf_op jit(solution)/shard_map/pallas_call | solution.py:103
  304.5 0.0 copy-done.4
  304.5 5.8 %all-to-all-start.1 = ((bf16[128,128,128]{2,1,0:T(8,128)(2,1)}), bf16[128,128,128]{2,1,0:T(8,128)(2,1)}, u32[]{:S(2)}, u32[]{:S(2)}) async-start(bf16[128,128,128]{2,1,0:T(8,128)(2,1)} %bitcast.17), calls=%async_computation.1 | async-start | bytes 8388608 | tf_op jit(solution)/shard_map/all_to_all | solution.py:176
  310.3 0.0 all-reduce.2.cloned.1.call-start
  310.4 0.0 copy-done.8
  310.4 0.1 convert_bitcast_fusion
  310.5 73.2 %all-to-all-done.1 = bf16[128,128,128]{2,1,0:T(8,128)(2,1)} async-done(((bf16[128,128,128]{2,1,0:T(8,128)(2,1)}), bf16[128,128,128]{2,1,0:T(8,128)(2,1)}, u32[]{:S(2)}, u32[]{:S(2)}) %all-to-all-start.1) | async-done | bytes 4194336 | tf_op jit(solution)/shard_map/all_to_all | solution.py:176
  383.6 0.0 copy-done.3
  383.6 10.9 %multiply_convert_fusion = bf16[16384,512]{1,0:T(8,128)(2,1)S(1)} fusion(bf16[16384,128]{1,0:T(8,128)(2,1)} %bitcast.3, bf16[512,128]{1,0:T(8,128)(2,1)S(1)} %copy-done.3, f32[16384]{0:T(1024)S(1)} %convert_bitcast_fusion), kind=kOutput, calls=%fused_computation | convolution fusion | flops 2189426688 | bytes 21168128 | tf_op jit(solution)/shard_map/uk,rk->ur/dot_general | solution.py:184
  394.6 0.0 copy-start
  394.6 4.7 convolution_convert_fusion
  399.3 1.0 copy-done
  400.3 0.0 copy-start.5
  400.3 0.0 copy-start.7
  400.3 0.0 copy-start.9
  400.3 62.8 %all_to_all.19 = bf16[128,128,128]{2,1,0:T(8,128)(2,1)} all-to-all(bf16[128,128,128]{2,1,0:T(8,128)(2,1)S(1)} %bitcast.16), channel_id=1, replica_groups=mesh['grp'=4,'shard'=32] {'grp','shard'}, dimensions={0} | all-to-all | bytes 8388608 | tf_op jit(solution)/shard_map/all_to_all | solution.py:193
  463.1 22.1 %shard_map.138 = f32[1024,128]{1,0:T(8,128)} custom-call(s32[1,16384]{1,0:T(1,128)} %bitcast.20, bf16[16384,128]{1,0:T(8,128)(2,1)} %bitcast.18), custom_call_target="tpu_custom_call" | custom-call | tf_op jit(solution)/shard_map/pallas_call | solution.py:132
  485.2 0.0 copy-done.5
  485.2 2.1 multiply_subtract_fusion
  487.4 0.0 reduce-scatter.2.cloned.1.call-done
  487.4 0.0 all-reduce.2.cloned.1.call-update
  487.4 0.0 copy-done.7
  487.4 0.0 copy-done.9
  487.4 0.0 copy-start.2
  487.4 0.0 copy-start.6
  487.4 12.6 %multiply_subtract_fusion.2 = (f32[512,128]{1,0:T(8,128)}, f32[512,128]{1,0:T(8,128)}) fusion(f32[512,128]{1,0:T(8,128)S(1)} %copy-done.7, f32[512,128]{1,0:T(8,128)S(1)} %copy-done.9, f32[512,128]{1,0:T(8,128)} %get-tuple-element.8, bf16[16384,512]{1,0:T(8,128)(2,1)} %copy-done, bf16[16384,128]{1,0:T(8,128)(2,1)} %bitcast.3), kind=kOutput, calls=%fused_computation.9 | convolution fusion | flops 2147876864 | bytes 22282240 | tf_op jit(solution)/shard_map/dot_general | solution.py:188
  500.0 26.7 %all-reduce.2.cloned.1.call-done = f32[1024,128]{1,0:T(8,128)} async-done(((f32[1024,128]{1,0:T(8,128)}), f32[1024,128]{1,0:T(8,128)}) %all-reduce.2.cloned.1.call-update) | async-done | bytes 524304 | tf_op jit(solution)/shard_map/psum | solution.py:169
  526.8 0.0 copy-done.2
  526.8 0.0 copy-done.6
  526.8 2.1 multiply_subtract_fusion.1
Async XLA Ops:
  7.2 58.8 %all-gather.2.cloned.1.call-start = ((), (), s32[]{:S(2)}) async-start(), calls=%async_computation.4 | async-start | bytes 8650752 | tf_op jit(solution)/shard_map/all_gather | solution.py:165
  9.0 478.3 %reduce-scatter.2.cloned.1.call-start = ((), (), s32[]{:S(2)}) async-start(), calls=%async_computation.5 | async-start | bytes 17301504 | tf_op jit(solution)/shard_map/reduce_scatter | solution.py:168
  264.5 8.4 %copy-start.1 = (f32[1024,128]{1,0:T(8,128)S(1)}, f32[1024,128]{1,0:T(8,128)}, u32[]{:S(2)}) copy-start(f32[1024,128]{1,0:T(8,128)} %param.14) | copy-start | bytes 1572868
  264.6 17.6 %all-to-all-start = ((s32[128,1,128]{2,1,0:T(1,128)}), s32[128,1,128]{2,1,0:T(1,128)S(1)}, u32[]{:S(2)}, u32[]{:S(2)}) async-start(s32[128,1,128]{2,1,0:T(1,128)} %bitcast), calls=%async_computation | async-start | bytes 131072 | tf_op jit(solution)/shard_map/all_to_all | solution.py:174
  282.1 22.4 %copy-start.4 = (s32[128,1,128]{2,1,0:T(1,128)}, s32[128,1,128]{2,1,0:T(1,128)S(1)}, u32[]{:S(2)}) copy-start(s32[128,1,128]{2,1,0:T(1,128)S(1)} %all-to-all-done) | copy-start | bytes 196612
  287.0 23.4 %copy-start.8 = (s32[1,128]{1,0:T(1,128)S(1)}, s32[1,128]{1,0:T(1,128)}, u32[]{:S(2)}) copy-start(s32[1,128]{1,0:T(1,128)} %param.17) | copy-start | bytes 1540
  287.0 96.6 %copy-start.3 = (bf16[512,128]{1,0:T(8,128)(2,1)S(1)}, bf16[512,128]{1,0:T(8,128)(2,1)}, u32[]{:S(2)}) copy-start(bf16[512,128]{1,0:T(8,128)(2,1)} %convert_element_type.29.u_ref) | copy-start | bytes 393220
  304.5 79.1 %all-to-all-start.1 = ((bf16[128,128,128]{2,1,0:T(8,128)(2,1)}), bf16[128,128,128]{2,1,0:T(8,128)(2,1)}, u32[]{:S(2)}, u32[]{:S(2)}) async-start(bf16[128,128,128]{2,1,0:T(8,128)(2,1)} %bitcast.17), calls=%async_computation.1 | async-start | bytes 8388608 | tf_op jit(solution)/shard_map/all_to_all | solution.py:176
  310.3 216.4 %all-reduce.2.cloned.1.call-start = ((), (), s32[]{:S(2)}) async-start(), calls=%async_computation.6 | async-start | bytes 1048576 | tf_op jit(solution)/shard_map/psum | solution.py:169
  394.6 5.7 %copy-start = (bf16[16384,512]{1,0:T(8,128)(2,1)}, bf16[16384,512]{1,0:T(8,128)(2,1)S(1)}, u32[]{:S(2)}) copy-start(bf16[16384,512]{1,0:T(8,128)(2,1)S(1)} %multiply_convert_fusion) | copy-start | bytes 50331652
  400.3 84.9 %copy-start.5 = (f32[1024,128]{1,0:T(8,128)S(1)}, f32[1024,128]{1,0:T(8,128)}, u32[]{:S(2)}) copy-start(f32[1024,128]{1,0:T(8,128)} %param.15) | copy-start | bytes 1572868
  400.3 87.0 %copy-start.7 = (f32[512,128]{1,0:T(8,128)S(1)}, f32[512,128]{1,0:T(8,128)}, u32[]{:S(2)}) copy-start(f32[512,128]{1,0:T(8,128)} %param.9) | copy-start | bytes 786436
  400.3 87.1 %copy-start.9 = (f32[512,128]{1,0:T(8,128)S(1)}, f32[512,128]{1,0:T(8,128)}, u32[]{:S(2)}) copy-start(f32[512,128]{1,0:T(8,128)} %param.10) | copy-start | bytes 786436
  487.4 39.4 %copy-start.2 = (f32[1024,128]{1,0:T(8,128)S(1)}, f32[1024,128]{1,0:T(8,128)}, u32[]{:S(2)}) copy-start(f32[1024,128]{1,0:T(8,128)} %param.12) | copy-start | bytes 1572868
  487.4 39.3 %copy-start.6 = (f32[1024,128]{1,0:T(8,128)S(1)}, f32[1024,128]{1,0:T(8,128)}, u32[]{:S(2)}) copy-start(f32[1024,128]{1,0:T(8,128)} %param.13) | copy-start | bytes 1572868
Sparse Core Ops, SparseCore 0:
  10.8 55.1 all-gather.1
  264.7 192.5 reduce-scatter.1
  487.5 39.2 all-reduce.1

commit v2 on v1

v2 whole, which is shorter than its diff:
```python
import functools

import jax
import jax.numpy as jnp
from jax import lax
from jax.experimental import pallas as pl
from jax.experimental.pallas import tpu as pltpu
from jax.sharding import Mesh, PartitionSpec as P

POSITIVE_WEIGHT = 32.0
LEARN_RATE = 0.5
LANES = 128
SUB = 8


def _nt(a, b):
    return lax.dot_general(a, b, (((1,), (1,)), ((), ())), preferred_element_type=jnp.float32)


def _tn(a, b):
    return lax.dot_general(a, b, (((0,), (0,)), ((), ())), preferred_element_type=jnp.float32)


def _hot_kernel(u_ref, h_ref, ph_ref, pl_ref, up_ref, ip_ref, m_ref, *, sub_users):
    i = pl.program_id(0)
    items = h_ref.shape[0]
    nh = items // LANES
    subtiles = ph_ref.shape[0]
    width = ph_ref.shape[1]
    per = width // sub_users
    r = lax.broadcasted_iota(jnp.int32, (nh * sub_users, width), 0)
    c = lax.broadcasted_iota(jnp.int32, (nh * sub_users, width), 1)
    diag = (r % sub_users) == (c // per)
    hrow = r // sub_users
    lrow = lax.broadcasted_iota(jnp.int32, (LANES, width), 0)

    def sub(s, carry):
        lhs = jnp.where(diag & (ph_ref[pl.ds(s, 1), :] == hrow), 1.0, 0.0).astype(jnp.bfloat16)
        rhs = jnp.where(pl_ref[pl.ds(s, 1), :] == lrow, 1.0, 0.0).astype(jnp.bfloat16)
        out = _nt(lhs, rhs)
        base = pl.multiple_of(s * sub_users, sub_users)
        for h in range(nh):
            m_ref[pl.ds(base, sub_users), pl.ds(h * LANES, LANES)] = out[
                h * sub_users:(h + 1) * sub_users, :
            ]
        return carry

    lax.fori_loop(0, subtiles, sub, 0, unroll=subtiles)
    u = u_ref[...]
    hj = h_ref[...]
    scores = _nt(u, hj)
    m = m_ref[...]
    w = ((1.0 + POSITIVE_WEIGHT * m) * jax.nn.sigmoid(scores) - POSITIVE_WEIGHT * m).astype(
        jnp.bfloat16
    )
    up_ref[...] = jnp.dot(w, hj, preferred_element_type=jnp.float32)

    @pl.when(i == 0)
    def _():
        ip_ref[...] = jnp.zeros_like(ip_ref)

    ip_ref[...] += _tn(w, u)


def hot_terms(user_half, positives, hot_rows, tile=512, sub_users=8):
    users, k = user_half.shape
    items = hot_rows.shape[0]
    pos_count = positives.shape[1]
    subtiles = users // sub_users
    width = sub_users * pos_count
    pos_hi = (positives // LANES).reshape(subtiles, width)
    pos_lo = (positives % LANES).reshape(subtiles, width)
    per_tile = tile // sub_users
    return pl.pallas_call(
        functools.partial(_hot_kernel, sub_users=sub_users),
        grid=(users // tile,),
        in_specs=[
            pl.BlockSpec((tile, k), lambda i: (i, 0)),
            pl.BlockSpec((items, k), lambda i: (0, 0)),
            pl.BlockSpec((per_tile, width), lambda i: (i, 0)),
            pl.BlockSpec((per_tile, width), lambda i: (i, 0)),
        ],
        out_specs=[
            pl.BlockSpec((tile, k), lambda i: (i, 0)),
            pl.BlockSpec((items, k), lambda i: (0, 0)),
        ],
        out_shape=[
            jax.ShapeDtypeStruct((users, k), jnp.float32),
            jax.ShapeDtypeStruct((items, k), jnp.float32),
        ],
        scratch_shapes=[pltpu.VMEM((tile, items), jnp.float32)],
        compiler_params=pltpu.CompilerParams(dimension_semantics=("arbitrary",)),
    )(user_half, hot_rows, pos_hi, pos_lo)


def _gather_kernel(idx_ref, table_ref, out_ref):
    rows = table_ref.shape[0]
    onehot = (idx_ref[...] == lax.broadcasted_iota(jnp.int32, (1, rows), 1)).astype(jnp.bfloat16)
    out_ref[...] = jnp.dot(onehot, table_ref[...], preferred_element_type=jnp.float32).astype(
        out_ref.dtype
    )


def onehot_gather(table, idx, chunk=1024):
    rows, k = table.shape
    n = idx.shape[0]
    return pl.pallas_call(
        _gather_kernel,
        grid=(n // chunk,),
        in_specs=[
            pl.BlockSpec((chunk, 1), lambda i: (i, 0)),
            pl.BlockSpec((rows, k), lambda i: (0, 0)),
        ],
        out_specs=pl.BlockSpec((chunk, k), lambda i: (i, 0)),
        out_shape=jax.ShapeDtypeStruct((n, k), table.dtype),
    )(idx.reshape(n, 1), table)


def _scatter_kernel(idx_ref, val_ref, out_ref):
    i = pl.program_id(0)
    rows = out_ref.shape[0]
    chunk = idx_ref.shape[1]
    onehot = (idx_ref[...] == lax.broadcasted_iota(jnp.int32, (rows, chunk), 0)).astype(
        jnp.bfloat16
    )

    @pl.when(i == 0)
    def _():
        out_ref[...] = jnp.zeros_like(out_ref)

    out_ref[...] += jnp.dot(onehot, val_ref[...], preferred_element_type=jnp.float32)


def onehot_scatter_add(idx, values, rows, chunk=1024):
    n, k = values.shape
    return pl.pallas_call(
        _scatter_kernel,
        grid=(n // chunk,),
        in_specs=[
            pl.BlockSpec((1, chunk), lambda i: (0, i)),
            pl.BlockSpec((chunk, k), lambda i: (i, 0)),
        ],
        out_specs=pl.BlockSpec((rows, k), lambda i: (0, 0)),
        out_shape=jax.ShapeDtypeStruct((rows, k), jnp.float32),
        compiler_params=pltpu.CompilerParams(dimension_semantics=("arbitrary",)),
    )(idx.reshape(1, n), values)


def adagrad(current, history, gradient):
    updated = history + gradient * gradient
    return (current - LEARN_RATE * gradient / jnp.sqrt(updated), updated)


def body(
    users,
    user_accum,
    positives,
    hot_table,
    hot_accum,
    cold_table,
    cold_accum,
    cold_requests,
    cold_counts,
):
    user_half = users.astype(jnp.bfloat16)
    hot_half = hot_table.astype(jnp.bfloat16)
    cold_half = cold_table.astype(jnp.bfloat16)
    feature_count = users.shape[1]
    item_sub = hot_table.shape[0]
    sb_count = lax.axis_size("sb")
    users_part = lax.all_gather(user_half, "sb", axis=0, tiled=True)
    pos_part = lax.all_gather(positives, "sb", axis=0, tiled=True)
    hot_part = lax.all_gather(hot_half, "sa", axis=0, tiled=True)
    owner = pos_part // item_sub
    local = (owner // sb_count) * item_sub + pos_part % item_sub
    local = jnp.where(owner % sb_count == lax.axis_index("sb"), local, hot_part.shape[0])
    user_hot_part, item_part = hot_terms(users_part, local, hot_part)
    user_hot = lax.psum_scatter(user_hot_part, "sb", scatter_dimension=0, tiled=True)
    item_grad = lax.psum_scatter(item_part, "sa", scatter_dimension=0, tiled=True)
    hot_grad = lax.psum(item_grad, "grp")
    devices = cold_requests.shape[1]
    slot_count = cold_requests.shape[2]
    requests = cold_requests.reshape(devices, slot_count)
    live_slots = lax.iota(jnp.int32, slot_count)[None, :] < cold_counts.reshape(devices, 1)
    asked_rows = lax.all_to_all(requests, ("grp", "sa", "sb"), split_axis=0, concat_axis=0, tiled=True)
    found = onehot_gather(cold_half, asked_rows.reshape(-1))
    fetched = lax.all_to_all(
        found.reshape(devices, slot_count, feature_count),
        ("grp", "sa", "sb"),
        split_axis=0,
        concat_axis=0,
        tiled=True,
    )
    flat_rows = fetched.reshape(devices * slot_count, feature_count)
    scores = jnp.einsum("uk,rk->ur", user_half, flat_rows, preferred_element_type=jnp.float32)
    weights = (jax.nn.sigmoid(scores) * live_slots.reshape(1, -1).astype(jnp.float32)).astype(
        jnp.bfloat16
    )
    user_cold = jnp.dot(weights, flat_rows, preferred_element_type=jnp.float32)
    row_terms = jnp.einsum(
        "ur,uk->rk", weights, user_half, preferred_element_type=jnp.float32
    ).astype(jnp.bfloat16)
    row_terms = row_terms.reshape(devices, slot_count, feature_count)
    returned = lax.all_to_all(row_terms, ("grp", "sa", "sb"), split_axis=0, concat_axis=0, tiled=True)
    cold_grad = onehot_scatter_add(
        asked_rows.reshape(-1),
        returned.reshape(devices * slot_count, feature_count),
        cold_table.shape[0],
    )
    user_grad = user_hot + user_cold
    new_users, new_user_accum = adagrad(users, user_accum, user_grad)
    new_hot, new_hot_accum = adagrad(hot_table, hot_accum, hot_grad)
    new_cold, new_cold_accum = adagrad(cold_table, cold_accum, cold_grad)
    return (new_users, new_user_accum, new_hot, new_hot_accum, new_cold, new_cold_accum)


def _split_mesh(mesh):
    shard = mesh.shape["shard"]
    sa = 4 if shard % 4 == 0 else 1
    return Mesh(mesh.devices.reshape(mesh.shape["grp"], sa, shard // sa), ("grp", "sa", "sb"))


def solution(mesh):
    return jax.shard_map(
        body,
        mesh=_split_mesh(mesh),
        in_specs=(
            P(("grp", "sa", "sb"), None),
            P(("grp", "sa", "sb"), None),
            P(("grp", "sa", "sb"), None),
            P(("sa", "sb"), None),
            P(("sa", "sb"), None),
            P(("grp", "sa", "sb"), None),
            P(("grp", "sa", "sb"), None),
            P(("grp", "sa", "sb"), None, None),
            P(("grp", "sa", "sb"), None),
        ),
        out_specs=(
            P(("grp", "sa", "sb"), None),
            P(("grp", "sa", "sb"), None),
            P(("sa", "sb"), None),
            P(("sa", "sb"), None),
            P(("grp", "sa", "sb"), None),
            P(("grp", "sa", "sb"), None),
        ),
        check_vma=False,
    )
```

time: 536 us -> 358 us (0.67)
  Pallas kernels: 238 us -> 103 us
  blocking collectives: 62.8 us -> 13.1 us
  starting transfers between devices: 14.3 us -> 26.6 us
  waiting for transfers between devices: 160 us -> 152 us
    pallas_call x1, Pallas kernels: 199 us -> 64.1 us  [hot_terms(): pl.pallas_call(functools.partial(_hot_kernel, sub_users=sub_users), grid=...]
    all_to_all x1 -> x0, blocking collectives: 62.8 us -> none  [body(): lax.all_to_all(row_terms, ('grp', 'shard'), split_axis=0, concat_axis=0,...]
    psum x1, waiting for transfers between devices: 26.7 us -> 66.3 us  [body(): hot_grad = lax.psum(item_grad, 'grp')]
    all_gather x1 -> x2, waiting for transfers between devices: 51.3 us -> 23.2 us  [the longest x1 23.2 us: body(): users_part = lax.all_gather(user_half, 'sb', axis=0, tiled=True)]
    all_gather x0 -> x1, blocking collectives: none -> 13.1 us  [body(): pos_part = lax.all_gather(positives, 'sb', axis=0, tiled=True)]
    all_to_all x1, waiting for transfers between devices: 73.2 us -> 61.7 us  [body(): lax.all_to_all(found.reshape(devices, slot_count, feature_count), ('grp',...]
    all_to_all x1 -> x2, starting transfers between devices: 8.32 us -> 17.1 us  [the longest x1 11.2 us: body(): lax.all_to_all(requests, ('grp', 'sa', 'sb'), split_axis=0, concat_axis=0...]
    all_to_all x1 -> x2, waiting for transfers between devices: 8.51 us -> 0.01 us  [the longest x1 0.01 us: body(): lax.all_to_all(requests, ('grp', 'sa', 'sb'), split_axis=0, concat_axis=0...]
  transfers between devices with their start and end apart: 5 -> 8, of which waited for: 4 -> 3; matrix products, arithmetic and copies ran while one was open for 8% -> 12% of each run, Pallas kernels for 7% -> 23%
where the time goes in v2:
time: 358 us; the launch traced here: 357 us
  waiting for transfers between devices  152 us (42%)
  Pallas kernels  103 us (29%)
  matrix products  30.2 us (8%)
  starting transfers between devices  26.6 us (7%)
  between operations  13.9 us (4%)
  blocking collectives  13.1 us (4%)
  other arithmetic  9.14 us (3%)
  local copies, waits for them, and re-layouts  8.84 us (2%)
    psum x1, waiting for transfers between devices, body(): hot_grad = lax.psum(item_grad, 'grp')  66.3 us
    pallas_call x1, Pallas kernels, hot_terms(): pl.pallas_call(functools.partial(_hot_kernel, sub_users=sub_users), grid=...  64.1 us
    all_to_all x1, waiting for transfers between devices, body(): lax.all_to_all(found.reshape(devices, slot_count, feature_count), ('grp',...  61.7 us
    all_gather x1, waiting for transfers between devices, body(): users_part = lax.all_gather(user_half, 'sb', axis=0, tiled=True)  23.2 us
    pallas_call x1, Pallas kernels, onehot_scatter_add(): pl.pallas_call(_scatter_kernel, grid=(n // chunk,), in_specs=[pl.BlockSpe...  22.1 us
    pallas_call x1, Pallas kernels, onehot_gather(): pl.pallas_call(_gather_kernel, grid=(n // chunk,), in_specs=[pl.BlockSpec...  17 us
    all_gather x1, blocking collectives, body(): pos_part = lax.all_gather(positives, 'sb', axis=0, tiled=True)  13.1 us
    dot_general x1, matrix products, body(): user_cold = jnp.dot(weights, flat_rows, preferred_element_type=jnp.float32)  12.5 us
  transfers between devices with their start and end apart: 8, of which 3 were waited for; matrix products, arithmetic and copies ran while one was open for 12% of the time, Pallas kernels for 23%

profile of v2, /device:TPU:0, one launch (start us, length us, event | category | flops | bytes accessed | tf_op | source)
XLA Modules:
  0.0 357.0 jit_solution(13367234293037609173)
XLA Ops:
  7.2 0.0 all-gather.5.cloned.1.call-start
  7.2 1.8 convert_element_type.27
  9.0 0.0 copy-start.2
  9.0 0.0 all-gather.5.cloned.1.call-update
  9.0 11.2 %all-to-all-start = ((s32[128,1,128]{2,1,0:T(1,128)}), s32[128,1,128]{2,1,0:T(1,128)S(1)}, u32[]{:S(2)}, u32[]{:S(2)}) async-start(s32[128,1,128]{2,1,0:T(1,128)} %bitcast.20), calls=%async_computation.1 | async-start | bytes 131072 | tf_op jit(solution)/shard_map/all_to_all | solution.py:185
  20.2 0.0 all-gather.3.cloned.1.call-start
  20.2 1.6 convert_element_type.26
  21.9 0.0 all-gather.3.cloned.1.call-update
  21.9 0.0 reduce-scatter.5.cloned.1.call-start
  21.9 13.1 %all_gather.11 = s32[4096,16]{0,1:T(8,128)S(1)} all-gather(s32[512,16]{0,1:T(8,128)} %param.11), channel_id=1, replica_groups=mesh['grp'=4,'sa'=4,'sb'=8] {'sb'}, dimensions={0}, use_global_device_ids=true | all-gather | bytes 294912 | tf_op jit(solution)/shard_map/all_gather | solution.py:172
  35.0 0.6 add_select_fusion
  35.6 0.1 add_select_fusion.1
  35.7 0.6 copy.20
  36.3 1.3 reshape.56.ph_ref
  37.6 0.6 copy.21
  38.2 1.3 reshape.57.pl_ref
  39.5 0.0 all-gather.5.cloned.1.call-done.h_ref
  39.5 23.2 %all-gather.3.cloned.1.call-done.u_ref = bf16[4096,128]{1,0:T(8,128)(2,1)} async-done(((bf16[512,128]{1,0:T(8,128)(2,1)}), bf16[4096,128]{1,0:T(8,128)(2,1)}) %all-gather.3.cloned.1.call-update) | async-done | bytes 1048592 | tf_op jit(solution)/shard_map/all_gather | solution.py:171
  62.7 64.1 %shard_map.136 = (f32[4096,128]{1,0:T(8,128)}, f32[4096,128]{1,0:T(8,128)}) custom-call(bf16[4096,128]{1,0:T(8,128)(2,1)} %all-gather.3.cloned.1.call-done.u_ref, bf16[4096,128]{1,0:T(8,128)(2,1)} %all-gather.5.cloned.1.call-done.h_ref, s32[512,128]{1,0:T(8,128)} %reshape.56.ph_ref, s32[512,128]{1,0:T(8,128)} %reshape.57.pl_ref), custom_call_target="tpu_custom_call" | custom-call | tf_op jit(solution)/shard_map/pallas_call | solution.py:74
  126.8 0.0 reduce-scatter.5.cloned.1.call-update
  126.8 0.0 copy-done.2
  126.8 0.7 convert_element_type.28.table_ref
  127.6 0.0 all-to-all-done
  127.6 0.0 copy-start.4
  127.6 4.9 %copy.22.idx_ref = s32[16384,1]{1,0:T(8,128)} copy(s32[16384,1]{0,1:T(1,128)S(1)} %bitcast.18) | data formatting | bytes 131072 | tf_op jit(solution)/shard_map/reshape;reshape | solution.py:116
  132.5 0.0 copy-start.8
  132.5 17.0 %shard_map.137 = bf16[16384,128]{1,0:T(8,128)(2,1)} custom-call(s32[16384,1]{1,0:T(8,128)} %copy.22.idx_ref, bf16[1024,128]{1,0:T(8,128)(2,1)} %convert_element_type.28.table_ref), custom_call_target="tpu_custom_call" | custom-call | tf_op jit(solution)/shard_map/pallas_call | solution.py:107
  149.5 0.0 copy-done.4
  149.5 0.0 copy-start.3
  149.5 9.0 %all-to-all-start.1 = ((bf16[128,128,128]{2,1,0:T(8,128)(2,1)}), bf16[128,128,128]{2,1,0:T(8,128)(2,1)}, u32[]{:S(2)}, u32[]{:S(2)}) async-start(bf16[128,128,128]{2,1,0:T(8,128)(2,1)} %bitcast.17), calls=%async_computation.2 | async-start | bytes 8388608 | tf_op jit(solution)/shard_map/all_to_all | solution.py:187
  158.6 0.2 reduce-scatter.3.cloned.1.call-start
  158.8 0.0 copy-done.8
  158.8 0.1 convert_bitcast_fusion
  158.9 0.2 reduce-scatter.3.cloned.1.call-update
  159.1 61.7 %all-to-all-done.1 = bf16[128,128,128]{2,1,0:T(8,128)(2,1)} async-done(((bf16[128,128,128]{2,1,0:T(8,128)(2,1)}), bf16[128,128,128]{2,1,0:T(8,128)(2,1)}, u32[]{:S(2)}, u32[]{:S(2)}) %all-to-all-start.1) | async-done | bytes 4194336 | tf_op jit(solution)/shard_map/all_to_all | solution.py:187
  220.8 0.0 copy-done.3
  220.8 10.9 %multiply_convert_fusion = bf16[16384,512]{1,0:T(8,128)(2,1)S(1)} fusion(bf16[16384,128]{1,0:T(8,128)(2,1)} %bitcast.3, bf16[512,128]{1,0:T(8,128)(2,1)S(1)} %copy-done.3, f32[16384]{0:T(1024)S(1)} %convert_bitcast_fusion), kind=kOutput, calls=%fused_computation | convolution fusion | flops 2189426688 | bytes 21168128 | tf_op jit(solution)/shard_map/uk,rk->ur/dot_general | solution.py:195
  231.7 0.0 copy-start
  231.7 6.8 %convolution_convert_fusion = bf16[16384,128]{1,0:T(8,128)(2,1)} fusion(bf16[16384,512]{1,0:T(8,128)(2,1)S(1)} %multiply_convert_fusion, bf16[512,128]{1,0:T(8,128)(2,1)S(1)} %copy-done.3), kind=kOutput, calls=%fused_computation.1 | convolution fusion | flops 2149580800 | bytes 21102592 | tf_op jit(solution)/shard_map/ur,uk->rk/dot_general | solution.py:200
  238.5 0.2 copy-done
  238.7 0.0 copy-start.7
  238.7 0.0 copy-start.9
  238.7 6.0 %all-to-all-start.2 = ((bf16[128,128,128]{2,1,0:T(8,128)(2,1)}), bf16[128,128,128]{2,1,0:T(8,128)(2,1)}, u32[]{:S(2)}, u32[]{:S(2)}) async-start(bf16[128,128,128]{2,1,0:T(8,128)(2,1)} %bitcast.16), calls=%async_computation.4 | async-start | bytes 8388608 | tf_op jit(solution)/shard_map/all_to_all | solution.py:204
  244.6 0.0 all-reduce.2.cloned.1.call-start
  244.7 0.0 reduce-scatter.5.cloned.1.call-done
  244.7 0.5 all-reduce.2.cloned.1.call-update
  245.2 0.0 copy-start.1
  245.2 0.0 copy-start.5
  245.2 0.0 copy-start.6
  245.3 0.0 reduce-scatter.3.cloned.1.call-done
  245.3 0.0 copy-done.7
  245.3 0.0 copy-done.9
  245.3 12.5 %multiply_subtract_fusion.2 = (f32[512,128]{1,0:T(8,128)}, f32[512,128]{1,0:T(8,128)}) fusion(f32[512,128]{1,0:T(8,128)S(1)} %copy-done.7, f32[512,128]{1,0:T(8,128)S(1)} %copy-done.9, f32[512,128]{1,0:T(8,128)} %reduce-scatter.3.cloned.1.call-done, bf16[16384,512]{1,0:T(8,128)(2,1)} %copy-done, bf16[16384,128]{1,0:T(8,128)(2,1)} %bitcast.3), kind=kOutput, calls=%fused_computation.26 | convolution fusion | flops 2147876864 | bytes 22282240 | tf_op jit(solution)/shard_map/dot_general | solution.py:199
  257.8 66.3 %all-reduce.2.cloned.1.call-done = f32[1024,128]{1,0:T(8,128)} async-done(((f32[1024,128]{1,0:T(8,128)}), f32[1024,128]{1,0:T(8,128)}) %all-reduce.2.cloned.1.call-update) | async-done | bytes 524304 | tf_op jit(solution)/shard_map/psum | solution.py:180
  324.1 0.0 copy-done.1
  324.1 0.0 copy-done.5
  324.1 2.1 multiply_subtract_fusion.1
  326.2 0.0 all-to-all-done.2
  326.2 22.1 %shard_map.138 = f32[1024,128]{1,0:T(8,128)} custom-call(s32[1,16384]{1,0:T(1,128)} %bitcast.19, bf16[16384,128]{1,0:T(8,128)(2,1)} %bitcast.8.val_ref), custom_call_target="tpu_custom_call" | custom-call | tf_op jit(solution)/shard_map/pallas_call | solution.py:136
  348.3 0.0 copy-done.6
  348.3 2.1 multiply_subtract_fusion
Async XLA Ops:
  7.2 32.3 %all-gather.5.cloned.1.call-start = ((), (), s32[]{:S(2)}) async-start(), calls=%async_computation.6 | async-start | bytes 1310720 | tf_op jit(solution)/shard_map/all_gather | solution.py:173
  9.0 117.8 %copy-start.2 = (f32[1024,128]{1,0:T(8,128)S(1)}, f32[1024,128]{1,0:T(8,128)}, u32[]{:S(2)}) copy-start(f32[1024,128]{1,0:T(8,128)} %param.14) | copy-start | bytes 1572868
  9.0 118.5 %all-to-all-start = ((s32[128,1,128]{2,1,0:T(1,128)}), s32[128,1,128]{2,1,0:T(1,128)S(1)}, u32[]{:S(2)}, u32[]{:S(2)}) async-start(s32[128,1,128]{2,1,0:T(1,128)} %bitcast.20), calls=%async_computation.1 | async-start | bytes 131072 | tf_op jit(solution)/shard_map/all_to_all | solution.py:185
  20.2 42.5 %all-gather.3.cloned.1.call-start = ((), (), s32[]{:S(2)}) async-start(), calls=%async_computation.5 | async-start | bytes 1179648 | tf_op jit(solution)/shard_map/all_gather | solution.py:171
  21.9 222.8 %reduce-scatter.5.cloned.1.call-start = ((), (), s32[]{:S(2)}) async-start(), calls=%async_computation.8 | async-start | bytes 2621440 | tf_op jit(solution)/shard_map/reduce_scatter | solution.py:179
  127.6 21.9 %copy-start.4 = (s32[128,1,128]{2,1,0:T(1,128)}, s32[128,1,128]{2,1,0:T(1,128)S(1)}, u32[]{:S(2)}) copy-start(s32[128,1,128]{2,1,0:T(1,128)S(1)} %all-to-all-done) | copy-start | bytes 196612
  132.5 26.3 %copy-start.8 = (s32[1,128]{1,0:T(1,128)S(1)}, s32[1,128]{1,0:T(1,128)}, u32[]{:S(2)}) copy-start(s32[1,128]{1,0:T(1,128)} %param.17) | copy-start | bytes 1540
  149.5 71.3 %copy-start.3 = (bf16[512,128]{1,0:T(8,128)(2,1)S(1)}, bf16[512,128]{1,0:T(8,128)(2,1)}, u32[]{:S(2)}) copy-start(bf16[512,128]{1,0:T(8,128)(2,1)} %convert_element_type.26) | copy-start | bytes 393220
  149.5 71.3 %all-to-all-start.1 = ((bf16[128,128,128]{2,1,0:T(8,128)(2,1)}), bf16[128,128,128]{2,1,0:T(8,128)(2,1)}, u32[]{:S(2)}, u32[]{:S(2)}) async-start(bf16[128,128,128]{2,1,0:T(8,128)(2,1)} %bitcast.17), calls=%async_computation.2 | async-start | bytes 8388608 | tf_op jit(solution)/shard_map/all_to_all | solution.py:187
  158.6 86.7 %reduce-scatter.3.cloned.1.call-start = ((), (), s32[]{:S(2)}) async-start(), calls=%async_computation.7 | async-start | bytes 2359296 | tf_op jit(solution)/shard_map/reduce_scatter | solution.py:178
  231.7 7.0 %copy-start = (bf16[16384,512]{1,0:T(8,128)(2,1)}, bf16[16384,512]{1,0:T(8,128)(2,1)S(1)}, u32[]{:S(2)}) copy-start(bf16[16384,512]{1,0:T(8,128)(2,1)S(1)} %multiply_convert_fusion) | copy-start | bytes 50331652
  238.7 6.6 %copy-start.7 = (f32[512,128]{1,0:T(8,128)S(1)}, f32[512,128]{1,0:T(8,128)}, u32[]{:S(2)}) copy-start(f32[512,128]{1,0:T(8,128)} %param.9) | copy-start | bytes 786436
  238.7 6.6 %copy-start.9 = (f32[512,128]{1,0:T(8,128)S(1)}, f32[512,128]{1,0:T(8,128)}, u32[]{:S(2)}) copy-start(f32[512,128]{1,0:T(8,128)} %param.10) | copy-start | bytes 786436
  238.7 87.5 %all-to-all-start.2 = ((bf16[128,128,128]{2,1,0:T(8,128)(2,1)}), bf16[128,128,128]{2,1,0:T(8,128)(2,1)}, u32[]{:S(2)}, u32[]{:S(2)}) async-start(bf16[128,128,128]{2,1,0:T(8,128)(2,1)} %bitcast.16), calls=%async_computation.4 | async-start | bytes 8388608 | tf_op jit(solution)/shard_map/all_to_all | solution.py:204
  244.6 79.5 %all-reduce.2.cloned.1.call-start = ((), (), s32[]{:S(2)}) async-start(), calls=%async_computation.9 | async-start | bytes 1048576 | tf_op jit(solution)/shard_map/psum | solution.py:180
  245.2 78.9 %copy-start.1 = (f32[1024,128]{1,0:T(8,128)S(1)}, f32[1024,128]{1,0:T(8,128)}, u32[]{:S(2)}) copy-start(f32[1024,128]{1,0:T(8,128)} %param.12) | copy-start | bytes 1572868
  245.2 78.9 %copy-start.5 = (f32[1024,128]{1,0:T(8,128)S(1)}, f32[1024,128]{1,0:T(8,128)}, u32[]{:S(2)}) copy-start(f32[1024,128]{1,0:T(8,128)} %param.13) | copy-start | bytes 1572868
  245.2 103.1 %copy-start.6 = (f32[1024,128]{1,0:T(8,128)S(1)}, f32[1024,128]{1,0:T(8,128)}, u32[]{:S(2)}) copy-start(f32[1024,128]{1,0:T(8,128)} %param.15) | copy-start | bytes 1572868
Sparse Core Ops, SparseCore 0:
  10.2 26.5 all-gather.4
  39.1 23.5 all-gather.2
  126.9 29.5 reduce-scatter.4
  161.5 54.4 reduce-scatter.2
  247.5 76.5 all-reduce.1

commit v3 on v2

--- a/solution.py
+++ b/solution.py
@@ -168,22 +168,20 @@
     feature_count = users.shape[1]
     item_sub = hot_table.shape[0]
     sb_count = lax.axis_size("sb")
-    users_part = lax.all_gather(user_half, "sb", axis=0, tiled=True)
-    pos_part = lax.all_gather(positives, "sb", axis=0, tiled=True)
-    hot_part = lax.all_gather(hot_half, "sa", axis=0, tiled=True)
-    owner = pos_part // item_sub
-    local = (owner // sb_count) * item_sub + pos_part % item_sub
-    local = jnp.where(owner % sb_count == lax.axis_index("sb"), local, hot_part.shape[0])
-    user_hot_part, item_part = hot_terms(users_part, local, hot_part)
-    user_hot = lax.psum_scatter(user_hot_part, "sb", scatter_dimension=0, tiled=True)
-    item_grad = lax.psum_scatter(item_part, "sa", scatter_dimension=0, tiled=True)
-    hot_grad = lax.psum(item_grad, "grp")
+    pos_count = positives.shape[1]
     devices = cold_requests.shape[1]
     slot_count = cold_requests.shape[2]
     requests = cold_requests.reshape(devices, slot_count)
     live_slots = lax.iota(jnp.int32, slot_count)[None, :] < cold_counts.reshape(devices, 1)
     asked_rows = lax.all_to_all(requests, ("grp", "sa", "sb"), split_axis=0, concat_axis=0, tiled=True)
     found = onehot_gather(cold_half, asked_rows.reshape(-1))
+    packed = jnp.concatenate(
+        [user_half, (positives // LANES).astype(jnp.bfloat16), (positives % LANES).astype(jnp.bfloat16)],
+        axis=1,
+    )
+    packed_part = lax.all_gather(packed, "sb", axis=0, tiled=True)
+    hot_part = lax.all_gather(hot_half, "sa", axis=0, tiled=True)
+    found, packed_part, hot_part = lax.optimization_barrier((found, packed_part, hot_part))
     fetched = lax.all_to_all(
         found.reshape(devices, slot_count, feature_count),
         ("grp", "sa", "sb"),
@@ -191,6 +189,18 @@
         concat_axis=0,
         tiled=True,
     )
+    users_part = packed_part[:, :feature_count]
+    pos_hi = packed_part[:, feature_count:feature_count + pos_count].astype(jnp.int32)
+    pos_lo = packed_part[:, feature_count + pos_count:].astype(jnp.int32)
+    hi_per_item = item_sub // LANES
+    owner = pos_hi // hi_per_item
+    local_hi = (owner // sb_count) * hi_per_item + pos_hi % hi_per_item
+    local = jnp.where(owner % sb_count == lax.axis_index("sb"), local_hi * LANES + pos_lo, hot_part.shape[0])
+    user_hot_part, item_part = hot_terms(users_part, local, hot_part)
+    fetched, user_hot_part, item_part = lax.optimization_barrier((fetched, user_hot_part, item_part))
+    user_hot = lax.psum_scatter(user_hot_part, "sb", scatter_dimension=0, tiled=True)
+    item_grad = lax.psum_scatter(item_part, "sa", scatter_dimension=0, tiled=True)
+    hot_grad = lax.psum(item_grad, "grp")
     flat_rows = fetched.reshape(devices * slot_count, feature_count)
     scores = jnp.einsum("uk,rk->ur", user_half, flat_rows, preferred_element_type=jnp.float32)
     weights = (jax.nn.sigmoid(scores) * live_slots.reshape(1, -1).astype(jnp.float32)).astype(

time: 358 us -> 319 us (0.89)
  waiting for transfers between devices: 152 us -> 107 us
  blocking collectives: 13.1 us -> 0 us
  other arithmetic: 9.14 us -> 17.8 us
  starting transfers between devices: 26.6 us -> 31.2 us
  local copies, waits for them, and re-layouts: 8.84 us -> 13.4 us
    all_to_all x1, waiting for transfers between devices: 61.7 us -> 0.01 us  [body(): lax.all_to_all(found.reshape(devices, slot_count, feature_count), ('grp',...]
    all_to_all x1, waiting for transfers between devices: 0.01 us -> 61.6 us  [body(): lax.all_to_all(row_terms, ('grp', 'sa', 'sb'), split_axis=0, concat_axis=...]
    psum x1, waiting for transfers between devices: 66.3 us -> 25.8 us  [body(): hot_grad = lax.psum(item_grad, 'grp')]
    all_gather x1 -> x0, blocking collectives: 13.1 us -> none  [body(): pos_part = lax.all_gather(positives, 'sb', axis=0, tiled=True)]
    all_gather x1, waiting for transfers between devices: 23.2 us -> 10.9 us  [body(): packed_part = lax.all_gather(packed, 'sb', axis=0, tiled=True)]
    all_to_all x1, waiting for transfers between devices: 0.01 us -> 8.51 us  [body(): lax.all_to_all(requests, ('grp', 'sa', 'sb'), split_axis=0, concat_axis=0...]
    select_n x1, other arithmetic: 0.58 us -> 6.4 us  [hot_terms(): pos_lo = (positives % LANES).reshape(subtiles, width)]
    all_to_all x1, starting transfers between devices: 5.95 us -> 10.2 us  [body(): lax.all_to_all(row_terms, ('grp', 'sa', 'sb'), split_axis=0, concat_axis=...]
  transfers between devices with their start and end apart: 8 -> 8, of which waited for: 3 -> 4; matrix products, arithmetic and copies ran while one was open for 12% -> 18% of each run, Pallas kernels for 23% -> 33%
where the time goes in v3:
time: 319 us; the launch traced here: 318 us
  waiting for transfers between devices  107 us (34%)
  Pallas kernels  103 us (32%)
  starting transfers between devices  31.2 us (10%)
  matrix products  30.6 us (10%)
  other arithmetic  17.8 us (6%)
  between operations  13.9 us (4%)
  local copies, waits for them, and re-layouts  13.4 us (4%)
    pallas_call x1, Pallas kernels, hot_terms(): pl.pallas_call(functools.partial(_hot_kernel, sub_users=sub_users), grid=...  64.1 us
    all_to_all x1, waiting for transfers between devices, body(): lax.all_to_all(row_terms, ('grp', 'sa', 'sb'), split_axis=0, concat_axis=...  61.6 us
    psum x1, waiting for transfers between devices, body(): hot_grad = lax.psum(item_grad, 'grp')  25.8 us
    pallas_call x1, Pallas kernels, onehot_scatter_add(): pl.pallas_call(_scatter_kernel, grid=(n // chunk,), in_specs=[pl.BlockSpe...  22.2 us
    pallas_call x1, Pallas kernels, onehot_gather(): pl.pallas_call(_gather_kernel, grid=(n // chunk,), in_specs=[pl.BlockSpec...  17 us
    dot_general x1, matrix products, body(): user_cold = jnp.dot(weights, flat_rows, preferred_element_type=jnp.float32)  12.6 us
    all_to_all x1, starting transfers between devices, body(): lax.all_to_all(requests, ('grp', 'sa', 'sb'), split_axis=0, concat_axis=0...  11.2 us
    dot_general x1, matrix products, body(): jnp.einsum('uk,rk->ur', user_half, flat_rows, preferred_element_type=jnp....  11.1 us
  transfers between devices with their start and end apart: 8, of which 4 were waited for; matrix products, arithmetic and copies ran while one was open for 18% of the time, Pallas kernels for 33%

profile of v3, /device:TPU:0, one launch (start us, length us, event | category | flops | bytes accessed | tf_op | source)
XLA Modules:
  0.0 317.7 jit_solution(16900127824837102081)
XLA Ops:
  7.2 0.0 copy-start.3
  7.2 0.0 all-gather.5.cloned.1.call-start
  7.2 1.8 convert_element_type.42
  9.0 0.0 all-gather.5.cloned.1.call-update
  9.1 0.0 all-gather.3.cloned.1.call-start
  9.1 1.0 convert_element_type.39
  10.1 0.9 copy.25
  11.0 0.3 fusion.14
  11.2 0.8 pad_maximum_fusion
  12.1 0.0 all-gather.3.cloned.1.call-update
  12.1 11.2 %all-to-all-start = ((s32[128,1,128]{2,1,0:T(1,128)}), s32[128,1,128]{2,1,0:T(1,128)S(1)}, u32[]{:S(2)}, u32[]{:S(2)}) async-start(s32[128,1,128]{2,1,0:T(1,128)} %bitcast), calls=%async_computation | async-start | bytes 131072 | tf_op jit(solution)/shard_map/all_to_all | solution.py:176
  23.3 0.0 copy-done.3
  23.3 0.7 convert_element_type.38.table_ref
  24.0 8.5 %all-to-all-done = s32[128,1,128]{2,1,0:T(1,128)S(1)} async-done(((s32[128,1,128]{2,1,0:T(1,128)}), s32[128,1,128]{2,1,0:T(1,128)S(1)}, u32[]{:S(2)}, u32[]{:S(2)}) %all-to-all-start) | async-done | bytes 65568 | tf_op jit(solution)/shard_map/all_to_all | solution.py:176
  32.5 0.0 copy-start.5
  32.5 4.9 %copy.24.idx_ref = s32[16384,1]{1,0:T(8,128)} copy(s32[16384,1]{0,1:T(1,128)S(1)} %bitcast.18) | data formatting | bytes 131072 | tf_op jit(solution)/shard_map/reshape;reshape | solution.py:116
  37.4 0.0 copy-done.5
  37.4 17.0 %shard_map.136 = bf16[16384,128]{1,0:T(8,128)(2,1)} custom-call(s32[16384,1]{1,0:T(8,128)} %copy.24.idx_ref, bf16[1024,128]{1,0:T(8,128)(2,1)} %convert_element_type.38.table_ref), custom_call_target="tpu_custom_call" | custom-call | tf_op jit(solution)/shard_map/pallas_call | solution.py:107
  54.4 0.0 all-gather.5.cloned.1.call-done.h_ref
  54.4 10.9 %all-gather.3.cloned.1.call-done = bf16[4096,160]{1,0:T(8,128)(2,1)} async-done(((bf16[512,160]{1,0:T(8,128)(2,1)}), bf16[4096,160]{1,0:T(8,128)(2,1)}) %all-gather.3.cloned.1.call-update) | async-done | bytes 1310736 | tf_op jit(solution)/shard_map/all_gather | solution.py:182
  65.3 0.0 copy-start.9
  65.3 0.0 copy-start.1
  65.3 9.6 %all-to-all-start.1 = ((bf16[128,128,128]{2,1,0:T(8,128)(2,1)}), bf16[128,128,128]{2,1,0:T(8,128)(2,1)}, u32[]{:S(2)}, u32[]{:S(2)}) async-start(bf16[128,128,128]{2,1,0:T(8,128)(2,1)} %bitcast.17), calls=%async_computation.1 | async-start | bytes 8388608 | tf_op jit(solution)/shard_map/all_to_all | solution.py:185
  75.0 0.0 reduce-scatter.5.cloned.1.call-start
  75.0 0.0 copy-start.2
  75.0 0.0 copy-done.9
  75.0 0.1 convert_bitcast_fusion
  75.1 0.0 copy-done.1
  75.1 1.1 slice.9.u_ref
  76.2 0.8 copy-done.2
  77.0 6.4 %add_select_fusion = (s32[4096,16]{1,0:T(8,128)}, s32[4096,16]{1,0:T(8,128)S(1)}) fusion(bf16[4096,160]{1,0:T(8,128)(2,1)S(1)} %copy-done.2, s32[]{:T(128)S(6)} %axis_index.12), kind=kLoop, calls=%fused_computation.6 | loop fusion | flops 3735552 | bytes 786436 | tf_op jit(solution)/shard_map/jit(remainder)/select_n | solution.py:72
  83.4 2.8 reshape.58.pl_ref
  86.2 2.4 add_select_fusion.1
  88.6 2.8 reshape.57.ph_ref
  91.4 64.1 %shard_map.137 = (f32[4096,128]{1,0:T(8,128)}, f32[4096,128]{1,0:T(8,128)}) custom-call(bf16[4096,128]{1,0:T(8,128)(2,1)} %slice.9.u_ref, bf16[4096,128]{1,0:T(8,128)(2,1)} %all-gather.5.cloned.1.call-done.h_ref, s32[512,128]{1,0:T(8,128)} %reshape.57.ph_ref, s32[512,128]{1,0:T(8,128)} %reshape.58.pl_ref), custom_call_target="tpu_custom_call" | custom-call | tf_op jit(solution)/shard_map/pallas_call | solution.py:74
  155.5 0.0 all-to-all-done.1
  155.5 0.0 reduce-scatter.5.cloned.1.call-update
  155.5 11.1 %multiply_convert_fusion = bf16[16384,512]{1,0:T(8,128)(2,1)S(1)} fusion(bf16[16384,128]{1,0:T(8,128)(2,1)} %bitcast.3, bf16[512,128]{1,0:T(8,128)(2,1)S(1)} %convert_element_type.39, f32[16384]{0:T(1024)S(1)} %convert_bitcast_fusion), kind=kOutput, calls=%fused_computation | convolution fusion | flops 2189426688 | bytes 21168128 | tf_op jit(solution)/shard_map/uk,rk->ur/dot_general | solution.py:205
  166.6 0.0 copy-start
  166.6 6.9 %convolution_convert_fusion = bf16[16384,128]{1,0:T(8,128)(2,1)} fusion(bf16[16384,512]{1,0:T(8,128)(2,1)S(1)} %multiply_convert_fusion, bf16[512,128]{1,0:T(8,128)(2,1)S(1)} %convert_element_type.39), kind=kOutput, calls=%fused_computation.1 | convolution fusion | flops 2149580800 | bytes 21102592 | tf_op jit(solution)/shard_map/ur,uk->rk/dot_general | solution.py:210
  173.5 0.2 copy-done
  173.7 10.2 %all-to-all-start.2 = ((bf16[128,128,128]{2,1,0:T(8,128)(2,1)}), bf16[128,128,128]{2,1,0:T(8,128)(2,1)}, u32[]{:S(2)}, u32[]{:S(2)}) async-start(bf16[128,128,128]{2,1,0:T(8,128)(2,1)} %bitcast.16), calls=%async_computation.4 | async-start | bytes 8388608 | tf_op jit(solution)/shard_map/all_to_all | solution.py:214
  183.9 0.0 reduce-scatter.3.cloned.1.call-start
  184.0 0.5 reduce-scatter.3.cloned.1.call-update
  184.5 0.0 all-reduce.2.cloned.1.call-start
  184.6 61.6 %all-to-all-done.2 = bf16[128,128,128]{2,1,0:T(8,128)(2,1)} async-done(((bf16[128,128,128]{2,1,0:T(8,128)(2,1)}), bf16[128,128,128]{2,1,0:T(8,128)(2,1)}, u32[]{:S(2)}, u32[]{:S(2)}) %all-to-all-start.2) | async-done | bytes 4194336 | tf_op jit(solution)/shard_map/all_to_all | solution.py:214
  246.2 0.0 copy-start.6
  246.2 22.2 %shard_map.138 = f32[1024,128]{1,0:T(8,128)} custom-call(s32[1,16384]{1,0:T(1,128)} %bitcast.19, bf16[16384,128]{1,0:T(8,128)(2,1)} %bitcast.8.val_ref), custom_call_target="tpu_custom_call" | custom-call | tf_op jit(solution)/shard_map/pallas_call | solution.py:136
  268.4 0.0 copy-done.6
  268.4 0.0 copy-start.8
  268.4 0.0 copy-start.10
  268.4 2.2 multiply_subtract_fusion
  270.5 0.0 reduce-scatter.5.cloned.1.call-done
  270.5 0.0 all-reduce.2.cloned.1.call-update
  270.6 0.0 copy-start.4
  270.6 0.0 copy-start.7
  270.6 0.0 reduce-scatter.3.cloned.1.call-done
  270.6 0.0 copy-done.8
  270.6 0.0 copy-done.10
  270.6 12.6 %multiply_subtract_fusion.2 = (f32[512,128]{1,0:T(8,128)}, f32[512,128]{1,0:T(8,128)}) fusion(f32[512,128]{1,0:T(8,128)S(1)} %copy-done.8, f32[512,128]{1,0:T(8,128)S(1)} %copy-done.10, f32[512,128]{1,0:T(8,128)} %reduce-scatter.3.cloned.1.call-done, bf16[16384,512]{1,0:T(8,128)(2,1)} %copy-done, bf16[16384,128]{1,0:T(8,128)(2,1)} %bitcast.3), kind=kOutput, calls=%fused_computation.49 | convolution fusion | flops 2147876864 | bytes 22282240 | tf_op jit(solution)/shard_map/dot_general | solution.py:209
  283.2 25.8 %all-reduce.2.cloned.1.call-done = f32[1024,128]{1,0:T(8,128)} async-done(((f32[1024,128]{1,0:T(8,128)}), f32[1024,128]{1,0:T(8,128)}) %all-reduce.2.cloned.1.call-update) | async-done | bytes 524304 | tf_op jit(solution)/shard_map/psum | solution.py:203
  309.1 0.0 copy-done.4
  309.1 0.0 copy-done.7
  309.1 2.1 multiply_subtract_fusion.1
Async XLA Ops:
  7.2 16.1 %copy-start.3 = (f32[1024,128]{1,0:T(8,128)S(1)}, f32[1024,128]{1,0:T(8,128)}, u32[]{:S(2)}) copy-start(f32[1024,128]{1,0:T(8,128)} %param.14) | copy-start | bytes 1572868
  7.2 47.3 %all-gather.5.cloned.1.call-start = ((), (), s32[]{:S(2)}) async-start(), calls=%async_computation.6 | async-start | bytes 1310720 | tf_op jit(solution)/shard_map/all_gather | solution.py:183
  9.1 56.3 %all-gather.3.cloned.1.call-start = ((), (), s32[]{:S(2)}) async-start(), calls=%async_computation.5 | async-start | bytes 2359296 | tf_op jit(solution)/shard_map/all_gather | solution.py:182
  12.1 20.4 %all-to-all-start = ((s32[128,1,128]{2,1,0:T(1,128)}), s32[128,1,128]{2,1,0:T(1,128)S(1)}, u32[]{:S(2)}, u32[]{:S(2)}) async-start(s32[128,1,128]{2,1,0:T(1,128)} %bitcast), calls=%async_computation | async-start | bytes 131072 | tf_op jit(solution)/shard_map/all_to_all | solution.py:176
  32.5 4.9 %copy-start.5 = (s32[128,1,128]{2,1,0:T(1,128)}, s32[128,1,128]{2,1,0:T(1,128)S(1)}, u32[]{:S(2)}) copy-start(s32[128,1,128]{2,1,0:T(1,128)S(1)} %all-to-all-done) | copy-start | bytes 196612
  65.3 9.7 %copy-start.9 = (s32[1,128]{1,0:T(1,128)S(1)}, s32[1,128]{1,0:T(1,128)}, u32[]{:S(2)}) copy-start(s32[1,128]{1,0:T(1,128)} %param.17) | copy-start | bytes 1540
  65.3 9.8 %copy-start.1 = (bf16[4096,160]{1,0:T(8,128)(2,1)S(1)}, bf16[4096,160]{1,0:T(8,128)(2,1)}, u32[]{:S(2)}) copy-start(bf16[4096,160]{1,0:T(8,128)(2,1)} %all-gather.3.cloned.1.call-done) | copy-start | bytes 3932164
  65.3 90.1 %all-to-all-start.1 = ((bf16[128,128,128]{2,1,0:T(8,128)(2,1)}), bf16[128,128,128]{2,1,0:T(8,128)(2,1)}, u32[]{:S(2)}, u32[]{:S(2)}) async-start(bf16[128,128,128]{2,1,0:T(8,128)(2,1)} %bitcast.17), calls=%async_computation.1 | async-start | bytes 8388608 | tf_op jit(solution)/shard_map/all_to_all | solution.py:185
  75.0 195.6 %reduce-scatter.5.cloned.1.call-start = ((), (), s32[]{:S(2)}) async-start(), calls=%async_computation.8 | async-start | bytes 2621440 | tf_op jit(solution)/shard_map/reduce_scatter | solution.py:202
  75.0 2.0 copy-start.2
  166.6 7.1 %copy-start = (bf16[16384,512]{1,0:T(8,128)(2,1)}, bf16[16384,512]{1,0:T(8,128)(2,1)S(1)}, u32[]{:S(2)}) copy-start(bf16[16384,512]{1,0:T(8,128)(2,1)S(1)} %multiply_convert_fusion) | copy-start | bytes 50331652
  173.7 72.5 %all-to-all-start.2 = ((bf16[128,128,128]{2,1,0:T(8,128)(2,1)}), bf16[128,128,128]{2,1,0:T(8,128)(2,1)}, u32[]{:S(2)}, u32[]{:S(2)}) async-start(bf16[128,128,128]{2,1,0:T(8,128)(2,1)} %bitcast.16), calls=%async_computation.4 | async-start | bytes 8388608 | tf_op jit(solution)/shard_map/all_to_all | solution.py:214
  183.9 86.7 %reduce-scatter.3.cloned.1.call-start = ((), (), s32[]{:S(2)}) async-start(), calls=%async_computation.7 | async-start | bytes 2359296 | tf_op jit(solution)/shard_map/reduce_scatter | solution.py:201
  184.5 124.5 %all-reduce.2.cloned.1.call-start = ((), (), s32[]{:S(2)}) async-start(), calls=%async_computation.9 | async-start | bytes 1048576 | tf_op jit(solution)/shard_map/psum | solution.py:203
  246.2 22.2 %copy-start.6 = (f32[1024,128]{1,0:T(8,128)S(1)}, f32[1024,128]{1,0:T(8,128)}, u32[]{:S(2)}) copy-start(f32[1024,128]{1,0:T(8,128)} %param.15) | copy-start | bytes 1572868
  268.4 2.3 copy-start.8
  268.4 2.3 copy-start.10
  270.6 38.5 %copy-start.4 = (f32[1024,128]{1,0:T(8,128)S(1)}, f32[1024,128]{1,0:T(8,128)}, u32[]{:S(2)}) copy-start(f32[1024,128]{1,0:T(8,128)} %param.12) | copy-start | bytes 1572868
  270.6 38.5 %copy-start.7 = (f32[1024,128]{1,0:T(8,128)S(1)}, f32[1024,128]{1,0:T(8,128)}, u32[]{:S(2)}) copy-start(f32[1024,128]{1,0:T(8,128)} %param.13) | copy-start | bytes 1572868
Sparse Core Ops, SparseCore 0:
  10.2 26.9 all-gather.4
  39.5 25.7 all-gather.2
  155.6 30.7 reduce-scatter.4
  188.6 52.6 reduce-scatter.2
  270.7 38.3 all-reduce.1

commit v4 on v3

--- a/solution.py
+++ b/solution.py
@@ -21,7 +21,12 @@
     return lax.dot_general(a, b, (((0,), (0,)), ((), ())), preferred_element_type=jnp.float32)
 
 
-def _hot_kernel(u_ref, h_ref, ph_ref, pl_ref, up_ref, ip_ref, m_ref, *, sub_users):
+def _hot_kernel(u_ref, h_ref, ph_ref, pl_ref, dep_ref, *rest, sub_users, chained):
+    del dep_ref
+    if chained:
+        _, ipin_ref, up_ref, ip_ref, m_ref = rest
+    else:
+        up_ref, ip_ref, m_ref = rest
     i = pl.program_id(0)
     items = h_ref.shape[0]
     nh = items // LANES
@@ -57,31 +62,48 @@
 
     @pl.when(i == 0)
     def _():
-        ip_ref[...] = jnp.zeros_like(ip_ref)
+        if chained:
+            ip_ref[...] = ipin_ref[...]
+        else:
+            ip_ref[...] = jnp.zeros_like(ip_ref)
 
     ip_ref[...] += _tn(w, u)
 
 
-def hot_terms(user_half, positives, hot_rows, tile=512, sub_users=8):
+def hot_prepare(positives, sub_users=8):
+    users, pos_count = positives.shape
+    subtiles = users // sub_users
+    width = sub_users * pos_count
+    return (
+        (positives // LANES).reshape(subtiles, width),
+        (positives % LANES).reshape(subtiles, width),
+    )
+
+
+def hot_terms(user_half, pos_hi, pos_lo, hot_rows, first, count, dep, prev=None, tile=512, sub_users=8):
     users, k = user_half.shape
     items = hot_rows.shape[0]
-    pos_count = positives.shape[1]
-    subtiles = users // sub_users
-    width = sub_users * pos_count
-    pos_hi = (positives // LANES).reshape(subtiles, width)
-    pos_lo = (positives % LANES).reshape(subtiles, width)
+    width = pos_hi.shape[1]
     per_tile = tile // sub_users
+    in_specs = [
+        pl.BlockSpec((tile, k), lambda i: (first + i, 0)),
+        pl.BlockSpec((items, k), lambda i: (0, 0)),
+        pl.BlockSpec((per_tile, width), lambda i: (first + i, 0)),
+        pl.BlockSpec((per_tile, width), lambda i: (first + i, 0)),
+        pl.BlockSpec(memory_space=pl.ANY),
+    ]
+    args = [user_half, hot_rows, pos_hi, pos_lo, dep]
+    aliases = {}
+    if prev is not None:
+        in_specs += [pl.BlockSpec(memory_space=pl.ANY), pl.BlockSpec((items, k), lambda i: (0, 0))]
+        args += list(prev)
+        aliases = {5: 0, 6: 1}
     return pl.pallas_call(
-        functools.partial(_hot_kernel, sub_users=sub_users),
-        grid=(users // tile,),
-        in_specs=[
-            pl.BlockSpec((tile, k), lambda i: (i, 0)),
-            pl.BlockSpec((items, k), lambda i: (0, 0)),
-            pl.BlockSpec((per_tile, width), lambda i: (i, 0)),
-            pl.BlockSpec((per_tile, width), lambda i: (i, 0)),
-        ],
+        functools.partial(_hot_kernel, sub_users=sub_users, chained=prev is not None),
+        grid=(count,),
+        in_specs=in_specs,
         out_specs=[
-            pl.BlockSpec((tile, k), lambda i: (i, 0)),
+            pl.BlockSpec((tile, k), lambda i: (first + i, 0)),
             pl.BlockSpec((items, k), lambda i: (0, 0)),
         ],
         out_shape=[
@@ -89,16 +111,18 @@
             jax.ShapeDtypeStruct((items, k), jnp.float32),
         ],
         scratch_shapes=[pltpu.VMEM((tile, items), jnp.float32)],
+        input_output_aliases=aliases,
         compiler_params=pltpu.CompilerParams(dimension_semantics=("arbitrary",)),
-    )(user_half, hot_rows, pos_hi, pos_lo)
+    )(*args)
 
 
 def _gather_kernel(idx_ref, table_ref, out_ref):
     rows = table_ref.shape[0]
-    onehot = (idx_ref[...] == lax.broadcasted_iota(jnp.int32, (1, rows), 1)).astype(jnp.bfloat16)
-    out_ref[...] = jnp.dot(onehot, table_ref[...], preferred_element_type=jnp.float32).astype(
-        out_ref.dtype
-    )
+    chunk = idx_ref.shape[1]
+    onehot = (idx_ref[...] == lax.broadcasted_iota(jnp.int32, (rows, chunk), 0)).astype(
+        jnp.bfloat16
+    )
+    out_ref[...] = _tn(onehot, table_ref[...]).astype(out_ref.dtype)
 
 
 def onehot_gather(table, idx, chunk=1024):
@@ -108,12 +132,12 @@
         _gather_kernel,
         grid=(n // chunk,),
         in_specs=[
-            pl.BlockSpec((chunk, 1), lambda i: (i, 0)),
+            pl.BlockSpec((1, chunk), lambda i: (0, i)),
             pl.BlockSpec((rows, k), lambda i: (0, 0)),
         ],
         out_specs=pl.BlockSpec((chunk, k), lambda i: (i, 0)),
         out_shape=jax.ShapeDtypeStruct((n, k), table.dtype),
-    )(idx.reshape(n, 1), table)
+    )(idx.reshape(1, n), table)
 
 
 def _scatter_kernel(idx_ref, val_ref, out_ref):
@@ -181,7 +205,6 @@
     )
     packed_part = lax.all_gather(packed, "sb", axis=0, tiled=True)
     hot_part = lax.all_gather(hot_half, "sa", axis=0, tiled=True)
-    found, packed_part, hot_part = lax.optimization_barrier((found, packed_part, hot_part))
     fetched = lax.all_to_all(
         found.reshape(devices, slot_count, feature_count),
         ("grp", "sa", "sb"),
@@ -196,11 +219,11 @@
     owner = pos_hi // hi_per_item
     local_hi = (owner // sb_count) * hi_per_item + pos_hi % hi_per_item
     local = jnp.where(owner % sb_count == lax.axis_index("sb"), local_hi * LANES + pos_lo, hot_part.shape[0])
-    user_hot_part, item_part = hot_terms(users_part, local, hot_part)
-    fetched, user_hot_part, item_part = lax.optimization_barrier((fetched, user_hot_part, item_part))
-    user_hot = lax.psum_scatter(user_hot_part, "sb", scatter_dimension=0, tiled=True)
-    item_grad = lax.psum_scatter(item_part, "sa", scatter_dimension=0, tiled=True)
-    hot_grad = lax.psum(item_grad, "grp")
+    pos_hi_t, pos_lo_t = hot_prepare(local)
+    tiles = users_part.shape[0] // 512
+    half = tiles // 2
+    part_a = hot_terms(users_part, pos_hi_t, pos_lo_t, hot_part, 0, half, found)
+    fetched, part_a = lax.optimization_barrier((fetched, part_a))
     flat_rows = fetched.reshape(devices * slot_count, feature_count)
     scores = jnp.einsum("uk,rk->ur", user_half, flat_rows, preferred_element_type=jnp.float32)
     weights = (jax.nn.sigmoid(scores) * live_slots.reshape(1, -1).astype(jnp.float32)).astype(
@@ -212,6 +235,13 @@
     ).astype(jnp.bfloat16)
     row_terms = row_terms.reshape(devices, slot_count, feature_count)
     returned = lax.all_to_all(row_terms, ("grp", "sa", "sb"), split_axis=0, concat_axis=0, tiled=True)
+    user_hot_part, item_part = hot_terms(
+        users_part, pos_hi_t, pos_lo_t, hot_part, half, tiles - half, row_terms, prev=part_a
+    )
+    returned, user_hot_part, item_part = lax.optimization_barrier((returned, user_hot_part, item_part))
+    user_hot = lax.psum_scatter(user_hot_part, "sb", scatter_dimension=0, tiled=True)
+    item_grad = lax.psum_scatter(item_part, "sa", scatter_dimension=0, tiled=True)
+    hot_grad = lax.psum(item_grad, "grp")
     cold_grad = onehot_scatter_add(
         asked_rows.reshape(-1),
         returned.reshape(devices * slot_count, feature_count),

time: 319 us -> 335 us (1.050)
  waiting for transfers between devices: 107 us -> 133 us
  local copies, waits for them, and re-layouts: 13.4 us -> 8.52 us
  starting transfers between devices: 31.2 us -> 26.5 us
    all_to_all x1, waiting for transfers between devices: 61.6 us -> 18 us  [body(): lax.all_to_all(row_terms, ('grp', 'sa', 'sb'), split_axis=0, concat_axis=...]
    all_gather x1, waiting for transfers between devices: 0.01 us -> 38 us  [body(): hot_part = lax.all_gather(hot_half, 'sa', axis=0, tiled=True)]
    reduce_scatter x1, waiting for transfers between devices: 0.02 us -> 35.7 us  [body(): lax.psum_scatter(user_hot_part, 'sb', scatter_dimension=0, tiled=True)]
    all_gather x1, waiting for transfers between devices: 10.9 us -> 0.02 us  [body(): packed_part = lax.all_gather(packed, 'sb', axis=0, tiled=True)]
    psum x1, waiting for transfers between devices: 25.8 us -> 32 us  [body(): hot_grad = lax.psum(item_grad, 'grp')]
    another operation x1 -> x0, local copies, waits for them, and re-layouts: 4.89 us -> none  [onehot_gather(): idx.reshape(n, 1)]
    pallas_call x1 -> x2, Pallas kernels: 64.1 us -> 67.8 us  [hot_terms(): pl.pallas_call(functools.partial(_hot_kernel, sub_users=sub_users, chaine...]
    all_to_all x1, starting transfers between devices: 9.62 us -> 5.95 us  [body(): lax.all_to_all(found.reshape(devices, slot_count, feature_count), ('grp',...]
  transfers between devices with their start and end apart: 8 -> 8, of which waited for: 4 -> 5; matrix products, arithmetic and copies ran while one was open for 18% -> 10% of each run, Pallas kernels for 33% -> 31%
where the time goes in v4:
time: 335 us; the launch traced here: 334 us
  waiting for transfers between devices  133 us (40%)
  Pallas kernels  104 us (31%)
  matrix products  30.2 us (9%)
  starting transfers between devices  26.5 us (8%)
  other arithmetic  18.1 us (5%)
  between operations  13.9 us (4%)
  local copies, waits for them, and re-layouts  8.52 us (3%)
    pallas_call x2, Pallas kernels, hot_terms(): pl.pallas_call(functools.partial(_hot_kernel, sub_users=sub_users, chaine...  67.8 us
    all_gather x1, waiting for transfers between devices, body(): hot_part = lax.all_gather(hot_half, 'sa', axis=0, tiled=True)  38 us
    reduce_scatter x1, waiting for transfers between devices, body(): lax.psum_scatter(user_hot_part, 'sb', scatter_dimension=0, tiled=True)  35.7 us
    psum x1, waiting for transfers between devices, body(): hot_grad = lax.psum(item_grad, 'grp')  32 us
    pallas_call x1, Pallas kernels, onehot_scatter_add(): pl.pallas_call(_scatter_kernel, grid=(n // chunk,), in_specs=[pl.BlockSpe...  22.4 us
    all_to_all x1, waiting for transfers between devices, body(): lax.all_to_all(row_terms, ('grp', 'sa', 'sb'), split_axis=0, concat_axis=...  18 us
    pallas_call x1, Pallas kernels, onehot_gather(): pl.pallas_call(_gather_kernel, grid=(n // chunk,), in_specs=[pl.BlockSpec...  14.2 us
    dot_general x1, matrix products, body(): user_cold = jnp.dot(weights, flat_rows, preferred_element_type=jnp.float32)  12.4 us
  transfers between devices with their start and end apart: 8, of which 5 were waited for; matrix products, arithmetic and copies ran while one was open for 10% of the time, Pallas kernels for 31%

profile of v4, /device:TPU:0, one launch (start us, length us, event | category | flops | bytes accessed | tf_op | source)
XLA Modules:
  0.0 334.3 jit_solution(14382112799579878055)
XLA Ops:
  7.2 0.0 copy-start.2
  7.2 0.0 all-gather.3.cloned.1.call-start
  7.2 1.0 convert_element_type.39
  8.2 0.9 copy.25
  9.1 0.3 fusion.14
  9.4 0.8 pad_maximum_fusion
  10.2 0.0 all-gather.3.cloned.1.call-update
  10.2 11.2 %all-to-all-start = ((s32[128,1,128]{2,1,0:T(1,128)}), s32[128,1,128]{2,1,0:T(1,128)S(1)}, u32[]{:S(2)}, u32[]{:S(2)}) async-start(s32[128,1,128]{2,1,0:T(1,128)} %bitcast), calls=%async_computation | async-start | bytes 131072 | tf_op jit(solution)/shard_map/all_to_all | solution.py:200
  21.4 0.0 copy-done.2
  21.4 0.7 convert_element_type.38.table_ref
  22.2 8.5 %all-to-all-done = s32[128,1,128]{2,1,0:T(1,128)S(1)} async-done(((s32[128,1,128]{2,1,0:T(1,128)}), s32[128,1,128]{2,1,0:T(1,128)S(1)}, u32[]{:S(2)}, u32[]{:S(2)}) %all-to-all-start) | async-done | bytes 65568 | tf_op jit(solution)/shard_map/all_to_all | solution.py:200
  30.7 0.0 copy-start.4
  30.7 0.6 copy-done.4
  31.3 14.2 %shard_map.136.dep_ref = bf16[16384,128]{1,0:T(8,128)(2,1)} custom-call(s32[1,16384]{1,0:T(1,128)} %bitcast.18, bf16[1024,128]{1,0:T(8,128)(2,1)} %convert_element_type.38.table_ref), custom_call_target="tpu_custom_call" | custom-call | tf_op jit(solution)/shard_map/pallas_call | solution.py:131
  45.5 0.0 copy-start.3
  45.5 0.0 copy-start.8
  45.5 6.0 %all-to-all-start.1 = ((bf16[128,128,128]{2,1,0:T(8,128)(2,1)}), bf16[128,128,128]{2,1,0:T(8,128)(2,1)}, u32[]{:S(2)}, u32[]{:S(2)}) async-start(bf16[128,128,128]{2,1,0:T(8,128)(2,1)} %bitcast.17), calls=%async_computation.1 | async-start | bytes 8388608 | tf_op jit(solution)/shard_map/all_to_all | solution.py:208
  51.4 0.0 all-gather.5.cloned.1.call-start
  51.5 0.0 copy-done.3
  51.5 0.7 convert_element_type.42
  52.2 0.0 all-gather.5.cloned.1.call-update
  52.2 0.0 copy-done.8
  52.3 0.1 convert_bitcast_fusion
  52.3 0.0 all-gather.3.cloned.1.call-done
  52.4 7.6 %add_select_fusion = (s32[4096,16]{1,0:T(8,128)}, s32[4096,16]{1,0:T(8,128)S(1)}) fusion(bf16[4096,160]{1,0:T(8,128)(2,1)} %all-gather.3.cloned.1.call-done, s32[]{:T(128)S(6)} %axis_index.12), kind=kLoop, calls=%fused_computation.6 | loop fusion | flops 3735552 | bytes 786436 | tf_op jit(solution)/shard_map/jit(remainder)/select_n | solution.py:79
  60.0 2.8 reshape.57.pl_ref
  62.8 2.5 add_select_fusion.1
  65.3 0.0 copy-start.1
  65.3 2.9 reshape.56.ph_ref
  68.3 0.0 copy-done.1
  68.3 1.0 slice.12.u_ref
  69.3 38.0 %all-gather.5.cloned.1.call-done.h_ref = bf16[4096,128]{1,0:T(8,128)(2,1)} async-done(((bf16[1024,128]{1,0:T(8,128)(2,1)}), bf16[4096,128]{1,0:T(8,128)(2,1)}) %all-gather.5.cloned.1.call-update) | async-done | bytes 1048592 | tf_op jit(solution)/shard_map/all_gather | solution.py:207
  107.3 33.4 %shard_map.137 = (f32[4096,128]{1,0:T(8,128)}, f32[4096,128]{1,0:T(8,128)}) custom-call(bf16[4096,128]{1,0:T(8,128)(2,1)} %slice.12.u_ref, bf16[4096,128]{1,0:T(8,128)(2,1)} %all-gather.5.cloned.1.call-done.h_ref, s32[512,128]{1,0:T(8,128)} %reshape.56.ph_ref, s32[512,128]{1,0:T(8,128)} %reshape.57.pl_ref, bf16[16384,128]{1,0:T(8,128)(2,1)} %shard_map.136.dep_ref), custom_call_target="tpu_custom_call" | custom-call | tf_op jit(solution)/shard_map/pallas_call | solution.py:101
  140.7 0.0 all-to-all-done.1
  140.7 10.9 %multiply_convert_fusion = bf16[16384,512]{1,0:T(8,128)(2,1)S(1)} fusion(bf16[16384,128]{1,0:T(8,128)(2,1)} %bitcast.3, bf16[512,128]{1,0:T(8,128)(2,1)S(1)} %convert_element_type.39, f32[16384]{0:T(1024)S(1)} %convert_bitcast_fusion), kind=kOutput, calls=%fused_computation | convolution fusion | flops 2189426688 | bytes 21168128 | tf_op jit(solution)/shard_map/uk,rk->ur/dot_general | solution.py:228
  151.6 0.0 copy-start
  151.6 6.9 %convolution_convert_fusion = bf16[16384,128]{1,0:T(8,128)(2,1)} fusion(bf16[16384,512]{1,0:T(8,128)(2,1)S(1)} %multiply_convert_fusion, bf16[512,128]{1,0:T(8,128)(2,1)S(1)} %convert_element_type.39), kind=kOutput, calls=%fused_computation.1 | convolution fusion | flops 2149580800 | bytes 21102592 | tf_op jit(solution)/shard_map/ur,uk->rk/dot_general | solution.py:233
  158.5 0.2 copy-done
  158.7 9.1 %all-to-all-start.2 = ((bf16[128,128,128]{2,1,0:T(8,128)(2,1)}), bf16[128,128,128]{2,1,0:T(8,128)(2,1)}, u32[]{:S(2)}, u32[]{:S(2)}) async-start(bf16[128,128,128]{2,1,0:T(8,128)(2,1)} %bitcast.15), calls=%async_computation.2 | async-start | bytes 8388608 | tf_op jit(solution)/shard_map/all_to_all | solution.py:237
  167.9 0.0 reduce-scatter.5.cloned.1.call-start
  167.9 34.4 %shard_map.138 = (f32[4096,128]{1,0:T(8,128)}, f32[4096,128]{1,0:T(8,128)}) custom-call(bf16[4096,128]{1,0:T(8,128)(2,1)} %slice.12.u_ref, bf16[4096,128]{1,0:T(8,128)(2,1)} %all-gather.5.cloned.1.call-done.h_ref, s32[512,128]{1,0:T(8,128)} %reshape.56.ph_ref, s32[512,128]{1,0:T(8,128)} %reshape.57.pl_ref, ...), custom_call_target="tpu_custom_call", output_to_operand_aliasing={{0}: (5, {}), {1}: (6, {})} | custom-call | tf_op jit(solution)/shard_map/pallas_call | solution.py:101
  202.3 18.0 %all-to-all-done.2 = bf16[128,128,128]{2,1,0:T(8,128)(2,1)} async-done(((bf16[128,128,128]{2,1,0:T(8,128)(2,1)}), bf16[128,128,128]{2,1,0:T(8,128)(2,1)}, u32[]{:S(2)}, u32[]{:S(2)}) %all-to-all-start.2) | async-done | bytes 4194336 | tf_op jit(solution)/shard_map/all_to_all | solution.py:237
  220.3 0.0 reduce-scatter.5.cloned.1.call-update
  220.3 0.0 reduce-scatter.3.cloned.1.call-start
  220.3 0.5 reduce-scatter.3.cloned.1.call-update
  220.9 0.0 all-reduce.2.cloned.1.call-start
  220.9 0.0 copy-start.5
  220.9 22.4 %shard_map.139 = f32[1024,128]{1,0:T(8,128)} custom-call(s32[1,16384]{1,0:T(1,128)} %bitcast.19, bf16[16384,128]{1,0:T(8,128)(2,1)} %bitcast.7.val_ref), custom_call_target="tpu_custom_call" | custom-call | tf_op jit(solution)/shard_map/pallas_call | solution.py:160
  243.3 0.0 copy-done.5
  243.3 0.0 copy-start.7
  243.3 0.0 copy-start.9
  243.3 2.2 multiply_subtract_fusion
  245.5 0.0 reduce-scatter.5.cloned.1.call-done
  245.5 0.0 all-reduce.2.cloned.1.call-update
  245.5 0.0 copy-start.6
  245.5 35.7 %reduce-scatter.3.cloned.1.call-done = f32[512,128]{1,0:T(8,128)} async-done(((f32[4096,128]{1,0:T(8,128)}), f32[512,128]{1,0:T(8,128)}) %reduce-scatter.3.cloned.1.call-update) | async-done | bytes 262160 | tf_op jit(solution)/shard_map/reduce_scatter | solution.py:242
  281.3 0.0 copy-done.7
  281.3 0.0 copy-done.9
  281.3 12.4 %multiply_subtract_fusion.2 = (f32[512,128]{1,0:T(8,128)}, f32[512,128]{1,0:T(8,128)}) fusion(f32[512,128]{1,0:T(8,128)S(1)} %copy-done.7, f32[512,128]{1,0:T(8,128)S(1)} %copy-done.9, f32[512,128]{1,0:T(8,128)} %reduce-scatter.3.cloned.1.call-done, bf16[16384,512]{1,0:T(8,128)(2,1)} %copy-done, bf16[16384,128]{1,0:T(8,128)(2,1)} %bitcast.3), kind=kOutput, calls=%fused_computation.49 | convolution fusion | flops 2147876864 | bytes 22282240 | tf_op jit(solution)/shard_map/dot_general | solution.py:232
  293.7 32.0 %all-reduce.2.cloned.1.call-done = f32[1024,128]{1,0:T(8,128)} async-done(((f32[1024,128]{1,0:T(8,128)}), f32[1024,128]{1,0:T(8,128)}) %all-reduce.2.cloned.1.call-update) | async-done | bytes 524304 | tf_op jit(solution)/shard_map/psum | solution.py:244
  325.7 0.0 copy-done.6
  325.7 2.1 multiply_subtract_fusion.1
Async XLA Ops:
  7.2 14.3 %copy-start.2 = (f32[1024,128]{1,0:T(8,128)S(1)}, f32[1024,128]{1,0:T(8,128)}, u32[]{:S(2)}) copy-start(f32[1024,128]{1,0:T(8,128)} %param.14) | copy-start | bytes 1572868
  7.2 45.2 %all-gather.3.cloned.1.call-start = ((), (), s32[]{:S(2)}) async-start(), calls=%async_computation.5 | async-start | bytes 2359296 | tf_op jit(solution)/shard_map/all_gather | solution.py:206
  10.2 20.4 %all-to-all-start = ((s32[128,1,128]{2,1,0:T(1,128)}), s32[128,1,128]{2,1,0:T(1,128)S(1)}, u32[]{:S(2)}, u32[]{:S(2)}) async-start(s32[128,1,128]{2,1,0:T(1,128)} %bitcast), calls=%async_computation | async-start | bytes 131072 | tf_op jit(solution)/shard_map/all_to_all | solution.py:200
  30.7 0.6 copy-start.4
  45.5 6.0 %copy-start.3 = (f32[1024,128]{1,0:T(8,128)S(1)}, f32[1024,128]{1,0:T(8,128)}, u32[]{:S(2)}) copy-start(f32[1024,128]{1,0:T(8,128)} %param.12) | copy-start | bytes 1572868
  45.5 6.8 %copy-start.8 = (s32[1,128]{1,0:T(1,128)S(1)}, s32[1,128]{1,0:T(1,128)}, u32[]{:S(2)}) copy-start(s32[1,128]{1,0:T(1,128)} %param.17) | copy-start | bytes 1540
  45.5 95.3 %all-to-all-start.1 = ((bf16[128,128,128]{2,1,0:T(8,128)(2,1)}), bf16[128,128,128]{2,1,0:T(8,128)(2,1)}, u32[]{:S(2)}, u32[]{:S(2)}) async-start(bf16[128,128,128]{2,1,0:T(8,128)(2,1)} %bitcast.17), calls=%async_computation.1 | async-start | bytes 8388608 | tf_op jit(solution)/shard_map/all_to_all | solution.py:208
  51.4 55.9 %all-gather.5.cloned.1.call-start = ((), (), s32[]{:S(2)}) async-start(), calls=%async_computation.6 | async-start | bytes 1310720 | tf_op jit(solution)/shard_map/all_gather | solution.py:207
  65.3 2.9 copy-start.1
  151.6 7.1 %copy-start = (bf16[16384,512]{1,0:T(8,128)(2,1)}, bf16[16384,512]{1,0:T(8,128)(2,1)S(1)}, u32[]{:S(2)}) copy-start(bf16[16384,512]{1,0:T(8,128)(2,1)S(1)} %multiply_convert_fusion) | copy-start | bytes 50331652
  158.7 61.5 %all-to-all-start.2 = ((bf16[128,128,128]{2,1,0:T(8,128)(2,1)}), bf16[128,128,128]{2,1,0:T(8,128)(2,1)}, u32[]{:S(2)}, u32[]{:S(2)}) async-start(bf16[128,128,128]{2,1,0:T(8,128)(2,1)} %bitcast.15), calls=%async_computation.2 | async-start | bytes 8388608 | tf_op jit(solution)/shard_map/all_to_all | solution.py:237
  167.9 77.6 %reduce-scatter.5.cloned.1.call-start = ((), (), s32[]{:S(2)}) async-start(), calls=%async_computation.8 | async-start | bytes 2621440 | tf_op jit(solution)/shard_map/reduce_scatter | solution.py:243
  220.3 61.0 %reduce-scatter.3.cloned.1.call-start = ((), (), s32[]{:S(2)}) async-start(), calls=%async_computation.7 | async-start | bytes 2359296 | tf_op jit(solution)/shard_map/reduce_scatter | solution.py:242
  220.9 104.8 %all-reduce.2.cloned.1.call-start = ((), (), s32[]{:S(2)}) async-start(), calls=%async_computation.9 | async-start | bytes 1048576 | tf_op jit(solution)/shard_map/psum | solution.py:244
  220.9 22.4 %copy-start.5 = (f32[1024,128]{1,0:T(8,128)S(1)}, f32[1024,128]{1,0:T(8,128)}, u32[]{:S(2)}) copy-start(f32[1024,128]{1,0:T(8,128)} %param.15) | copy-start | bytes 1572868
  243.3 37.9 %copy-start.7 = (f32[512,128]{1,0:T(8,128)S(1)}, f32[512,128]{1,0:T(8,128)}, u32[]{:S(2)}) copy-start(f32[512,128]{1,0:T(8,128)} %param.9) | copy-start | bytes 786436
  243.3 37.9 %copy-start.9 = (f32[512,128]{1,0:T(8,128)S(1)}, f32[512,128]{1,0:T(8,128)}, u32[]{:S(2)}) copy-start(f32[512,128]{1,0:T(8,128)} %param.10) | copy-start | bytes 786436
  245.5 80.2 %copy-start.6 = (f32[1024,128]{1,0:T(8,128)S(1)}, f32[1024,128]{1,0:T(8,128)}, u32[]{:S(2)}) copy-start(f32[1024,128]{1,0:T(8,128)} %param.13) | copy-start | bytes 1572868
Sparse Core Ops, SparseCore 0:
  10.4 27.7 all-gather.2
  54.5 52.7 all-gather.4
  220.4 24.9 reduce-scatter.4
  247.7 33.4 reduce-scatter.2
  283.4 42.1 all-reduce.1

commit v5 on v4

--- a/solution.py
+++ b/solution.py
@@ -205,6 +205,7 @@
     )
     packed_part = lax.all_gather(packed, "sb", axis=0, tiled=True)
     hot_part = lax.all_gather(hot_half, "sa", axis=0, tiled=True)
+    found, packed_part, hot_part = lax.optimization_barrier((found, packed_part, hot_part))
     fetched = lax.all_to_all(
         found.reshape(devices, slot_count, feature_count),
         ("grp", "sa", "sb"),
@@ -221,9 +222,12 @@
     local = jnp.where(owner % sb_count == lax.axis_index("sb"), local_hi * LANES + pos_lo, hot_part.shape[0])
     pos_hi_t, pos_lo_t = hot_prepare(local)
     tiles = users_part.shape[0] // 512
-    half = tiles // 2
-    part_a = hot_terms(users_part, pos_hi_t, pos_lo_t, hot_part, 0, half, found)
-    fetched, part_a = lax.optimization_barrier((fetched, part_a))
+    user_hot_part, item_part = hot_terms(users_part, pos_hi_t, pos_lo_t, hot_part, 0, tiles, found)
+    fetched, user_hot_part, item_part = lax.optimization_barrier((fetched, user_hot_part, item_part))
+    item_grad = lax.psum_scatter(item_part, "sa", scatter_dimension=0, tiled=True)
+    hot_grad = lax.psum(item_grad, "grp")
+    user_hot_part, hot_grad = lax.optimization_barrier((user_hot_part, hot_grad))
+    user_hot = lax.psum_scatter(user_hot_part, "sb", scatter_dimension=0, tiled=True)
     flat_rows = fetched.reshape(devices * slot_count, feature_count)
     scores = jnp.einsum("uk,rk->ur", user_half, flat_rows, preferred_element_type=jnp.float32)
     weights = (jax.nn.sigmoid(scores) * live_slots.reshape(1, -1).astype(jnp.float32)).astype(
@@ -235,13 +239,7 @@
     ).astype(jnp.bfloat16)
     row_terms = row_terms.reshape(devices, slot_count, feature_count)
     returned = lax.all_to_all(row_terms, ("grp", "sa", "sb"), split_axis=0, concat_axis=0, tiled=True)
-    user_hot_part, item_part = hot_terms(
-        users_part, pos_hi_t, pos_lo_t, hot_part, half, tiles - half, row_terms, prev=part_a
-    )
-    returned, user_hot_part, item_part = lax.optimization_barrier((returned, user_hot_part, item_part))
-    user_hot = lax.psum_scatter(user_hot_part, "sb", scatter_dimension=0, tiled=True)
-    item_grad = lax.psum_scatter(item_part, "sa", scatter_dimension=0, tiled=True)
-    hot_grad = lax.psum(item_grad, "grp")
+    returned, user_cold = lax.optimization_barrier((returned, user_cold))
     cold_grad = onehot_scatter_add(
         asked_rows.reshape(-1),
         returned.reshape(devices * slot_count, feature_count),

time: 335 us -> 309 us (0.922)
  waiting for transfers between devices: 133 us -> 101 us
  matrix products: 30.2 us -> 35.5 us
  starting transfers between devices: 26.5 us -> 29.9 us
    all_gather x1, waiting for transfers between devices: 38 us -> 0.01 us  [body(): hot_part = lax.all_gather(hot_half, 'sa', axis=0, tiled=True)]
    reduce_scatter x1, waiting for transfers between devices: 35.7 us -> 5.9 us  [body(): lax.psum_scatter(user_hot_part, 'sb', scatter_dimension=0, tiled=True)]
    psum x1, waiting for transfers between devices: 32 us -> 51.7 us  [body(): hot_grad = lax.psum(item_grad, 'grp')]
    all_gather x1, waiting for transfers between devices: 0.02 us -> 18 us  [body(): packed_part = lax.all_gather(packed, 'sb', axis=0, tiled=True)]
    all_to_all x1, waiting for transfers between devices: 18 us -> 0.01 us  [body(): lax.all_to_all(row_terms, ('grp', 'sa', 'sb'), split_axis=0, concat_axis=...]
    reduce_scatter x1, waiting for transfers between devices: 0.01 us -> 17.3 us  [body(): lax.psum_scatter(item_part, 'sa', scatter_dimension=0, tiled=True)]
    dot_general x1, matrix products: 6.86 us -> 12.3 us  [body(): jnp.einsum('ur,uk->rk', weights, user_half, preferred_element_type=jnp.fl...]
    pallas_call x2 -> x1, Pallas kernels: 67.8 us -> 64.1 us  [hot_terms(): pl.pallas_call(functools.partial(_hot_kernel, sub_users=sub_users, chaine...]
  transfers between devices with their start and end apart: 8 -> 8, of which waited for: 5 -> 5; matrix products, arithmetic and copies ran while one was open for 10% -> 19% of each run, Pallas kernels for 31% -> 33%
where the time goes in v5:
time: 309 us; the launch traced here: 308 us
  waiting for transfers between devices  101 us (33%)
  Pallas kernels  101 us (33%)
  matrix products  35.5 us (11%)
  starting transfers between devices  29.9 us (10%)
  other arithmetic  17.9 us (6%)
  between operations  14 us (5%)
  local copies, waits for them, and re-layouts  8.95 us (3%)
    pallas_call x1, Pallas kernels, hot_terms(): pl.pallas_call(functools.partial(_hot_kernel, sub_users=sub_users, chaine...  64.1 us
    psum x1, waiting for transfers between devices, body(): hot_grad = lax.psum(item_grad, 'grp')  51.7 us
    pallas_call x1, Pallas kernels, onehot_scatter_add(): pl.pallas_call(_scatter_kernel, grid=(n // chunk,), in_specs=[pl.BlockSpe...  22.3 us
    all_gather x1, waiting for transfers between devices, body(): packed_part = lax.all_gather(packed, 'sb', axis=0, tiled=True)  18 us
    reduce_scatter x1, waiting for transfers between devices, body(): lax.psum_scatter(item_part, 'sa', scatter_dimension=0, tiled=True)  17.3 us
    pallas_call x1, Pallas kernels, onehot_gather(): pl.pallas_call(_gather_kernel, grid=(n // chunk,), in_specs=[pl.BlockSpec...  14.2 us
    dot_general x1, matrix products, body(): jnp.einsum('uk,rk->ur', user_half, flat_rows, preferred_element_type=jnp....  13.5 us
    dot_general x1, matrix products, body(): jnp.einsum('ur,uk->rk', weights, user_half, preferred_element_type=jnp.fl...  12.3 us
  transfers between devices with their start and end apart: 8, of which 5 were waited for; matrix products, arithmetic and copies ran while one was open for 19% of the time, Pallas kernels for 33%

profile of v5, /device:TPU:0, one launch (start us, length us, event | category | flops | bytes accessed | tf_op | source)
XLA Modules:
  0.0 308.3 jit_solution(12816589210418119360)
XLA Ops:
  7.2 0.0 copy-start.3
  7.2 0.0 all-gather.5.cloned.1.call-start
  7.2 1.8 convert_element_type.42
  9.0 0.0 all-gather.5.cloned.1.call-update
  9.1 0.0 all-gather.3.cloned.1.call-start
  9.1 1.0 convert_element_type.39
  10.1 0.9 copy.23
  11.0 0.3 fusion.14
  11.2 0.8 pad_maximum_fusion
  12.1 0.0 all-gather.3.cloned.1.call-update
  12.1 11.2 %all-to-all-start = ((s32[128,1,128]{2,1,0:T(1,128)}), s32[128,1,128]{2,1,0:T(1,128)S(1)}, u32[]{:S(2)}, u32[]{:S(2)}) async-start(s32[128,1,128]{2,1,0:T(1,128)} %bitcast), calls=%async_computation | async-start | bytes 131072 | tf_op jit(solution)/shard_map/all_to_all | solution.py:200
  23.3 0.0 copy-done.3
  23.3 0.7 convert_element_type.38.table_ref
  24.0 8.5 %all-to-all-done = s32[128,1,128]{2,1,0:T(1,128)S(1)} async-done(((s32[128,1,128]{2,1,0:T(1,128)}), s32[128,1,128]{2,1,0:T(1,128)S(1)}, u32[]{:S(2)}, u32[]{:S(2)}) %all-to-all-start) | async-done | bytes 65568 | tf_op jit(solution)/shard_map/all_to_all | solution.py:200
  32.5 0.0 copy-start.5
  32.5 0.6 copy-done.5
  33.2 14.2 %shard_map.136.dep_ref = bf16[16384,128]{1,0:T(8,128)(2,1)} custom-call(s32[1,16384]{1,0:T(1,128)} %bitcast.17, bf16[1024,128]{1,0:T(8,128)(2,1)} %convert_element_type.38.table_ref), custom_call_target="tpu_custom_call" | custom-call | tf_op jit(solution)/shard_map/pallas_call | solution.py:131
  47.3 0.0 all-gather.5.cloned.1.call-done.h_ref
  47.3 18.0 %all-gather.3.cloned.1.call-done = bf16[4096,160]{1,0:T(8,128)(2,1)} async-done(((bf16[512,160]{1,0:T(8,128)(2,1)}), bf16[4096,160]{1,0:T(8,128)(2,1)}) %all-gather.3.cloned.1.call-update) | async-done | bytes 1310736 | tf_op jit(solution)/shard_map/all_gather | solution.py:206
  65.3 0.0 copy-start.10
  65.3 0.0 copy-start
  65.3 9.6 %all-to-all-start.1 = ((bf16[128,128,128]{2,1,0:T(8,128)(2,1)}), bf16[128,128,128]{2,1,0:T(8,128)(2,1)}, u32[]{:S(2)}, u32[]{:S(2)}) async-start(bf16[128,128,128]{2,1,0:T(8,128)(2,1)} %bitcast.15), calls=%async_computation.1 | async-start | bytes 8388608 | tf_op jit(solution)/shard_map/all_to_all | solution.py:209
  75.0 0.0 reduce-scatter.3.cloned.1.call-start
  75.0 0.0 copy-start.1
  75.0 0.0 copy-done.10
  75.0 0.1 convert_bitcast_fusion
  75.1 0.0 copy-done
  75.1 1.2 slice.9.u_ref
  76.3 0.7 copy-done.1
  77.0 6.4 %add_select_fusion = (s32[4096,16]{1,0:T(8,128)}, s32[4096,16]{1,0:T(8,128)S(1)}) fusion(bf16[4096,160]{1,0:T(8,128)(2,1)S(1)} %copy-done.1, s32[]{:T(128)S(6)} %axis_index.12), kind=kLoop, calls=%fused_computation.6 | loop fusion | flops 3735552 | bytes 786436 | tf_op jit(solution)/shard_map/jit(remainder)/select_n | solution.py:79
  83.4 2.8 reshape.57.pl_ref
  86.2 2.5 add_select_fusion.1
  88.7 2.8 reshape.56.ph_ref
  91.4 64.1 %shard_map.137 = (f32[4096,128]{1,0:T(8,128)}, f32[4096,128]{1,0:T(8,128)}) custom-call(bf16[4096,128]{1,0:T(8,128)(2,1)} %slice.9.u_ref, bf16[4096,128]{1,0:T(8,128)(2,1)} %all-gather.5.cloned.1.call-done.h_ref, s32[512,128]{1,0:T(8,128)} %reshape.56.ph_ref, s32[512,128]{1,0:T(8,128)} %reshape.57.pl_ref, bf16[16384,128]{1,0:T(8,128)(2,1)} %shard_map.136.dep_ref), custom_call_target="tpu_custom_call" | custom-call | tf_op jit(solution)/shard_map/pallas_call | solution.py:101
  155.5 0.0 all-to-all-done.1
  155.5 0.0 reduce-scatter.3.cloned.1.call-update
  155.6 0.0 all-reduce.2.cloned.1.call-start
  155.6 13.5 %multiply_convert_fusion = bf16[16384,512]{1,0:T(8,128)(2,1)} fusion(bf16[16384,128]{1,0:T(8,128)(2,1)} %bitcast.3, bf16[512,128]{1,0:T(8,128)(2,1)S(1)} %convert_element_type.39, f32[16384]{0:T(1024)S(1)} %convert_bitcast_fusion), kind=kOutput, calls=%fused_computation | convolution fusion | flops 2189426688 | bytes 21168128 | tf_op jit(solution)/shard_map/uk,rk->ur/dot_general | solution.py:232
  169.2 17.3 %reduce-scatter.3.cloned.1.call-done = f32[1024,128]{1,0:T(8,128)} async-done(((f32[4096,128]{1,0:T(8,128)}), f32[1024,128]{1,0:T(8,128)}) %reduce-scatter.3.cloned.1.call-update) | async-done | bytes 524304 | tf_op jit(solution)/shard_map/reduce_scatter | solution.py:227
  186.5 0.0 all-reduce.2.cloned.1.call-update
  186.5 12.3 %convolution_convert_fusion = bf16[16384,128]{1,0:T(8,128)(2,1)} fusion(bf16[16384,512]{1,0:T(8,128)(2,1)} %multiply_convert_fusion, bf16[512,128]{1,0:T(8,128)(2,1)S(1)} %convert_element_type.39), kind=kOutput, calls=%fused_computation.1 | convolution fusion | flops 2149580800 | bytes 21102592 | tf_op jit(solution)/shard_map/ur,uk->rk/dot_general | solution.py:237
  198.8 8.9 %all-to-all-start.2 = ((bf16[128,128,128]{2,1,0:T(8,128)(2,1)}), bf16[128,128,128]{2,1,0:T(8,128)(2,1)}, u32[]{:S(2)}, u32[]{:S(2)}) async-start(bf16[128,128,128]{2,1,0:T(8,128)(2,1)} %bitcast.16), calls=%async_computation.4 | async-start | bytes 8388608 | tf_op jit(solution)/shard_map/all_to_all | solution.py:241
  207.7 0.0 reduce-scatter.5.cloned.1.call-start
  207.8 51.7 %all-reduce.2.cloned.1.call-done = f32[1024,128]{1,0:T(8,128)} async-done(((f32[1024,128]{1,0:T(8,128)}), f32[1024,128]{1,0:T(8,128)}) %all-reduce.2.cloned.1.call-update) | async-done | bytes 524304 | tf_op jit(solution)/shard_map/psum | solution.py:228
  259.4 0.0 reduce-scatter.5.cloned.1.call-update
  259.5 9.7 %fusion.19 = f32[512,128]{1,0:T(8,128)S(1)} fusion(bf16[16384,512]{1,0:T(8,128)(2,1)} %multiply_convert_fusion, bf16[16384,128]{1,0:T(8,128)(2,1)} %bitcast.3), kind=kOutput, calls=%fused_computation.55 | convolution fusion | flops 2147483648 | bytes 21233664 | tf_op jit(solution)/shard_map/dot_general | solution.py:236
  269.1 0.0 all-to-all-done.2
  269.1 0.0 copy-start.2
  269.2 0.0 copy-start.6
  269.2 0.0 copy-start.7
  269.2 0.0 copy-start.8
  269.2 22.3 %shard_map.138 = f32[1024,128]{1,0:T(8,128)} custom-call(s32[1,16384]{1,0:T(1,128)} %bitcast.18, bf16[16384,128]{1,0:T(8,128)(2,1)} %bitcast.7.val_ref), custom_call_target="tpu_custom_call" | custom-call | tf_op jit(solution)/shard_map/pallas_call | solution.py:160
  291.5 0.0 copy-done.2
  291.5 0.0 copy-done.6
  291.5 0.0 copy-done.7
  291.5 0.0 copy-done.8
  291.5 0.0 copy-start.4
  291.5 0.0 copy-start.9
  291.5 2.5 multiply_subtract_fusion
  294.0 5.9 %reduce-scatter.5.cloned.1.call-done = f32[512,128]{1,0:T(8,128)} async-done(((f32[4096,128]{1,0:T(8,128)}), f32[512,128]{1,0:T(8,128)}) %reduce-scatter.5.cloned.1.call-update) | async-done | bytes 262160 | tf_op jit(solution)/shard_map/reduce_scatter | solution.py:230
  299.9 0.0 copy-done.4
  299.9 0.0 copy-done.9
  299.9 1.8 multiply_subtract_fusion.2
Async XLA Ops:
  7.2 16.1 %copy-start.3 = (f32[1024,128]{1,0:T(8,128)S(1)}, f32[1024,128]{1,0:T(8,128)}, u32[]{:S(2)}) copy-start(f32[1024,128]{1,0:T(8,128)} %param.14) | copy-start | bytes 1572868
  7.2 40.1 %all-gather.5.cloned.1.call-start = ((), (), s32[]{:S(2)}) async-start(), calls=%async_computation.6 | async-start | bytes 1310720 | tf_op jit(solution)/shard_map/all_gather | solution.py:207
  9.1 56.3 %all-gather.3.cloned.1.call-start = ((), (), s32[]{:S(2)}) async-start(), calls=%async_computation.5 | async-start | bytes 2359296 | tf_op jit(solution)/shard_map/all_gather | solution.py:206
  12.1 20.4 %all-to-all-start = ((s32[128,1,128]{2,1,0:T(1,128)}), s32[128,1,128]{2,1,0:T(1,128)S(1)}, u32[]{:S(2)}, u32[]{:S(2)}) async-start(s32[128,1,128]{2,1,0:T(1,128)} %bitcast), calls=%async_computation | async-start | bytes 131072 | tf_op jit(solution)/shard_map/all_to_all | solution.py:200
  32.5 0.6 copy-start.5
  65.3 9.7 %copy-start.10 = (s32[1,128]{1,0:T(1,128)S(1)}, s32[1,128]{1,0:T(1,128)}, u32[]{:S(2)}) copy-start(s32[1,128]{1,0:T(1,128)} %param.17) | copy-start | bytes 1540
  65.3 9.8 %copy-start = (bf16[4096,160]{1,0:T(8,128)(2,1)S(1)}, bf16[4096,160]{1,0:T(8,128)(2,1)}, u32[]{:S(2)}) copy-start(bf16[4096,160]{1,0:T(8,128)(2,1)} %all-gather.3.cloned.1.call-done) | copy-start | bytes 3932164
  65.3 90.2 %all-to-all-start.1 = ((bf16[128,128,128]{2,1,0:T(8,128)(2,1)}), bf16[128,128,128]{2,1,0:T(8,128)(2,1)}, u32[]{:S(2)}, u32[]{:S(2)}) async-start(bf16[128,128,128]{2,1,0:T(8,128)(2,1)} %bitcast.15), calls=%async_computation.1 | async-start | bytes 8388608 | tf_op jit(solution)/shard_map/all_to_all | solution.py:209
  75.0 111.5 %reduce-scatter.3.cloned.1.call-start = ((), (), s32[]{:S(2)}) async-start(), calls=%async_computation.7 | async-start | bytes 2621440 | tf_op jit(solution)/shard_map/reduce_scatter | solution.py:227
  75.0 2.0 copy-start.1
  155.6 103.9 %all-reduce.2.cloned.1.call-start = ((), (), s32[]{:S(2)}) async-start(), calls=%async_computation.8 | async-start | bytes 1048576 | tf_op jit(solution)/shard_map/psum | solution.py:228
  198.8 70.4 %all-to-all-start.2 = ((bf16[128,128,128]{2,1,0:T(8,128)(2,1)}), bf16[128,128,128]{2,1,0:T(8,128)(2,1)}, u32[]{:S(2)}, u32[]{:S(2)}) async-start(bf16[128,128,128]{2,1,0:T(8,128)(2,1)} %bitcast.16), calls=%async_computation.4 | async-start | bytes 8388608 | tf_op jit(solution)/shard_map/all_to_all | solution.py:241
  207.7 92.2 %reduce-scatter.5.cloned.1.call-start = ((), (), s32[]{:S(2)}) async-start(), calls=%async_computation.9 | async-start | bytes 2359296 | tf_op jit(solution)/shard_map/reduce_scatter | solution.py:230
  269.1 22.3 %copy-start.2 = (f32[1024,128]{1,0:T(8,128)S(1)}, f32[1024,128]{1,0:T(8,128)}, u32[]{:S(2)}) copy-start(f32[1024,128]{1,0:T(8,128)} %param.12) | copy-start | bytes 1572868
  269.2 22.3 %copy-start.6 = (f32[1024,128]{1,0:T(8,128)S(1)}, f32[1024,128]{1,0:T(8,128)}, u32[]{:S(2)}) copy-start(f32[1024,128]{1,0:T(8,128)} %param.15) | copy-start | bytes 1572868
  269.2 22.3 %copy-start.7 = (f32[1024,128]{1,0:T(8,128)S(1)}, f32[1024,128]{1,0:T(8,128)}, u32[]{:S(2)}) copy-start(f32[1024,128]{1,0:T(8,128)} %param.13) | copy-start | bytes 1572868
  269.2 22.3 %copy-start.8 = (f32[1024,128]{1,0:T(8,128)S(1)}, f32[1024,128]{1,0:T(8,128)}, u32[]{:S(2)}) copy-start(f32[1024,128]{1,0:T(8,128)} %all-reduce.2.cloned.1.call-done) | copy-start | bytes 1572868
  291.5 8.4 %copy-start.4 = (f32[512,128]{1,0:T(8,128)S(1)}, f32[512,128]{1,0:T(8,128)}, u32[]{:S(2)}) copy-start(f32[512,128]{1,0:T(8,128)} %param.9) | copy-start | bytes 786436
  291.5 8.4 %copy-start.9 = (f32[512,128]{1,0:T(8,128)S(1)}, f32[512,128]{1,0:T(8,128)}, u32[]{:S(2)}) copy-start(f32[512,128]{1,0:T(8,128)} %param.10) | copy-start | bytes 786436
Sparse Core Ops, SparseCore 0:
  10.2 26.9 all-gather.4
  39.5 25.7 all-gather.2
  155.7 30.7 reduce-scatter.2
  188.7 70.7 all-reduce.1
  261.7 38.2 reduce-scatter.4

commit v6 on v5

--- a/solution.py
+++ b/solution.py
@@ -138,6 +138,44 @@
         out_specs=pl.BlockSpec((chunk, k), lambda i: (i, 0)),
         out_shape=jax.ShapeDtypeStruct((n, k), table.dtype),
     )(idx.reshape(1, n), table)
+
+
+def _cold_kernel(u_ref, r_ref, live_ref, uc_ref, t_ref):
+    j = pl.program_id(0)
+    u = u_ref[...]
+    rows = r_ref[...]
+    scores = _nt(u, rows)
+    w = (jax.nn.sigmoid(scores) * live_ref[...]).astype(jnp.bfloat16)
+
+    @pl.when(j == 0)
+    def _():
+        uc_ref[...] = jnp.zeros_like(uc_ref)
+
+    uc_ref[...] += jnp.dot(w, rows, preferred_element_type=jnp.float32)
+    t_ref[...] = _tn(w, u).astype(t_ref.dtype)
+
+
+def cold_terms(user_half, flat_rows, live, chunk=2048):
+    users, k = user_half.shape
+    n = flat_rows.shape[0]
+    return pl.pallas_call(
+        _cold_kernel,
+        grid=(n // chunk,),
+        in_specs=[
+            pl.BlockSpec((users, k), lambda j: (0, 0)),
+            pl.BlockSpec((chunk, k), lambda j: (j, 0)),
+            pl.BlockSpec((1, chunk), lambda j: (0, j)),
+        ],
+        out_specs=[
+            pl.BlockSpec((users, k), lambda j: (0, 0)),
+            pl.BlockSpec((chunk, k), lambda j: (j, 0)),
+        ],
+        out_shape=[
+            jax.ShapeDtypeStruct((users, k), jnp.float32),
+            jax.ShapeDtypeStruct((n, k), jnp.bfloat16),
+        ],
+        compiler_params=pltpu.CompilerParams(dimension_semantics=("arbitrary",)),
+    )(user_half, flat_rows, live.reshape(1, n))
 
 
 def _scatter_kernel(idx_ref, val_ref, out_ref):
@@ -226,20 +264,12 @@
     fetched, user_hot_part, item_part = lax.optimization_barrier((fetched, user_hot_part, item_part))
     item_grad = lax.psum_scatter(item_part, "sa", scatter_dimension=0, tiled=True)
     hot_grad = lax.psum(item_grad, "grp")
-    user_hot_part, hot_grad = lax.optimization_barrier((user_hot_part, hot_grad))
     user_hot = lax.psum_scatter(user_hot_part, "sb", scatter_dimension=0, tiled=True)
     flat_rows = fetched.reshape(devices * slot_count, feature_count)
-    scores = jnp.einsum("uk,rk->ur", user_half, flat_rows, preferred_element_type=jnp.float32)
-    weights = (jax.nn.sigmoid(scores) * live_slots.reshape(1, -1).astype(jnp.float32)).astype(
-        jnp.bfloat16
-    )
-    user_cold = jnp.dot(weights, flat_rows, preferred_element_type=jnp.float32)
-    row_terms = jnp.einsum(
-        "ur,uk->rk", weights, user_half, preferred_element_type=jnp.float32
-    ).astype(jnp.bfloat16)
+    user_cold, row_terms = cold_terms(user_half, flat_rows, live_slots.reshape(-1).astype(jnp.float32))
     row_terms = row_terms.reshape(devices, slot_count, feature_count)
     returned = lax.all_to_all(row_terms, ("grp", "sa", "sb"), split_axis=0, concat_axis=0, tiled=True)
-    returned, user_cold = lax.optimization_barrier((returned, user_cold))
+    returned, user_cold, hot_grad = lax.optimization_barrier((returned, user_cold, hot_grad))
     cold_grad = onehot_scatter_add(
         asked_rows.reshape(-1),
         returned.reshape(devices * slot_count, feature_count),

time: 309 us -> 313 us (1.013)
  matrix products: 35.5 us -> 0 us
  waiting for transfers between devices: 101 us -> 124 us
  Pallas kernels: 101 us -> 118 us
    all_to_all x1, waiting for transfers between devices: 0.01 us -> 51.8 us  [body(): lax.all_to_all(row_terms, ('grp', 'sa', 'sb'), split_axis=0, concat_axis=...]
    psum x1, waiting for transfers between devices: 51.7 us -> 0.01 us  [body(): hot_grad = lax.psum(item_grad, 'grp')]
    dot_general x3 -> x0, matrix products: 35.5 us -> none  [the longest x1 13.5 us: body(): jnp.einsum('uk,rk->ur', user_half, flat_rows, preferred_element_type=jnp....]
    pallas_call x0 -> x1, Pallas kernels: none -> 18 us  [cold_terms(): pl.pallas_call(_cold_kernel, grid=(n // chunk,), in_specs=[pl.BlockSpec((...]
    reduce_scatter x1, waiting for transfers between devices: 17.3 us -> 30.6 us  [body(): lax.psum_scatter(item_part, 'sa', scatter_dimension=0, tiled=True)]
    reduce_scatter x1, waiting for transfers between devices: 5.9 us -> 14.6 us  [body(): lax.psum_scatter(user_hot_part, 'sb', scatter_dimension=0, tiled=True)]
  transfers between devices with their start and end apart: 8 -> 8, of which waited for: 5 -> 5; matrix products, arithmetic and copies ran while one was open for 19% -> 6% of each run, Pallas kernels for 33% -> 38%
where the time goes in v6:
time: 313 us; the launch traced here: 312 us
  waiting for transfers between devices  124 us (40%)
  Pallas kernels  118 us (38%)
  starting transfers between devices  30.3 us (10%)
  other arithmetic  17.5 us (6%)
  between operations  13.9 us (4%)
  local copies, waits for them, and re-layouts  7.55 us (2%)
    pallas_call x1, Pallas kernels, hot_terms(): pl.pallas_call(functools.partial(_hot_kernel, sub_users=sub_users, chaine...  64.1 us
    all_to_all x1, waiting for transfers between devices, body(): lax.all_to_all(row_terms, ('grp', 'sa', 'sb'), split_axis=0, concat_axis=...  51.8 us
    reduce_scatter x1, waiting for transfers between devices, body(): lax.psum_scatter(item_part, 'sa', scatter_dimension=0, tiled=True)  30.6 us
    pallas_call x1, Pallas kernels, onehot_scatter_add(): pl.pallas_call(_scatter_kernel, grid=(n // chunk,), in_specs=[pl.BlockSpe...  22.3 us
    all_gather x1, waiting for transfers between devices, body(): packed_part = lax.all_gather(packed, 'sb', axis=0, tiled=True)  18 us
    pallas_call x1, Pallas kernels, cold_terms(): pl.pallas_call(_cold_kernel, grid=(n // chunk,), in_specs=[pl.BlockSpec((...  18 us
    reduce_scatter x1, waiting for transfers between devices, body(): lax.psum_scatter(user_hot_part, 'sb', scatter_dimension=0, tiled=True)  14.6 us
    pallas_call x1, Pallas kernels, onehot_gather(): pl.pallas_call(_gather_kernel, grid=(n // chunk,), in_specs=[pl.BlockSpec...  14.2 us
  transfers between devices with their start and end apart: 8, of which 5 were waited for; matrix products, arithmetic and copies ran while one was open for 6% of the time, Pallas kernels for 38%

profile of v6, /device:TPU:0, one launch (start us, length us, event | category | flops | bytes accessed | tf_op | source)
XLA Modules:
  0.0 311.9 jit_solution(9555568172980858797)
XLA Ops:
  7.2 0.0 copy-start.3
  7.2 0.0 all-gather.5.cloned.1.call-start
  7.2 1.8 convert_element_type.38
  9.0 0.0 all-gather.5.cloned.1.call-update
  9.1 0.0 all-gather.3.cloned.1.call-start
  9.1 0.9 copy.23
  10.0 1.0 convert_element_type.35.u_ref
  11.0 0.0 copy-start.4
  11.0 0.3 fusion.14
  11.3 0.8 pad_maximum_fusion
  12.1 0.0 all-gather.3.cloned.1.call-update
  12.1 11.2 %all-to-all-start = ((s32[128,1,128]{2,1,0:T(1,128)}), s32[128,1,128]{2,1,0:T(1,128)S(1)}, u32[]{:S(2)}, u32[]{:S(2)}) async-start(s32[128,1,128]{2,1,0:T(1,128)} %bitcast), calls=%async_computation | async-start | bytes 131072 | tf_op jit(solution)/shard_map/all_to_all | solution.py:238
  23.3 0.0 copy-done.3
  23.3 0.7 convert_element_type.34.table_ref
  24.0 8.5 %all-to-all-done = s32[128,1,128]{2,1,0:T(1,128)S(1)} async-done(((s32[128,1,128]{2,1,0:T(1,128)}), s32[128,1,128]{2,1,0:T(1,128)S(1)}, u32[]{:S(2)}, u32[]{:S(2)}) %all-to-all-start) | async-done | bytes 65568 | tf_op jit(solution)/shard_map/all_to_all | solution.py:238
  32.5 0.0 copy-start.6
  32.5 0.6 copy-done.6
  33.2 14.2 %shard_map.136.dep_ref = bf16[16384,128]{1,0:T(8,128)(2,1)} custom-call(s32[1,16384]{1,0:T(1,128)} %bitcast.10, bf16[1024,128]{1,0:T(8,128)(2,1)} %convert_element_type.34.table_ref), custom_call_target="tpu_custom_call" | custom-call | tf_op jit(solution)/shard_map/pallas_call | solution.py:131
  47.3 0.0 copy-done.4
  47.3 0.0 all-gather.5.cloned.1.call-done.h_ref
  47.3 18.0 %all-gather.3.cloned.1.call-done = bf16[4096,160]{1,0:T(8,128)(2,1)} async-done(((bf16[512,160]{1,0:T(8,128)(2,1)}), bf16[4096,160]{1,0:T(8,128)(2,1)}) %all-gather.3.cloned.1.call-update) | async-done | bytes 1310736 | tf_op jit(solution)/shard_map/all_gather | solution.py:244
  65.3 0.0 copy-start
  65.3 9.6 %all-to-all-start.1 = ((bf16[128,128,128]{2,1,0:T(8,128)(2,1)}), bf16[128,128,128]{2,1,0:T(8,128)(2,1)}, u32[]{:S(2)}, u32[]{:S(2)}) async-start(bf16[128,128,128]{2,1,0:T(8,128)(2,1)} %bitcast.8), calls=%async_computation.1 | async-start | bytes 8388608 | tf_op jit(solution)/shard_map/all_to_all | solution.py:247
  75.0 0.2 reduce-scatter.5.cloned.1.call-start
  75.2 0.0 copy-done
  75.2 0.0 copy-start.1
  75.2 1.0 slice.9.u_ref
  76.3 0.9 copy-done.1
  77.2 5.3 %add_select_fusion = (s32[4096,16]{1,0:T(8,128)S(1)}, s32[4096,16]{1,0:T(8,128)S(1)}) fusion(bf16[4096,160]{1,0:T(8,128)(2,1)S(1)} %copy-done.1, s32[]{:T(128)S(6)} %axis_index.12), kind=kLoop, calls=%fused_computation.4 | loop fusion | flops 3735552 | bytes 786436 | tf_op jit(solution)/shard_map/jit(remainder)/select_n | solution.py:79
  82.5 2.5 add_select_fusion.1
  85.1 2.8 reshape.65.ph_ref
  87.8 1.3 reshape.66.pl_ref
  89.1 64.1 %shard_map.137 = (f32[4096,128]{1,0:T(8,128)}, f32[4096,128]{1,0:T(8,128)}) custom-call(bf16[4096,128]{1,0:T(8,128)(2,1)} %slice.9.u_ref, bf16[4096,128]{1,0:T(8,128)(2,1)} %all-gather.5.cloned.1.call-done.h_ref, s32[512,128]{1,0:T(8,128)} %reshape.65.ph_ref, s32[512,128]{1,0:T(8,128)} %reshape.66.pl_ref, bf16[16384,128]{1,0:T(8,128)(2,1)} %shard_map.136.dep_ref), custom_call_target="tpu_custom_call" | custom-call | tf_op jit(solution)/shard_map/pallas_call | solution.py:101
  153.2 0.0 copy-start.12
  153.2 0.0 all-to-all-done.1
  153.2 0.0 reduce-scatter.5.cloned.1.call-update
  153.2 0.3 all-reduce.2.cloned.1.call-start
  153.5 30.6 %reduce-scatter.5.cloned.1.call-done = f32[1024,128]{1,0:T(8,128)} async-done(((f32[4096,128]{1,0:T(8,128)}), f32[1024,128]{1,0:T(8,128)}) %reduce-scatter.5.cloned.1.call-update) | async-done | bytes 524304 | tf_op jit(solution)/shard_map/reduce_scatter | solution.py:265
  184.1 0.0 all-reduce.2.cloned.1.call-update
  184.1 0.0 copy-done.12
  184.1 0.7 fusion.18
  184.8 18.0 %shard_map.138 = (f32[512,128]{1,0:T(8,128)}, bf16[16384,128]{1,0:T(8,128)(2,1)}) custom-call(bf16[512,128]{1,0:T(8,128)(2,1)} %copy-done.4, bf16[16384,128]{1,0:T(8,128)(2,1)} %bitcast.3.r_ref, f32[1,16384]{1,0:T(1,128)} %bitcast.12), custom_call_target="tpu_custom_call" | custom-call | tf_op jit(solution)/shard_map/pallas_call | solution.py:161
  202.8 8.9 %all-to-all-start.2 = ((bf16[128,128,128]{2,1,0:T(8,128)(2,1)}), bf16[128,128,128]{2,1,0:T(8,128)(2,1)}, u32[]{:S(2)}, u32[]{:S(2)}) async-start(bf16[128,128,128]{2,1,0:T(8,128)(2,1)} %bitcast.9), calls=%async_computation.3 | async-start | bytes 8388608 | tf_op jit(solution)/shard_map/all_to_all | solution.py:271
  211.7 0.0 reduce-scatter.3.cloned.1.call-start
  211.8 0.5 reduce-scatter.3.cloned.1.call-update
  212.3 51.8 %all-to-all-done.2 = bf16[128,128,128]{2,1,0:T(8,128)(2,1)} async-done(((bf16[128,128,128]{2,1,0:T(8,128)(2,1)}), bf16[128,128,128]{2,1,0:T(8,128)(2,1)}, u32[]{:S(2)}, u32[]{:S(2)}) %all-to-all-start.2) | async-done | bytes 4194336 | tf_op jit(solution)/shard_map/all_to_all | solution.py:271
  264.1 0.0 all-reduce.2.cloned.1.call-done
  264.1 0.0 copy-start.2
  264.1 0.0 copy-start.7
  264.1 0.0 copy-start.9
  264.1 22.3 %shard_map.139 = f32[1024,128]{1,0:T(8,128)} custom-call(s32[1,16384]{1,0:T(1,128)} %bitcast.11, bf16[16384,128]{1,0:T(8,128)(2,1)} %bitcast.7.val_ref), custom_call_target="tpu_custom_call" | custom-call | tf_op jit(solution)/shard_map/pallas_call | solution.py:198
  286.4 0.0 copy-done.2
  286.4 0.0 copy-done.7
  286.4 0.0 copy-done.8
  286.4 0.0 copy-done.9
  286.4 0.0 copy-start.5
  286.4 0.0 copy-start.10
  286.5 0.0 copy-start.11
  286.5 2.5 multiply_subtract_fusion
  289.0 14.6 %reduce-scatter.3.cloned.1.call-done = f32[512,128]{1,0:T(8,128)} async-done(((f32[4096,128]{1,0:T(8,128)}), f32[512,128]{1,0:T(8,128)}) %reduce-scatter.3.cloned.1.call-update) | async-done | bytes 262160 | tf_op jit(solution)/shard_map/reduce_scatter | solution.py:267
  303.6 0.0 copy-done.5
  303.6 0.0 copy-done.10
  303.6 0.0 copy-done.11
  303.6 1.8 multiply_subtract_fusion.2
  (1 shorter events, 0.0 us)
Async XLA Ops:
  7.2 16.1 %copy-start.3 = (f32[1024,128]{1,0:T(8,128)S(1)}, f32[1024,128]{1,0:T(8,128)}, u32[]{:S(2)}) copy-start(f32[1024,128]{1,0:T(8,128)} %param.14) | copy-start | bytes 1572868
  7.2 40.2 %all-gather.5.cloned.1.call-start = ((), (), s32[]{:S(2)}) async-start(), calls=%async_computation.6 | async-start | bytes 1310720 | tf_op jit(solution)/shard_map/all_gather | solution.py:245
  9.1 56.3 %all-gather.3.cloned.1.call-start = ((), (), s32[]{:S(2)}) async-start(), calls=%async_computation.5 | async-start | bytes 2359296 | tf_op jit(solution)/shard_map/all_gather | solution.py:244
  11.0 36.4 %copy-start.4 = (bf16[512,128]{1,0:T(8,128)(2,1)}, bf16[512,128]{1,0:T(8,128)(2,1)S(1)}, u32[]{:S(2)}) copy-start(bf16[512,128]{1,0:T(8,128)(2,1)S(1)} %convert_element_type.35.u_ref) | copy-start | bytes 393220
  12.1 20.4 %all-to-all-start = ((s32[128,1,128]{2,1,0:T(1,128)}), s32[128,1,128]{2,1,0:T(1,128)S(1)}, u32[]{:S(2)}, u32[]{:S(2)}) async-start(s32[128,1,128]{2,1,0:T(1,128)} %bitcast), calls=%async_computation | async-start | bytes 131072 | tf_op jit(solution)/shard_map/all_to_all | solution.py:238
  32.5 0.6 copy-start.6
  65.3 9.9 %copy-start = (bf16[4096,160]{1,0:T(8,128)(2,1)S(1)}, bf16[4096,160]{1,0:T(8,128)(2,1)}, u32[]{:S(2)}) copy-start(bf16[4096,160]{1,0:T(8,128)(2,1)} %all-gather.3.cloned.1.call-done) | copy-start | bytes 3932164
  65.3 87.8 %all-to-all-start.1 = ((bf16[128,128,128]{2,1,0:T(8,128)(2,1)}), bf16[128,128,128]{2,1,0:T(8,128)(2,1)}, u32[]{:S(2)}, u32[]{:S(2)}) async-start(bf16[128,128,128]{2,1,0:T(8,128)(2,1)} %bitcast.8), calls=%async_computation.1 | async-start | bytes 8388608 | tf_op jit(solution)/shard_map/all_to_all | solution.py:247
  75.0 109.1 %reduce-scatter.5.cloned.1.call-start = ((), (), s32[]{:S(2)}) async-start(), calls=%async_computation.8 | async-start | bytes 2621440 | tf_op jit(solution)/shard_map/reduce_scatter | solution.py:265
  75.2 2.0 copy-start.1
  153.2 30.9 %copy-start.12 = (s32[1,128]{1,0:T(1,128)S(1)}, s32[1,128]{1,0:T(1,128)}, u32[]{:S(2)}) copy-start(s32[1,128]{1,0:T(1,128)} %param.17) | copy-start | bytes 1540
  153.2 110.9 %all-reduce.2.cloned.1.call-start = ((), (), s32[]{:S(2)}) async-start(), calls=%async_computation.9 | async-start | bytes 1048576 | tf_op jit(solution)/shard_map/psum | solution.py:266
  202.8 61.3 %all-to-all-start.2 = ((bf16[128,128,128]{2,1,0:T(8,128)(2,1)}), bf16[128,128,128]{2,1,0:T(8,128)(2,1)}, u32[]{:S(2)}, u32[]{:S(2)}) async-start(bf16[128,128,128]{2,1,0:T(8,128)(2,1)} %bitcast.9), calls=%async_computation.3 | async-start | bytes 8388608 | tf_op jit(solution)/shard_map/all_to_all | solution.py:271
  211.7 91.9 %reduce-scatter.3.cloned.1.call-start = ((), (), s32[]{:S(2)}) async-start(), calls=%async_computation.7 | async-start | bytes 2359296 | tf_op jit(solution)/shard_map/reduce_scatter | solution.py:267
  264.1 22.3 %copy-start.2 = (f32[1024,128]{1,0:T(8,128)S(1)}, f32[1024,128]{1,0:T(8,128)}, u32[]{:S(2)}) copy-start(f32[1024,128]{1,0:T(8,128)} %param.12) | copy-start | bytes 1572868
  264.1 22.3 %copy-start.7 = (f32[1024,128]{1,0:T(8,128)S(1)}, f32[1024,128]{1,0:T(8,128)}, u32[]{:S(2)}) copy-start(f32[1024,128]{1,0:T(8,128)} %param.15) | copy-start | bytes 1572868
  264.1 22.3 %copy-start.8 = (f32[1024,128]{1,0:T(8,128)S(1)}, f32[1024,128]{1,0:T(8,128)}, u32[]{:S(2)}) copy-start(f32[1024,128]{1,0:T(8,128)} %param.13) | copy-start | bytes 1572868
  264.1 22.3 %copy-start.9 = (f32[1024,128]{1,0:T(8,128)S(1)}, f32[1024,128]{1,0:T(8,128)}, u32[]{:S(2)}) copy-start(f32[1024,128]{1,0:T(8,128)} %all-reduce.2.cloned.1.call-done) | copy-start | bytes 1572868
  286.4 17.1 %copy-start.5 = (f32[512,128]{1,0:T(8,128)S(1)}, f32[512,128]{1,0:T(8,128)}, u32[]{:S(2)}) copy-start(f32[512,128]{1,0:T(8,128)} %param.9) | copy-start | bytes 786436
  286.4 17.1 %copy-start.10 = (f32[512,128]{1,0:T(8,128)S(1)}, f32[512,128]{1,0:T(8,128)}, u32[]{:S(2)}) copy-start(f32[512,128]{1,0:T(8,128)} %param.10) | copy-start | bytes 786436
  286.5 17.1 %copy-start.11 = (f32[512,128]{1,0:T(8,128)S(1)}, f32[512,128]{1,0:T(8,128)}, u32[]{:S(2)}) copy-start(f32[512,128]{1,0:T(8,128)} %get-tuple-element.29) | copy-start | bytes 786436
Sparse Core Ops, SparseCore 0:
  10.2 26.9 all-gather.4
  39.5 25.7 all-gather.2
  153.3 30.7 reduce-scatter.4
  186.3 77.0 all-reduce.1
  265.7 37.8 reduce-scatter.2

commit v7 on v5

--- a/solution.py
+++ b/solution.py
@@ -199,11 +199,16 @@
     live_slots = lax.iota(jnp.int32, slot_count)[None, :] < cold_counts.reshape(devices, 1)
     asked_rows = lax.all_to_all(requests, ("grp", "sa", "sb"), split_axis=0, concat_axis=0, tiled=True)
     found = onehot_gather(cold_half, asked_rows.reshape(-1))
+    sub_rows = positives.shape[0] * pos_count // LANES
     packed = jnp.concatenate(
-        [user_half, (positives // LANES).astype(jnp.bfloat16), (positives % LANES).astype(jnp.bfloat16)],
-        axis=1,
-    )
-    packed_part = lax.all_gather(packed, "sb", axis=0, tiled=True)
+        [
+            user_half,
+            (positives // LANES).reshape(sub_rows, LANES).astype(jnp.bfloat16),
+            (positives % LANES).reshape(sub_rows, LANES).astype(jnp.bfloat16),
+        ],
+        axis=0,
+    )
+    packed_part = lax.all_gather(packed, "sb", axis=0, tiled=False)
     hot_part = lax.all_gather(hot_half, "sa", axis=0, tiled=True)
     found, packed_part, hot_part = lax.optimization_barrier((found, packed_part, hot_part))
     fetched = lax.all_to_all(
@@ -213,14 +218,15 @@
         concat_axis=0,
         tiled=True,
     )
-    users_part = packed_part[:, :feature_count]
-    pos_hi = packed_part[:, feature_count:feature_count + pos_count].astype(jnp.int32)
-    pos_lo = packed_part[:, feature_count + pos_count:].astype(jnp.int32)
+    local_users = user_half.shape[0]
+    users_part = packed_part[:, :local_users].reshape(-1, feature_count)
+    pos_hi = packed_part[:, local_users:local_users + sub_rows].reshape(-1, LANES).astype(jnp.int32)
+    pos_lo = packed_part[:, local_users + sub_rows:].reshape(-1, LANES).astype(jnp.int32)
     hi_per_item = item_sub // LANES
     owner = pos_hi // hi_per_item
     local_hi = (owner // sb_count) * hi_per_item + pos_hi % hi_per_item
-    local = jnp.where(owner % sb_count == lax.axis_index("sb"), local_hi * LANES + pos_lo, hot_part.shape[0])
-    pos_hi_t, pos_lo_t = hot_prepare(local)
+    pos_hi_t = jnp.where(owner % sb_count == lax.axis_index("sb"), local_hi, hot_part.shape[0] // LANES)
+    pos_lo_t = pos_lo
     tiles = users_part.shape[0] // 512
     user_hot_part, item_part = hot_terms(users_part, pos_hi_t, pos_lo_t, hot_part, 0, tiles, found)
     fetched, user_hot_part, item_part = lax.optimization_barrier((fetched, user_hot_part, item_part))

time: 309 us -> 297 us (0.961)
  other arithmetic: 17.9 us -> 12.9 us
  local copies, waits for them, and re-layouts: 8.95 us -> 4.55 us
    select_n x2 -> x1, other arithmetic: 8.91 us -> 1.22 us  [body(): jnp.where(owner % sb_count == lax.axis_index('sb'), local_hi, hot_part.sh...]
    reshape x2 -> x0, local copies, waits for them, and re-layouts: 5.54 us -> none  [the longest x1 2.77 us: hot_prepare(): (positives // LANES).reshape(subtiles, width)]
  transfers between devices with their start and end apart: 8 -> 8, of which waited for: 5 -> 5; matrix products, arithmetic and copies ran while one was open for 19% -> 16% of each run, Pallas kernels for 33% -> 34%
where the time goes in v7:
time: 297 us; the launch traced here: 296 us
  Pallas kernels  100 us (34%)
  waiting for transfers between devices  99.2 us (33%)
  matrix products  35.2 us (12%)
  starting transfers between devices  30.1 us (10%)
  between operations  13.9 us (5%)
  other arithmetic  12.9 us (4%)
  local copies, waits for them, and re-layouts  4.55 us (2%)
    pallas_call x1, Pallas kernels, hot_terms(): pl.pallas_call(functools.partial(_hot_kernel, sub_users=sub_users, chaine...  64.1 us
    psum x1, waiting for transfers between devices, body(): hot_grad = lax.psum(item_grad, 'grp')  51.5 us
    pallas_call x1, Pallas kernels, onehot_scatter_add(): pl.pallas_call(_scatter_kernel, grid=(n // chunk,), in_specs=[pl.BlockSpe...  22.1 us
    reduce_scatter x1, waiting for transfers between devices, body(): lax.psum_scatter(item_part, 'sa', scatter_dimension=0, tiled=True)  17.3 us
    all_gather x1, waiting for transfers between devices, body(): packed_part = lax.all_gather(packed, 'sb', axis=0, tiled=False)  16.7 us
    pallas_call x1, Pallas kernels, onehot_gather(): pl.pallas_call(_gather_kernel, grid=(n // chunk,), in_specs=[pl.BlockSpec...  14.2 us
    dot_general x1, matrix products, body(): jnp.einsum('uk,rk->ur', user_half, flat_rows, preferred_element_type=jnp....  13.3 us
    dot_general x1, matrix products, body(): jnp.einsum('ur,uk->rk', weights, user_half, preferred_element_type=jnp.fl...  12.3 us
  transfers between devices with their start and end apart: 8, of which 5 were waited for; matrix products, arithmetic and copies ran while one was open for 16% of the time, Pallas kernels for 34%

profile of v7, /device:TPU:0, one launch (start us, length us, event | category | flops | bytes accessed | tf_op | source)
XLA Modules:
  0.0 296.3 jit_solution(6598543689372074473)
XLA Ops:
  7.2 0.0 all-gather.4.cloned.1.call-start
  7.2 1.8 convert_element_type.55
  9.0 0.0 all-gather.4.cloned.1.call-update
  9.0 0.0 all-gather.6.cloned.1.call-start
  9.1 0.8 fusion.10
  9.9 0.1 copy.17
  10.0 0.1 convert_element_type.52
  10.1 1.0 convert_element_type.50
  11.1 0.1 copy.18
  11.2 0.1 convert_element_type.54
  11.4 0.7 pad_maximum_fusion
  12.0 0.0 all-gather.6.cloned.1.call-update
  12.1 11.2 %all-to-all-start = ((s32[128,1,128]{2,1,0:T(1,128)}), s32[128,1,128]{2,1,0:T(1,128)S(1)}, u32[]{:S(2)}, u32[]{:S(2)}) async-start(s32[128,1,128]{2,1,0:T(1,128)} %bitcast.30), calls=%async_computation | async-start | bytes 131072 | tf_op jit(solution)/shard_map/all_to_all | solution.py:200
  23.2 1.8 convert_element_type.49.table_ref
  25.0 7.5 %all-to-all-done = s32[128,1,128]{2,1,0:T(1,128)S(1)} async-done(((s32[128,1,128]{2,1,0:T(1,128)}), s32[128,1,128]{2,1,0:T(1,128)S(1)}, u32[]{:S(2)}, u32[]{:S(2)}) %all-to-all-start) | async-done | bytes 65568 | tf_op jit(solution)/shard_map/all_to_all | solution.py:200
  32.5 0.0 copy-start.3
  32.5 0.6 copy-done.3
  33.1 14.2 %shard_map.136.dep_ref = bf16[16384,128]{1,0:T(8,128)(2,1)} custom-call(s32[1,16384]{1,0:T(1,128)} %bitcast.28, bf16[1024,128]{1,0:T(8,128)(2,1)} %convert_element_type.49.table_ref), custom_call_target="tpu_custom_call" | custom-call | tf_op jit(solution)/shard_map/pallas_call | solution.py:131
  47.3 0.0 all-gather.4.cloned.1.call-done.h_ref
  47.3 16.7 %all-gather.6.cloned.1.call-done = bf16[5120,128]{1,0:T(8,128)(2,1)} async-done(((bf16[640,128]{1,0:T(8,128)(2,1)}), bf16[5120,128]{1,0:T(8,128)(2,1)}) %all-gather.6.cloned.1.call-update) | async-done | bytes 1310736 | tf_op jit(solution)/shard_map/all_gather | solution.py:211
  64.0 9.3 %all-to-all-start.1 = ((bf16[128,128,128]{2,1,0:T(8,128)(2,1)}), bf16[128,128,128]{2,1,0:T(8,128)(2,1)}, u32[]{:S(2)}, u32[]{:S(2)}) async-start(bf16[128,128,128]{2,1,0:T(8,128)(2,1)} %bitcast.23), calls=%async_computation.1 | async-start | bytes 8388608 | tf_op jit(solution)/shard_map/all_to_all | solution.py:214
  73.3 0.0 reduce-scatter.3.cloned.1.call-start
  73.4 0.7 convert_bitcast_fusion
  74.1 2.4 slice.9
  76.5 1.0 fusion.14
  77.5 0.7 bitcast_convert_fusion.pl_ref
  78.2 1.2 fusion.5.ph_ref
  79.5 64.1 %shard_map.137 = (f32[4096,128]{1,0:T(8,128)}, f32[4096,128]{1,0:T(8,128)}) custom-call(bf16[4096,128]{1,0:T(8,128)(2,1)} %bitcast.25, bf16[4096,128]{1,0:T(8,128)(2,1)} %all-gather.4.cloned.1.call-done.h_ref, s32[512,128]{1,0:T(8,128)} %fusion.5.ph_ref, s32[512,128]{1,0:T(8,128)} %bitcast_convert_fusion.pl_ref, bf16[16384,128]{1,0:T(8,128)(2,1)} %shard_map.136.dep_ref), custom_call_target="tpu_custom_call" | custom-call | tf_op jit(solution)/shard_map/pallas_call | solution.py:101
  143.6 0.0 all-to-all-done.1
  143.6 0.0 reduce-scatter.3.cloned.1.call-update
  143.6 0.2 all-reduce.2.cloned.1.call-start
  143.8 13.3 %multiply_convert_fusion = bf16[16384,512]{1,0:T(8,128)(2,1)} fusion(bf16[16384,128]{1,0:T(8,128)(2,1)} %bitcast.8, bf16[512,128]{1,0:T(8,128)(2,1)S(1)} %convert_element_type.50, f32[16384]{0:T(1024)S(1)} %convert_bitcast_fusion), kind=kOutput, calls=%fused_computation | convolution fusion | flops 2189426688 | bytes 21168128 | tf_op jit(solution)/shard_map/uk,rk->ur/dot_general | solution.py:238
  157.2 17.3 %reduce-scatter.3.cloned.1.call-done = f32[1024,128]{1,0:T(8,128)} async-done(((f32[4096,128]{1,0:T(8,128)}), f32[1024,128]{1,0:T(8,128)}) %reduce-scatter.3.cloned.1.call-update) | async-done | bytes 524304 | tf_op jit(solution)/shard_map/reduce_scatter | solution.py:233
  174.5 0.0 all-reduce.2.cloned.1.call-update
  174.5 12.3 %convolution_convert_fusion = bf16[16384,128]{1,0:T(8,128)(2,1)} fusion(bf16[16384,512]{1,0:T(8,128)(2,1)} %multiply_convert_fusion, bf16[512,128]{1,0:T(8,128)(2,1)S(1)} %convert_element_type.50), kind=kOutput, calls=%fused_computation.1 | convolution fusion | flops 2149580800 | bytes 21102592 | tf_op jit(solution)/shard_map/ur,uk->rk/dot_general | solution.py:243
  186.8 8.9 %all-to-all-start.2 = ((bf16[128,128,128]{2,1,0:T(8,128)(2,1)}), bf16[128,128,128]{2,1,0:T(8,128)(2,1)}, u32[]{:S(2)}, u32[]{:S(2)}) async-start(bf16[128,128,128]{2,1,0:T(8,128)(2,1)} %bitcast.24), calls=%async_computation.4 | async-start | bytes 8388608 | tf_op jit(solution)/shard_map/all_to_all | solution.py:247
  195.7 0.3 reduce-scatter.5.cloned.1.call-start
  196.0 51.5 %all-reduce.2.cloned.1.call-done = f32[1024,128]{1,0:T(8,128)} async-done(((f32[1024,128]{1,0:T(8,128)}), f32[1024,128]{1,0:T(8,128)}) %all-reduce.2.cloned.1.call-update) | async-done | bytes 524304 | tf_op jit(solution)/shard_map/psum | solution.py:234
  247.4 0.0 reduce-scatter.5.cloned.1.call-update
  247.5 0.0 copy-start
  247.5 0.0 copy-start.1
  247.5 0.0 copy-start.4
  247.5 0.0 copy-start.5
  247.5 0.0 copy-start.6
  247.5 0.0 copy-start.2
  247.5 0.0 copy-start.7
  247.6 9.5 %fusion.15 = f32[512,128]{1,0:T(8,128)S(1)} fusion(bf16[16384,512]{1,0:T(8,128)(2,1)} %multiply_convert_fusion, bf16[16384,128]{1,0:T(8,128)(2,1)} %bitcast.8), kind=kOutput, calls=%fused_computation.47 | convolution fusion | flops 2147483648 | bytes 21233664 | tf_op jit(solution)/shard_map/dot_general | solution.py:242
  257.1 0.0 all-to-all-done.2
  257.1 22.1 %shard_map.138 = f32[1024,128]{1,0:T(8,128)} custom-call(s32[1,16384]{1,0:T(1,128)} %bitcast.29, bf16[16384,128]{1,0:T(8,128)(2,1)} %bitcast.12.val_ref), custom_call_target="tpu_custom_call" | custom-call | tf_op jit(solution)/shard_map/pallas_call | solution.py:160
  279.2 0.0 copy-done
  279.2 0.0 copy-done.1
  279.3 0.0 copy-done.4
  279.3 0.0 copy-done.5
  279.3 0.0 copy-done.6
  279.3 2.5 multiply_subtract_fusion
  281.7 6.2 %reduce-scatter.5.cloned.1.call-done = f32[512,128]{1,0:T(8,128)} async-done(((f32[4096,128]{1,0:T(8,128)}), f32[512,128]{1,0:T(8,128)}) %reduce-scatter.5.cloned.1.call-update) | async-done | bytes 262160 | tf_op jit(solution)/shard_map/reduce_scatter | solution.py:236
  287.9 0.0 copy-done.2
  287.9 0.0 copy-done.7
  287.9 1.8 multiply_subtract_fusion.2
Async XLA Ops:
  7.2 40.1 %all-gather.4.cloned.1.call-start = ((), (), s32[]{:S(2)}) async-start(), calls=%async_computation.5 | async-start | bytes 1310720 | tf_op jit(solution)/shard_map/all_gather | solution.py:212
  9.0 55.0 %all-gather.6.cloned.1.call-start = ((), (), s32[]{:S(2)}) async-start(), calls=%async_computation.9 | async-start | bytes 1474560 | tf_op jit(solution)/shard_map/all_gather | solution.py:211
  12.1 20.4 %all-to-all-start = ((s32[128,1,128]{2,1,0:T(1,128)}), s32[128,1,128]{2,1,0:T(1,128)S(1)}, u32[]{:S(2)}, u32[]{:S(2)}) async-start(s32[128,1,128]{2,1,0:T(1,128)} %bitcast.30), calls=%async_computation | async-start | bytes 131072 | tf_op jit(solution)/shard_map/all_to_all | solution.py:200
  32.5 0.6 copy-start.3
  64.0 79.6 %all-to-all-start.1 = ((bf16[128,128,128]{2,1,0:T(8,128)(2,1)}), bf16[128,128,128]{2,1,0:T(8,128)(2,1)}, u32[]{:S(2)}, u32[]{:S(2)}) async-start(bf16[128,128,128]{2,1,0:T(8,128)(2,1)} %bitcast.23), calls=%async_computation.1 | async-start | bytes 8388608 | tf_op jit(solution)/shard_map/all_to_all | solution.py:214
  73.3 101.1 %reduce-scatter.3.cloned.1.call-start = ((), (), s32[]{:S(2)}) async-start(), calls=%async_computation.6 | async-start | bytes 2621440 | tf_op jit(solution)/shard_map/reduce_scatter | solution.py:233
  143.6 103.9 %all-reduce.2.cloned.1.call-start = ((), (), s32[]{:S(2)}) async-start(), calls=%async_computation.7 | async-start | bytes 1048576 | tf_op jit(solution)/shard_map/psum | solution.py:234
  186.8 70.3 %all-to-all-start.2 = ((bf16[128,128,128]{2,1,0:T(8,128)(2,1)}), bf16[128,128,128]{2,1,0:T(8,128)(2,1)}, u32[]{:S(2)}, u32[]{:S(2)}) async-start(bf16[128,128,128]{2,1,0:T(8,128)(2,1)} %bitcast.24), calls=%async_computation.4 | async-start | bytes 8388608 | tf_op jit(solution)/shard_map/all_to_all | solution.py:247
  195.7 92.2 %reduce-scatter.5.cloned.1.call-start = ((), (), s32[]{:S(2)}) async-start(), calls=%async_computation.8 | async-start | bytes 2359296 | tf_op jit(solution)/shard_map/reduce_scatter | solution.py:236
  247.5 31.8 %copy-start = (f32[1024,128]{1,0:T(8,128)S(1)}, f32[1024,128]{1,0:T(8,128)}, u32[]{:S(2)}) copy-start(f32[1024,128]{1,0:T(8,128)} %param.12) | copy-start | bytes 1572868
  247.5 31.8 %copy-start.1 = (f32[1024,128]{1,0:T(8,128)S(1)}, f32[1024,128]{1,0:T(8,128)}, u32[]{:S(2)}) copy-start(f32[1024,128]{1,0:T(8,128)} %param.14) | copy-start | bytes 1572868
  247.5 31.8 %copy-start.4 = (f32[1024,128]{1,0:T(8,128)S(1)}, f32[1024,128]{1,0:T(8,128)}, u32[]{:S(2)}) copy-start(f32[1024,128]{1,0:T(8,128)} %param.15) | copy-start | bytes 1572868
  247.5 31.8 %copy-start.5 = (f32[1024,128]{1,0:T(8,128)S(1)}, f32[1024,128]{1,0:T(8,128)}, u32[]{:S(2)}) copy-start(f32[1024,128]{1,0:T(8,128)} %param.13) | copy-start | bytes 1572868
  247.5 31.7 %copy-start.6 = (f32[1024,128]{1,0:T(8,128)S(1)}, f32[1024,128]{1,0:T(8,128)}, u32[]{:S(2)}) copy-start(f32[1024,128]{1,0:T(8,128)} %all-reduce.2.cloned.1.call-done) | copy-start | bytes 1572868
  247.5 40.4 %copy-start.2 = (f32[512,128]{1,0:T(8,128)S(1)}, f32[512,128]{1,0:T(8,128)}, u32[]{:S(2)}) copy-start(f32[512,128]{1,0:T(8,128)} %param.9) | copy-start | bytes 786436
  247.5 40.4 %copy-start.7 = (f32[512,128]{1,0:T(8,128)S(1)}, f32[512,128]{1,0:T(8,128)}, u32[]{:S(2)}) copy-start(f32[512,128]{1,0:T(8,128)} %param.10) | copy-start | bytes 786436
Sparse Core Ops, SparseCore 0:
  10.2 26.9 all-gather.3
  39.5 24.4 all-gather.5
  143.7 30.7 reduce-scatter.2
  176.7 70.7 all-reduce.1
  249.7 38.2 reduce-scatter.4

commit v8 on v7

--- a/solution.py
+++ b/solution.py
@@ -230,8 +230,8 @@
     tiles = users_part.shape[0] // 512
     user_hot_part, item_part = hot_terms(users_part, pos_hi_t, pos_lo_t, hot_part, 0, tiles, found)
     fetched, user_hot_part, item_part = lax.optimization_barrier((fetched, user_hot_part, item_part))
-    item_grad = lax.psum_scatter(item_part, "sa", scatter_dimension=0, tiled=True)
-    hot_grad = lax.psum(item_grad, "grp")
+    item_grad = lax.psum_scatter(item_part, ("sa", "grp"), scatter_dimension=0, tiled=True)
+    hot_grad = lax.all_gather(item_grad, "grp", axis=0, tiled=True)
     user_hot_part, hot_grad = lax.optimization_barrier((user_hot_part, hot_grad))
     user_hot = lax.psum_scatter(user_hot_part, "sb", scatter_dimension=0, tiled=True)
     flat_rows = fetched.reshape(devices * slot_count, feature_count)

time: 297 us -> 313 us (1.054)
  blocking collectives: 0 us -> 13.5 us
  matrix products: 35.2 us -> 26.5 us
  local copies, waits for them, and re-layouts: 4.55 us -> 10.2 us
  waiting for transfers between devices: 99.2 us -> 104 us
    reduce_scatter x1, waiting for transfers between devices: 17.3 us -> 79.7 us  [body(): lax.psum_scatter(item_part, ('sa', 'grp'), scatter_dimension=0, tiled=True)]
    psum x1 -> x0, waiting for transfers between devices: 51.5 us -> none  [body(): hot_grad = lax.psum(item_grad, 'grp')]
    all_gather x0 -> x1, blocking collectives: none -> 13.5 us  [body(): hot_grad = lax.all_gather(item_grad, 'grp', axis=0, tiled=True)]
    dot_general x1, matrix products: 12.3 us -> 6.04 us  [body(): jnp.einsum('ur,uk->rk', weights, user_half, preferred_element_type=jnp.fl...]
    reduce_scatter x1, waiting for transfers between devices: 6.2 us -> 0.01 us  [body(): lax.psum_scatter(user_hot_part, 'sb', scatter_dimension=0, tiled=True)]
    unnamed x16, local copies, waits for them, and re-layouts: 0.67 us -> 6.39 us
  transfers between devices with their start and end apart: 8 -> 7, of which waited for: 5 -> 3; matrix products, arithmetic and copies ran while one was open for 16% -> 13% of each run, Pallas kernels for 34% -> 32%
where the time goes in v8:
time: 313 us; the launch traced here: 312 us
  waiting for transfers between devices  104 us (33%)
  Pallas kernels  100 us (32%)
  starting transfers between devices  31.1 us (10%)
  matrix products  26.5 us (8%)
  between operations  13.9 us (4%)
  blocking collectives  13.5 us (4%)
  other arithmetic  13 us (4%)
  local copies, waits for them, and re-layouts  10.2 us (3%)
    reduce_scatter x1, waiting for transfers between devices, body(): lax.psum_scatter(item_part, ('sa', 'grp'), scatter_dimension=0, tiled=True)  79.7 us
    pallas_call x1, Pallas kernels, hot_terms(): pl.pallas_call(functools.partial(_hot_kernel, sub_users=sub_users, chaine...  64.1 us
    pallas_call x1, Pallas kernels, onehot_scatter_add(): pl.pallas_call(_scatter_kernel, grid=(n // chunk,), in_specs=[pl.BlockSpe...  22.1 us
    all_gather x1, waiting for transfers between devices, body(): packed_part = lax.all_gather(packed, 'sb', axis=0, tiled=False)  16.7 us
    pallas_call x1, Pallas kernels, onehot_gather(): pl.pallas_call(_gather_kernel, grid=(n // chunk,), in_specs=[pl.BlockSpec...  14.2 us
    all_gather x1, blocking collectives, body(): hot_grad = lax.all_gather(item_grad, 'grp', axis=0, tiled=True)  13.5 us
    all_to_all x1, starting transfers between devices, body(): lax.all_to_all(requests, ('grp', 'sa', 'sb'), split_axis=0, concat_axis=0...  11.2 us
    dot_general x1, matrix products, body(): jnp.einsum('uk,rk->ur', user_half, flat_rows, preferred_element_type=jnp....  10.9 us
  transfers between devices with their start and end apart: 7, of which 3 were waited for; matrix products, arithmetic and copies ran while one was open for 13% of the time, Pallas kernels for 32%

profile of v8, /device:TPU:0, one launch (start us, length us, event | category | flops | bytes accessed | tf_op | source)
XLA Modules:
  0.0 312.5 jit_solution(2839735879453926171)
XLA Ops:
  7.2 0.0 all-gather.4.cloned.1.call-start
  7.2 1.8 convert_element_type.55
  9.0 0.0 all-gather.4.cloned.1.call-update
  9.0 0.0 all-gather.6.cloned.1.call-start
  9.1 0.8 fusion.10
  9.9 0.1 copy.17
  10.0 0.1 convert_element_type.52
  10.1 1.0 convert_element_type.50
  11.1 0.1 copy.18
  11.2 0.1 convert_element_type.54
  11.4 0.7 pad_maximum_fusion
  12.0 0.0 all-gather.6.cloned.1.call-update
  12.1 11.2 %all-to-all-start = ((s32[128,1,128]{2,1,0:T(1,128)}), s32[128,1,128]{2,1,0:T(1,128)S(1)}, u32[]{:S(2)}, u32[]{:S(2)}) async-start(s32[128,1,128]{2,1,0:T(1,128)} %bitcast.30), calls=%async_computation | async-start | bytes 131072 | tf_op jit(solution)/shard_map/all_to_all | solution.py:200
  23.2 1.8 convert_element_type.49.table_ref
  25.0 7.5 %all-to-all-done = s32[128,1,128]{2,1,0:T(1,128)S(1)} async-done(((s32[128,1,128]{2,1,0:T(1,128)}), s32[128,1,128]{2,1,0:T(1,128)S(1)}, u32[]{:S(2)}, u32[]{:S(2)}) %all-to-all-start) | async-done | bytes 65568 | tf_op jit(solution)/shard_map/all_to_all | solution.py:200
  32.5 0.0 copy-start.4
  32.5 0.6 copy-done.4
  33.1 14.2 %shard_map.136.dep_ref = bf16[16384,128]{1,0:T(8,128)(2,1)} custom-call(s32[1,16384]{1,0:T(1,128)} %bitcast.28, bf16[1024,128]{1,0:T(8,128)(2,1)} %convert_element_type.49.table_ref), custom_call_target="tpu_custom_call" | custom-call | tf_op jit(solution)/shard_map/pallas_call | solution.py:131
  47.3 0.0 all-gather.4.cloned.1.call-done.h_ref
  47.3 16.7 %all-gather.6.cloned.1.call-done = bf16[5120,128]{1,0:T(8,128)(2,1)} async-done(((bf16[640,128]{1,0:T(8,128)(2,1)}), bf16[5120,128]{1,0:T(8,128)(2,1)}) %all-gather.6.cloned.1.call-update) | async-done | bytes 1310736 | tf_op jit(solution)/shard_map/all_gather | solution.py:211
  64.0 9.3 %all-to-all-start.1 = ((bf16[128,128,128]{2,1,0:T(8,128)(2,1)}), bf16[128,128,128]{2,1,0:T(8,128)(2,1)}, u32[]{:S(2)}, u32[]{:S(2)}) async-start(bf16[128,128,128]{2,1,0:T(8,128)(2,1)} %bitcast.23), calls=%async_computation.1 | async-start | bytes 8388608 | tf_op jit(solution)/shard_map/all_to_all | solution.py:214
  73.3 0.2 reduce-scatter.3.cloned.1.call-start
  73.6 0.7 convert_bitcast_fusion
  74.3 2.3 slice.9
  76.6 1.0 fusion.14
  77.6 0.7 bitcast_convert_fusion.pl_ref
  78.3 1.2 fusion.5.ph_ref
  79.5 64.1 %shard_map.137 = (f32[4096,128]{1,0:T(8,128)}, f32[4096,128]{1,0:T(8,128)}) custom-call(bf16[4096,128]{1,0:T(8,128)(2,1)} %bitcast.25, bf16[4096,128]{1,0:T(8,128)(2,1)} %all-gather.4.cloned.1.call-done.h_ref, s32[512,128]{1,0:T(8,128)} %fusion.5.ph_ref, s32[512,128]{1,0:T(8,128)} %bitcast_convert_fusion.pl_ref, bf16[16384,128]{1,0:T(8,128)(2,1)} %shard_map.136.dep_ref), custom_call_target="tpu_custom_call" | custom-call | tf_op jit(solution)/shard_map/pallas_call | solution.py:101
  143.6 0.0 all-to-all-done.1
  143.6 0.0 reduce-scatter.3.cloned.1.call-update
  143.7 10.9 %multiply_convert_fusion = bf16[16384,512]{1,0:T(8,128)(2,1)S(1)} fusion(bf16[16384,128]{1,0:T(8,128)(2,1)} %bitcast.8, bf16[512,128]{1,0:T(8,128)(2,1)S(1)} %convert_element_type.50, f32[16384]{0:T(1024)S(1)} %convert_bitcast_fusion), kind=kOutput, calls=%fused_computation | convolution fusion | flops 2189426688 | bytes 21168128 | tf_op jit(solution)/shard_map/uk,rk->ur/dot_general | solution.py:238
  154.6 0.0 copy-start
  154.6 5.7 %copy-done = bf16[16384,512]{1,0:T(8,128)(2,1)} copy-done((bf16[16384,512]{1,0:T(8,128)(2,1)}, bf16[16384,512]{1,0:T(8,128)(2,1)S(1)}, u32[]{:S(2)}) %copy-start) | copy-done | bytes 16777240
  160.3 6.0 %convolution_convert_fusion = bf16[16384,128]{1,0:T(8,128)(2,1)} fusion(bf16[16384,512]{1,0:T(8,128)(2,1)S(1)} %multiply_convert_fusion, bf16[512,128]{1,0:T(8,128)(2,1)S(1)} %convert_element_type.50), kind=kOutput, calls=%fused_computation.1 | convolution fusion | flops 2149580800 | bytes 21102592 | tf_op jit(solution)/shard_map/ur,uk->rk/dot_general | solution.py:243
  166.3 10.2 %all-to-all-start.2 = ((bf16[128,128,128]{2,1,0:T(8,128)(2,1)}), bf16[128,128,128]{2,1,0:T(8,128)(2,1)}, u32[]{:S(2)}, u32[]{:S(2)}) async-start(bf16[128,128,128]{2,1,0:T(8,128)(2,1)} %bitcast.24), calls=%async_computation.4 | async-start | bytes 8388608 | tf_op jit(solution)/shard_map/all_to_all | solution.py:247
  176.6 0.0 reduce-scatter.5.cloned.1.call-start
  176.6 79.7 %reduce-scatter.3.cloned.1.call-done = f32[256,128]{1,0:T(8,128)} async-done(((f32[4096,128]{1,0:T(8,128)}), f32[256,128]{1,0:T(8,128)}) %reduce-scatter.3.cloned.1.call-update) | async-done | bytes 131088 | tf_op jit(solution)/shard_map/reduce_scatter | solution.py:233
  256.3 13.5 %all_gather.15 = f32[1024,128]{1,0:T(8,128)S(1)} all-gather(f32[256,128]{1,0:T(8,128)} %reduce-scatter.3.cloned.1.call-done), channel_id=1, replica_groups=mesh['grp'=4,'sa'=4,'sb'=8] {'grp'}, dimensions={0}, use_global_device_ids=true | all-gather | bytes 655360 | tf_op jit(solution)/shard_map/all_gather | solution.py:234
  269.8 0.0 reduce-scatter.5.cloned.1.call-update
  269.9 0.0 copy-start.1
  269.9 0.0 copy-start.2
  269.9 0.0 copy-start.5
  269.9 0.0 copy-start.6
  269.9 0.0 copy-start.3
  269.9 0.0 copy-start.7
  269.9 9.5 %fusion.15 = f32[512,128]{1,0:T(8,128)S(1)} fusion(bf16[16384,512]{1,0:T(8,128)(2,1)} %copy-done, bf16[16384,128]{1,0:T(8,128)(2,1)} %bitcast.8), kind=kOutput, calls=%fused_computation.47 | convolution fusion | flops 2147483648 | bytes 21233664 | tf_op jit(solution)/shard_map/dot_general | solution.py:242
  279.5 0.0 all-to-all-done.2
  279.5 22.1 %shard_map.138 = f32[1024,128]{1,0:T(8,128)} custom-call(s32[1,16384]{1,0:T(1,128)} %bitcast.29, bf16[16384,128]{1,0:T(8,128)(2,1)} %bitcast.12.val_ref), custom_call_target="tpu_custom_call" | custom-call | tf_op jit(solution)/shard_map/pallas_call | solution.py:160
  301.6 0.0 copy-done.1
  301.6 0.0 copy-done.2
  301.6 0.0 copy-done.5
  301.6 0.0 copy-done.6
  301.7 2.5 multiply_subtract_fusion
  304.1 0.0 reduce-scatter.5.cloned.1.call-done
  304.1 0.0 copy-done.3
  304.1 0.0 copy-done.7
  304.1 1.8 multiply_subtract_fusion.2
Async XLA Ops:
  7.2 40.1 %all-gather.4.cloned.1.call-start = ((), (), s32[]{:S(2)}) async-start(), calls=%async_computation.5 | async-start | bytes 1310720 | tf_op jit(solution)/shard_map/all_gather | solution.py:212
  9.0 55.0 %all-gather.6.cloned.1.call-start = ((), (), s32[]{:S(2)}) async-start(), calls=%async_computation.8 | async-start | bytes 1474560 | tf_op jit(solution)/shard_map/all_gather | solution.py:211
  12.1 20.4 %all-to-all-start = ((s32[128,1,128]{2,1,0:T(1,128)}), s32[128,1,128]{2,1,0:T(1,128)S(1)}, u32[]{:S(2)}, u32[]{:S(2)}) async-start(s32[128,1,128]{2,1,0:T(1,128)} %bitcast.30), calls=%async_computation | async-start | bytes 131072 | tf_op jit(solution)/shard_map/all_to_all | solution.py:200
  32.5 0.6 copy-start.4
  64.0 79.6 %all-to-all-start.1 = ((bf16[128,128,128]{2,1,0:T(8,128)(2,1)}), bf16[128,128,128]{2,1,0:T(8,128)(2,1)}, u32[]{:S(2)}, u32[]{:S(2)}) async-start(bf16[128,128,128]{2,1,0:T(8,128)(2,1)} %bitcast.23), calls=%async_computation.1 | async-start | bytes 8388608 | tf_op jit(solution)/shard_map/all_to_all | solution.py:214
  73.3 183.0 %reduce-scatter.3.cloned.1.call-start = ((), (), s32[]{:S(2)}) async-start(), calls=%async_computation.6 | async-start | bytes 2228224 | tf_op jit(solution)/shard_map/reduce_scatter | solution.py:233
  154.6 5.7 %copy-start = (bf16[16384,512]{1,0:T(8,128)(2,1)}, bf16[16384,512]{1,0:T(8,128)(2,1)S(1)}, u32[]{:S(2)}) copy-start(bf16[16384,512]{1,0:T(8,128)(2,1)S(1)} %multiply_convert_fusion) | copy-start | bytes 50331652
  166.3 113.2 %all-to-all-start.2 = ((bf16[128,128,128]{2,1,0:T(8,128)(2,1)}), bf16[128,128,128]{2,1,0:T(8,128)(2,1)}, u32[]{:S(2)}, u32[]{:S(2)}) async-start(bf16[128,128,128]{2,1,0:T(8,128)(2,1)} %bitcast.24), calls=%async_computation.4 | async-start | bytes 8388608 | tf_op jit(solution)/shard_map/all_to_all | solution.py:247
  176.6 127.6 %reduce-scatter.5.cloned.1.call-start = ((), (), s32[]{:S(2)}) async-start(), calls=%async_computation.7 | async-start | bytes 2359296 | tf_op jit(solution)/shard_map/reduce_scatter | solution.py:236
  269.9 31.8 %copy-start.1 = (f32[1024,128]{1,0:T(8,128)S(1)}, f32[1024,128]{1,0:T(8,128)}, u32[]{:S(2)}) copy-start(f32[1024,128]{1,0:T(8,128)} %param.12) | copy-start | bytes 1572868
  269.9 31.8 %copy-start.2 = (f32[1024,128]{1,0:T(8,128)S(1)}, f32[1024,128]{1,0:T(8,128)}, u32[]{:S(2)}) copy-start(f32[1024,128]{1,0:T(8,128)} %param.14) | copy-start | bytes 1572868
  269.9 31.7 %copy-start.5 = (f32[1024,128]{1,0:T(8,128)S(1)}, f32[1024,128]{1,0:T(8,128)}, u32[]{:S(2)}) copy-start(f32[1024,128]{1,0:T(8,128)} %param.15) | copy-start | bytes 1572868
  269.9 31.7 %copy-start.6 = (f32[1024,128]{1,0:T(8,128)S(1)}, f32[1024,128]{1,0:T(8,128)}, u32[]{:S(2)}) copy-start(f32[1024,128]{1,0:T(8,128)} %param.13) | copy-start | bytes 1572868
  269.9 34.2 %copy-start.3 = (f32[512,128]{1,0:T(8,128)S(1)}, f32[512,128]{1,0:T(8,128)}, u32[]{:S(2)}) copy-start(f32[512,128]{1,0:T(8,128)} %param.9) | copy-start | bytes 786436
  269.9 34.2 %copy-start.7 = (f32[512,128]{1,0:T(8,128)S(1)}, f32[512,128]{1,0:T(8,128)}, u32[]{:S(2)}) copy-start(f32[512,128]{1,0:T(8,128)} %param.10) | copy-start | bytes 786436
Sparse Core Ops, SparseCore 0:
  10.2 26.9 all-gather.3
  39.5 24.4 all-gather.5
  143.8 112.5 reduce-scatter.2
  270.0 32.4 reduce-scatter.4

commit v9 on v7

--- a/solution.py
+++ b/solution.py
@@ -231,8 +231,6 @@
     user_hot_part, item_part = hot_terms(users_part, pos_hi_t, pos_lo_t, hot_part, 0, tiles, found)
     fetched, user_hot_part, item_part = lax.optimization_barrier((fetched, user_hot_part, item_part))
     item_grad = lax.psum_scatter(item_part, "sa", scatter_dimension=0, tiled=True)
-    hot_grad = lax.psum(item_grad, "grp")
-    user_hot_part, hot_grad = lax.optimization_barrier((user_hot_part, hot_grad))
     user_hot = lax.psum_scatter(user_hot_part, "sb", scatter_dimension=0, tiled=True)
     flat_rows = fetched.reshape(devices * slot_count, feature_count)
     scores = jnp.einsum("uk,rk->ur", user_half, flat_rows, preferred_element_type=jnp.float32)
@@ -245,7 +243,10 @@
     ).astype(jnp.bfloat16)
     row_terms = row_terms.reshape(devices, slot_count, feature_count)
     returned = lax.all_to_all(row_terms, ("grp", "sa", "sb"), split_axis=0, concat_axis=0, tiled=True)
-    returned, user_cold = lax.optimization_barrier((returned, user_cold))
+    returned, user_cold, item_grad, user_hot = lax.optimization_barrier(
+        (returned, user_cold, item_grad, user_hot)
+    )
+    hot_grad = lax.psum(item_grad, "grp")
     cold_grad = onehot_scatter_add(
         asked_rows.reshape(-1),
         returned.reshape(devices * slot_count, feature_count),

time: 297 us -> 289 us (0.973)
  matrix products: 35.2 us -> 26.5 us
  waiting for transfers between devices: 99.2 us -> 91.5 us
  local copies, waits for them, and re-layouts: 4.55 us -> 10.2 us
    all_to_all x1, waiting for transfers between devices: 0.01 us -> 52.6 us  [body(): lax.all_to_all(row_terms, ('grp', 'sa', 'sb'), split_axis=0, concat_axis=...]
    psum x1, waiting for transfers between devices: 51.5 us -> 14.5 us  [body(): hot_grad = lax.psum(item_grad, 'grp')]
    reduce_scatter x1, waiting for transfers between devices: 17.3 us -> 0.01 us  [body(): lax.psum_scatter(item_part, 'sa', scatter_dimension=0, tiled=True)]
    dot_general x1, matrix products: 12.3 us -> 6.04 us  [body(): jnp.einsum('ur,uk->rk', weights, user_half, preferred_element_type=jnp.fl...]
    reduce_scatter x1, waiting for transfers between devices: 6.2 us -> 0.01 us  [body(): lax.psum_scatter(user_hot_part, 'sb', scatter_dimension=0, tiled=True)]
    unnamed x16 -> x18, local copies, waits for them, and re-layouts: 0.67 us -> 6.38 us
    sub x2 -> x3, other arithmetic: 4.26 us -> 6.01 us  [adagrad(): return (current - LEARN_RATE * gradient / jnp.sqrt(updated), updated)]
  transfers between devices with their start and end apart: 8 -> 8, of which waited for: 5 -> 4; matrix products, arithmetic and copies ran while one was open for 16% -> 14% of each run, Pallas kernels for 34% -> 35%
where the time goes in v9:
time: 289 us; the launch traced here: 288 us
  Pallas kernels  100 us (35%)
  waiting for transfers between devices  91.5 us (32%)
  starting transfers between devices  31.1 us (11%)
  matrix products  26.5 us (9%)
  other arithmetic  14 us (5%)
  between operations  13.9 us (5%)
  local copies, waits for them, and re-layouts  10.2 us (4%)
    pallas_call x1, Pallas kernels, hot_terms(): pl.pallas_call(functools.partial(_hot_kernel, sub_users=sub_users, chaine...  64.1 us
    all_to_all x1, waiting for transfers between devices, body(): lax.all_to_all(row_terms, ('grp', 'sa', 'sb'), split_axis=0, concat_axis=...  52.6 us
    pallas_call x1, Pallas kernels, onehot_scatter_add(): pl.pallas_call(_scatter_kernel, grid=(n // chunk,), in_specs=[pl.BlockSpe...  22.1 us
    all_gather x1, waiting for transfers between devices, body(): packed_part = lax.all_gather(packed, 'sb', axis=0, tiled=False)  16.7 us
    psum x1, waiting for transfers between devices, body(): hot_grad = lax.psum(item_grad, 'grp')  14.5 us
    pallas_call x1, Pallas kernels, onehot_gather(): pl.pallas_call(_gather_kernel, grid=(n // chunk,), in_specs=[pl.BlockSpec...  14.2 us
    all_to_all x1, starting transfers between devices, body(): lax.all_to_all(requests, ('grp', 'sa', 'sb'), split_axis=0, concat_axis=0...  11.2 us
    dot_general x1, matrix products, body(): jnp.einsum('uk,rk->ur', user_half, flat_rows, preferred_element_type=jnp....  10.9 us
  transfers between devices with their start and end apart: 8, of which 4 were waited for; matrix products, arithmetic and copies ran while one was open for 14% of the time, Pallas kernels for 35%

profile of v9, /device:TPU:0, one launch (start us, length us, event | category | flops | bytes accessed | tf_op | source)
XLA Modules:
  0.0 287.6 jit_solution(6188628814816508960)
XLA Ops:
  7.2 0.0 copy-start.8
  7.2 0.0 all-gather.4.cloned.1.call-start
  7.2 1.8 convert_element_type.55
  9.0 0.0 all-gather.4.cloned.1.call-update
  9.0 0.0 all-gather.6.cloned.1.call-start
  9.1 0.8 fusion.10
  9.9 0.1 copy.17
  10.0 0.1 convert_element_type.52
  10.1 1.0 convert_element_type.50
  11.1 0.1 copy.18
  11.2 0.1 convert_element_type.54
  11.4 0.7 pad_maximum_fusion
  12.0 0.0 all-gather.6.cloned.1.call-update
  12.1 11.2 %all-to-all-start = ((s32[128,1,128]{2,1,0:T(1,128)}), s32[128,1,128]{2,1,0:T(1,128)S(1)}, u32[]{:S(2)}, u32[]{:S(2)}) async-start(s32[128,1,128]{2,1,0:T(1,128)} %bitcast.30), calls=%async_computation | async-start | bytes 131072 | tf_op jit(solution)/shard_map/all_to_all | solution.py:200
  23.3 1.8 convert_element_type.49.table_ref
  25.0 7.5 %all-to-all-done = s32[128,1,128]{2,1,0:T(1,128)S(1)} async-done(((s32[128,1,128]{2,1,0:T(1,128)}), s32[128,1,128]{2,1,0:T(1,128)S(1)}, u32[]{:S(2)}, u32[]{:S(2)}) %all-to-all-start) | async-done | bytes 65568 | tf_op jit(solution)/shard_map/all_to_all | solution.py:200
  32.5 0.0 copy-start.4
  32.5 0.6 copy-done.4
  33.1 14.2 %shard_map.136.dep_ref = bf16[16384,128]{1,0:T(8,128)(2,1)} custom-call(s32[1,16384]{1,0:T(1,128)} %bitcast.28, bf16[1024,128]{1,0:T(8,128)(2,1)} %convert_element_type.49.table_ref), custom_call_target="tpu_custom_call" | custom-call | tf_op jit(solution)/shard_map/pallas_call | solution.py:131
  47.3 0.0 all-gather.4.cloned.1.call-done.h_ref
  47.3 16.7 %all-gather.6.cloned.1.call-done = bf16[5120,128]{1,0:T(8,128)(2,1)} async-done(((bf16[640,128]{1,0:T(8,128)(2,1)}), bf16[5120,128]{1,0:T(8,128)(2,1)}) %all-gather.6.cloned.1.call-update) | async-done | bytes 1310736 | tf_op jit(solution)/shard_map/all_gather | solution.py:211
  64.0 9.3 %all-to-all-start.1 = ((bf16[128,128,128]{2,1,0:T(8,128)(2,1)}), bf16[128,128,128]{2,1,0:T(8,128)(2,1)}, u32[]{:S(2)}, u32[]{:S(2)}) async-start(bf16[128,128,128]{2,1,0:T(8,128)(2,1)} %bitcast.23), calls=%async_computation.1 | async-start | bytes 8388608 | tf_op jit(solution)/shard_map/all_to_all | solution.py:214
  73.3 0.0 reduce-scatter.3.cloned.1.call-start
  73.4 2.3 slice.9
  75.7 1.0 fusion.14
  76.7 0.7 bitcast_convert_fusion.pl_ref
  77.4 1.2 fusion.5.ph_ref
  78.6 64.1 %shard_map.137 = (f32[4096,128]{1,0:T(8,128)}, f32[4096,128]{1,0:T(8,128)}) custom-call(bf16[4096,128]{1,0:T(8,128)(2,1)} %bitcast.25, bf16[4096,128]{1,0:T(8,128)(2,1)} %all-gather.4.cloned.1.call-done.h_ref, s32[512,128]{1,0:T(8,128)} %fusion.5.ph_ref, s32[512,128]{1,0:T(8,128)} %bitcast_convert_fusion.pl_ref, bf16[16384,128]{1,0:T(8,128)(2,1)} %shard_map.136.dep_ref), custom_call_target="tpu_custom_call" | custom-call | tf_op jit(solution)/shard_map/pallas_call | solution.py:101
  142.7 0.0 all-to-all-done.1
  142.7 0.0 reduce-scatter.3.cloned.1.call-update
  142.7 0.2 reduce-scatter.5.cloned.1.call-start
  143.0 0.0 copy-done.8
  143.0 0.1 convert_bitcast_fusion
  143.1 0.2 reduce-scatter.5.cloned.1.call-update
  143.3 10.9 %multiply_convert_fusion = bf16[16384,512]{1,0:T(8,128)(2,1)S(1)} fusion(bf16[16384,128]{1,0:T(8,128)(2,1)} %bitcast.8, bf16[512,128]{1,0:T(8,128)(2,1)S(1)} %convert_element_type.50, f32[16384]{0:T(1024)S(1)} %convert_bitcast_fusion), kind=kOutput, calls=%fused_computation | convolution fusion | flops 2189426688 | bytes 21168128 | tf_op jit(solution)/shard_map/uk,rk->ur/dot_general | solution.py:236
  154.2 0.0 copy-start
  154.2 5.7 %copy-done = bf16[16384,512]{1,0:T(8,128)(2,1)} copy-done((bf16[16384,512]{1,0:T(8,128)(2,1)}, bf16[16384,512]{1,0:T(8,128)(2,1)S(1)}, u32[]{:S(2)}) %copy-start) | copy-done | bytes 16777240
  159.9 6.0 %convolution_convert_fusion = bf16[16384,128]{1,0:T(8,128)(2,1)} fusion(bf16[16384,512]{1,0:T(8,128)(2,1)S(1)} %multiply_convert_fusion, bf16[512,128]{1,0:T(8,128)(2,1)S(1)} %convert_element_type.50), kind=kOutput, calls=%fused_computation.1 | convolution fusion | flops 2149580800 | bytes 21102592 | tf_op jit(solution)/shard_map/ur,uk->rk/dot_general | solution.py:241
  166.0 10.2 %all-to-all-start.2 = ((bf16[128,128,128]{2,1,0:T(8,128)(2,1)}), bf16[128,128,128]{2,1,0:T(8,128)(2,1)}, u32[]{:S(2)}, u32[]{:S(2)}) async-start(bf16[128,128,128]{2,1,0:T(8,128)(2,1)} %bitcast.24), calls=%async_computation.2 | async-start | bytes 8388608 | tf_op jit(solution)/shard_map/all_to_all | solution.py:245
  176.2 0.0 copy-start.3
  176.2 0.0 copy-start.7
  176.2 0.0 copy-start.1
  176.2 0.0 copy-start.5
  176.3 0.0 copy-start.2
  176.3 0.0 copy-start.6
  176.3 0.0 all-reduce.2.cloned.1.call-start
  176.3 9.5 %fusion.15 = f32[512,128]{1,0:T(8,128)S(1)} fusion(bf16[16384,512]{1,0:T(8,128)(2,1)} %copy-done, bf16[16384,128]{1,0:T(8,128)(2,1)} %bitcast.8), kind=kOutput, calls=%fused_computation.47 | convolution fusion | flops 2147483648 | bytes 21233664 | tf_op jit(solution)/shard_map/dot_general | solution.py:240
  185.9 52.6 %all-to-all-done.2 = bf16[128,128,128]{2,1,0:T(8,128)(2,1)} async-done(((bf16[128,128,128]{2,1,0:T(8,128)(2,1)}), bf16[128,128,128]{2,1,0:T(8,128)(2,1)}, u32[]{:S(2)}, u32[]{:S(2)}) %all-to-all-start.2) | async-done | bytes 4194336 | tf_op jit(solution)/shard_map/all_to_all | solution.py:245
  238.4 0.0 reduce-scatter.3.cloned.1.call-done
  238.4 0.0 reduce-scatter.5.cloned.1.call-done
  238.5 0.0 all-reduce.2.cloned.1.call-update
  238.5 22.1 %shard_map.138 = f32[1024,128]{1,0:T(8,128)} custom-call(s32[1,16384]{1,0:T(1,128)} %bitcast.29, bf16[16384,128]{1,0:T(8,128)(2,1)} %bitcast.12.val_ref), custom_call_target="tpu_custom_call" | custom-call | tf_op jit(solution)/shard_map/pallas_call | solution.py:160
  260.6 0.0 copy-done.3
  260.6 0.0 copy-done.7
  260.6 1.8 multiply_subtract_fusion.2
  262.4 0.0 copy-done.1
  262.4 0.0 copy-done.5
  262.4 2.1 multiply_subtract_fusion
  264.5 14.5 %all-reduce.2.cloned.1.call-done = f32[1024,128]{1,0:T(8,128)} async-done(((f32[1024,128]{1,0:T(8,128)}), f32[1024,128]{1,0:T(8,128)}) %all-reduce.2.cloned.1.call-update) | async-done | bytes 524304 | tf_op jit(solution)/shard_map/psum | solution.py:249
  279.0 0.0 copy-done.2
  279.0 0.0 copy-done.6
  279.0 2.1 multiply_subtract_fusion.1
Async XLA Ops:
  7.2 135.8 %copy-start.8 = (s32[1,128]{1,0:T(1,128)S(1)}, s32[1,128]{1,0:T(1,128)}, u32[]{:S(2)}) copy-start(s32[1,128]{1,0:T(1,128)} %param.17) | copy-start | bytes 1540
  7.2 40.1 %all-gather.4.cloned.1.call-start = ((), (), s32[]{:S(2)}) async-start(), calls=%async_computation.5 | async-start | bytes 1310720 | tf_op jit(solution)/shard_map/all_gather | solution.py:212
  9.0 55.0 %all-gather.6.cloned.1.call-start = ((), (), s32[]{:S(2)}) async-start(), calls=%async_computation.9 | async-start | bytes 1474560 | tf_op jit(solution)/shard_map/all_gather | solution.py:211
  12.1 20.4 %all-to-all-start = ((s32[128,1,128]{2,1,0:T(1,128)}), s32[128,1,128]{2,1,0:T(1,128)S(1)}, u32[]{:S(2)}, u32[]{:S(2)}) async-start(s32[128,1,128]{2,1,0:T(1,128)} %bitcast.30), calls=%async_computation | async-start | bytes 131072 | tf_op jit(solution)/shard_map/all_to_all | solution.py:200
  32.5 0.6 copy-start.4
  64.0 78.7 %all-to-all-start.1 = ((bf16[128,128,128]{2,1,0:T(8,128)(2,1)}), bf16[128,128,128]{2,1,0:T(8,128)(2,1)}, u32[]{:S(2)}, u32[]{:S(2)}) async-start(bf16[128,128,128]{2,1,0:T(8,128)(2,1)} %bitcast.23), calls=%async_computation.1 | async-start | bytes 8388608 | tf_op jit(solution)/shard_map/all_to_all | solution.py:214
  73.3 165.1 %reduce-scatter.3.cloned.1.call-start = ((), (), s32[]{:S(2)}) async-start(), calls=%async_computation.6 | async-start | bytes 2621440 | tf_op jit(solution)/shard_map/reduce_scatter | solution.py:233
  142.7 95.7 %reduce-scatter.5.cloned.1.call-start = ((), (), s32[]{:S(2)}) async-start(), calls=%async_computation.7 | async-start | bytes 2359296 | tf_op jit(solution)/shard_map/reduce_scatter | solution.py:234
  154.2 5.7 %copy-start = (bf16[16384,512]{1,0:T(8,128)(2,1)}, bf16[16384,512]{1,0:T(8,128)(2,1)S(1)}, u32[]{:S(2)}) copy-start(bf16[16384,512]{1,0:T(8,128)(2,1)S(1)} %multiply_convert_fusion) | copy-start | bytes 50331652
  166.0 72.5 %all-to-all-start.2 = ((bf16[128,128,128]{2,1,0:T(8,128)(2,1)}), bf16[128,128,128]{2,1,0:T(8,128)(2,1)}, u32[]{:S(2)}, u32[]{:S(2)}) async-start(bf16[128,128,128]{2,1,0:T(8,128)(2,1)} %bitcast.24), calls=%async_computation.2 | async-start | bytes 8388608 | tf_op jit(solution)/shard_map/all_to_all | solution.py:245
  176.2 84.4 %copy-start.3 = (f32[512,128]{1,0:T(8,128)S(1)}, f32[512,128]{1,0:T(8,128)}, u32[]{:S(2)}) copy-start(f32[512,128]{1,0:T(8,128)} %param.9) | copy-start | bytes 786436
  176.2 84.4 %copy-start.7 = (f32[512,128]{1,0:T(8,128)S(1)}, f32[512,128]{1,0:T(8,128)}, u32[]{:S(2)}) copy-start(f32[512,128]{1,0:T(8,128)} %param.10) | copy-start | bytes 786436
  176.2 86.2 %copy-start.1 = (f32[1024,128]{1,0:T(8,128)S(1)}, f32[1024,128]{1,0:T(8,128)}, u32[]{:S(2)}) copy-start(f32[1024,128]{1,0:T(8,128)} %param.14) | copy-start | bytes 1572868
  176.2 86.2 %copy-start.5 = (f32[1024,128]{1,0:T(8,128)S(1)}, f32[1024,128]{1,0:T(8,128)}, u32[]{:S(2)}) copy-start(f32[1024,128]{1,0:T(8,128)} %param.15) | copy-start | bytes 1572868
  176.3 102.7 %copy-start.2 = (f32[1024,128]{1,0:T(8,128)S(1)}, f32[1024,128]{1,0:T(8,128)}, u32[]{:S(2)}) copy-start(f32[1024,128]{1,0:T(8,128)} %param.12) | copy-start | bytes 1572868
  176.3 102.7 %copy-start.6 = (f32[1024,128]{1,0:T(8,128)S(1)}, f32[1024,128]{1,0:T(8,128)}, u32[]{:S(2)}) copy-start(f32[1024,128]{1,0:T(8,128)} %param.13) | copy-start | bytes 1572868
  176.3 102.7 %all-reduce.2.cloned.1.call-start = ((), (), s32[]{:S(2)}) async-start(), calls=%async_computation.8 | async-start | bytes 1048576 | tf_op jit(solution)/shard_map/psum | solution.py:249
Sparse Core Ops, SparseCore 0:
  10.2 26.9 all-gather.3
  39.5 24.4 all-gather.5
  142.9 30.7 reduce-scatter.2
  175.9 57.5 reduce-scatter.4
  238.6 40.3 all-reduce.1

commit v10 on v9

--- a/solution.py
+++ b/solution.py
@@ -155,7 +155,7 @@
     out_ref[...] += jnp.dot(onehot, val_ref[...], preferred_element_type=jnp.float32)
 
 
-def onehot_scatter_add(idx, values, rows, chunk=1024):
+def onehot_scatter_add(idx, values, rows, chunk=4096):
     n, k = values.shape
     return pl.pallas_call(
         _scatter_kernel,

time: 289 us -> 289 us (level)
  transfers between devices with their start and end apart: 8 -> 8, of which waited for: 4 -> 4; matrix products, arithmetic and copies ran while one was open for 14% -> 14% of each run, Pallas kernels for 35% -> 34%
where the time goes in v10:
time: 289 us; the launch traced here: 288 us
  Pallas kernels  98.3 us (34%)
  waiting for transfers between devices  93.6 us (32%)
  starting transfers between devices  31.1 us (11%)
  matrix products  26.5 us (9%)
  other arithmetic  14 us (5%)
  between operations  13.9 us (5%)
  local copies, waits for them, and re-layouts  10.2 us (4%)
    pallas_call x1, Pallas kernels, hot_terms(): pl.pallas_call(functools.partial(_hot_kernel, sub_users=sub_users, chaine...  64.1 us
    all_to_all x1, waiting for transfers between devices, body(): lax.all_to_all(row_terms, ('grp', 'sa', 'sb'), split_axis=0, concat_axis=...  52.6 us
    pallas_call x1, Pallas kernels, onehot_scatter_add(): pl.pallas_call(_scatter_kernel, grid=(n // chunk,), in_specs=[pl.BlockSpe...  20.1 us
    all_gather x1, waiting for transfers between devices, body(): packed_part = lax.all_gather(packed, 'sb', axis=0, tiled=False)  16.7 us
    psum x1, waiting for transfers between devices, body(): hot_grad = lax.psum(item_grad, 'grp')  16.5 us
    pallas_call x1, Pallas kernels, onehot_gather(): pl.pallas_call(_gather_kernel, grid=(n // chunk,), in_specs=[pl.BlockSpec...  14.2 us
    all_to_all x1, starting transfers between devices, body(): lax.all_to_all(requests, ('grp', 'sa', 'sb'), split_axis=0, concat_axis=0...  11.2 us
    dot_general x1, matrix products, body(): jnp.einsum('uk,rk->ur', user_half, flat_rows, preferred_element_type=jnp....  10.9 us
  transfers between devices with their start and end apart: 8, of which 4 were waited for; matrix products, arithmetic and copies ran while one was open for 14% of the time, Pallas kernels for 34%

profile of v10, /device:TPU:0, one launch (start us, length us, event | category | flops | bytes accessed | tf_op | source)
XLA Modules:
  0.0 287.6 jit_solution(545539132523241896)
XLA Ops:
  7.2 0.0 copy-start.8
  7.2 0.0 all-gather.4.cloned.1.call-start
  7.2 1.8 convert_element_type.55
  9.0 0.0 all-gather.4.cloned.1.call-update
  9.0 0.0 all-gather.6.cloned.1.call-start
  9.1 0.8 fusion.10
  9.9 0.1 copy.17
  10.0 0.1 convert_element_type.52
  10.1 1.0 convert_element_type.50
  11.1 0.1 copy.18
  11.2 0.1 convert_element_type.54
  11.4 0.7 pad_maximum_fusion
  12.0 0.0 all-gather.6.cloned.1.call-update
  12.1 11.2 %all-to-all-start = ((s32[128,1,128]{2,1,0:T(1,128)}), s32[128,1,128]{2,1,0:T(1,128)S(1)}, u32[]{:S(2)}, u32[]{:S(2)}) async-start(s32[128,1,128]{2,1,0:T(1,128)} %bitcast.30), calls=%async_computation | async-start | bytes 131072 | tf_op jit(solution)/shard_map/all_to_all | solution.py:200
  23.3 1.8 convert_element_type.49.table_ref
  25.0 7.5 %all-to-all-done = s32[128,1,128]{2,1,0:T(1,128)S(1)} async-done(((s32[128,1,128]{2,1,0:T(1,128)}), s32[128,1,128]{2,1,0:T(1,128)S(1)}, u32[]{:S(2)}, u32[]{:S(2)}) %all-to-all-start) | async-done | bytes 65568 | tf_op jit(solution)/shard_map/all_to_all | solution.py:200
  32.5 0.0 copy-start.4
  32.5 0.6 copy-done.4
  33.1 14.2 %shard_map.136.dep_ref = bf16[16384,128]{1,0:T(8,128)(2,1)} custom-call(s32[1,16384]{1,0:T(1,128)} %bitcast.28, bf16[1024,128]{1,0:T(8,128)(2,1)} %convert_element_type.49.table_ref), custom_call_target="tpu_custom_call" | custom-call | tf_op jit(solution)/shard_map/pallas_call | solution.py:131
  47.3 0.0 all-gather.4.cloned.1.call-done.h_ref
  47.3 16.7 %all-gather.6.cloned.1.call-done = bf16[5120,128]{1,0:T(8,128)(2,1)} async-done(((bf16[640,128]{1,0:T(8,128)(2,1)}), bf16[5120,128]{1,0:T(8,128)(2,1)}) %all-gather.6.cloned.1.call-update) | async-done | bytes 1310736 | tf_op jit(solution)/shard_map/all_gather | solution.py:211
  64.0 9.3 %all-to-all-start.1 = ((bf16[128,128,128]{2,1,0:T(8,128)(2,1)}), bf16[128,128,128]{2,1,0:T(8,128)(2,1)}, u32[]{:S(2)}, u32[]{:S(2)}) async-start(bf16[128,128,128]{2,1,0:T(8,128)(2,1)} %bitcast.23), calls=%async_computation.1 | async-start | bytes 8388608 | tf_op jit(solution)/shard_map/all_to_all | solution.py:214
  73.3 0.0 reduce-scatter.3.cloned.1.call-start
  73.4 2.3 slice.9
  75.7 1.0 fusion.14
  76.7 0.7 bitcast_convert_fusion.pl_ref
  77.4 1.2 fusion.5.ph_ref
  78.6 64.1 %shard_map.137 = (f32[4096,128]{1,0:T(8,128)}, f32[4096,128]{1,0:T(8,128)}) custom-call(bf16[4096,128]{1,0:T(8,128)(2,1)} %bitcast.25, bf16[4096,128]{1,0:T(8,128)(2,1)} %all-gather.4.cloned.1.call-done.h_ref, s32[512,128]{1,0:T(8,128)} %fusion.5.ph_ref, s32[512,128]{1,0:T(8,128)} %bitcast_convert_fusion.pl_ref, bf16[16384,128]{1,0:T(8,128)(2,1)} %shard_map.136.dep_ref), custom_call_target="tpu_custom_call" | custom-call | tf_op jit(solution)/shard_map/pallas_call | solution.py:101
  142.7 0.0 all-to-all-done.1
  142.7 0.0 reduce-scatter.3.cloned.1.call-update
  142.7 0.2 reduce-scatter.5.cloned.1.call-start
  143.0 0.0 copy-done.8
  143.0 0.1 convert_bitcast_fusion
  143.1 0.2 reduce-scatter.5.cloned.1.call-update
  143.3 10.9 %multiply_convert_fusion = bf16[16384,512]{1,0:T(8,128)(2,1)S(1)} fusion(bf16[16384,128]{1,0:T(8,128)(2,1)} %bitcast.8, bf16[512,128]{1,0:T(8,128)(2,1)S(1)} %convert_element_type.50, f32[16384]{0:T(1024)S(1)} %convert_bitcast_fusion), kind=kOutput, calls=%fused_computation | convolution fusion | flops 2189426688 | bytes 21168128 | tf_op jit(solution)/shard_map/uk,rk->ur/dot_general | solution.py:236
  154.2 0.0 copy-start
  154.2 5.7 %copy-done = bf16[16384,512]{1,0:T(8,128)(2,1)} copy-done((bf16[16384,512]{1,0:T(8,128)(2,1)}, bf16[16384,512]{1,0:T(8,128)(2,1)S(1)}, u32[]{:S(2)}) %copy-start) | copy-done | bytes 16777240
  159.9 6.0 %convolution_convert_fusion = bf16[16384,128]{1,0:T(8,128)(2,1)} fusion(bf16[16384,512]{1,0:T(8,128)(2,1)S(1)} %multiply_convert_fusion, bf16[512,128]{1,0:T(8,128)(2,1)S(1)} %convert_element_type.50), kind=kOutput, calls=%fused_computation.1 | convolution fusion | flops 2149580800 | bytes 21102592 | tf_op jit(solution)/shard_map/ur,uk->rk/dot_general | solution.py:241
  166.0 10.2 %all-to-all-start.2 = ((bf16[128,128,128]{2,1,0:T(8,128)(2,1)}), bf16[128,128,128]{2,1,0:T(8,128)(2,1)}, u32[]{:S(2)}, u32[]{:S(2)}) async-start(bf16[128,128,128]{2,1,0:T(8,128)(2,1)} %bitcast.24), calls=%async_computation.2 | async-start | bytes 8388608 | tf_op jit(solution)/shard_map/all_to_all | solution.py:245
  176.2 0.0 copy-start.3
  176.2 0.0 copy-start.7
  176.2 0.0 copy-start.1
  176.2 0.0 copy-start.5
  176.3 0.0 copy-start.2
  176.3 0.0 copy-start.6
  176.3 0.0 all-reduce.2.cloned.1.call-start
  176.3 9.5 %fusion.15 = f32[512,128]{1,0:T(8,128)S(1)} fusion(bf16[16384,512]{1,0:T(8,128)(2,1)} %copy-done, bf16[16384,128]{1,0:T(8,128)(2,1)} %bitcast.8), kind=kOutput, calls=%fused_computation.47 | convolution fusion | flops 2147483648 | bytes 21233664 | tf_op jit(solution)/shard_map/dot_general | solution.py:240
  185.9 52.6 %all-to-all-done.2 = bf16[128,128,128]{2,1,0:T(8,128)(2,1)} async-done(((bf16[128,128,128]{2,1,0:T(8,128)(2,1)}), bf16[128,128,128]{2,1,0:T(8,128)(2,1)}, u32[]{:S(2)}, u32[]{:S(2)}) %all-to-all-start.2) | async-done | bytes 4194336 | tf_op jit(solution)/shard_map/all_to_all | solution.py:245
  238.4 0.0 reduce-scatter.3.cloned.1.call-done
  238.4 0.0 reduce-scatter.5.cloned.1.call-done
  238.5 0.0 all-reduce.2.cloned.1.call-update
  238.5 20.1 %shard_map.138 = f32[1024,128]{1,0:T(8,128)} custom-call(s32[1,16384]{1,0:T(1,128)} %bitcast.29, bf16[16384,128]{1,0:T(8,128)(2,1)} %bitcast.12.val_ref), custom_call_target="tpu_custom_call" | custom-call | tf_op jit(solution)/shard_map/pallas_call | solution.py:160
  258.6 0.0 copy-done.3
  258.6 0.0 copy-done.7
  258.6 1.8 multiply_subtract_fusion.2
  260.4 0.0 copy-done.1
  260.4 0.0 copy-done.5
  260.4 2.1 multiply_subtract_fusion
  262.5 16.5 %all-reduce.2.cloned.1.call-done = f32[1024,128]{1,0:T(8,128)} async-done(((f32[1024,128]{1,0:T(8,128)}), f32[1024,128]{1,0:T(8,128)}) %all-reduce.2.cloned.1.call-update) | async-done | bytes 524304 | tf_op jit(solution)/shard_map/psum | solution.py:249
  279.0 0.0 copy-done.2
  279.0 0.0 copy-done.6
  279.0 2.1 multiply_subtract_fusion.1
Async XLA Ops:
  7.2 135.8 %copy-start.8 = (s32[1,128]{1,0:T(1,128)S(1)}, s32[1,128]{1,0:T(1,128)}, u32[]{:S(2)}) copy-start(s32[1,128]{1,0:T(1,128)} %param.17) | copy-start | bytes 1540
  7.2 40.1 %all-gather.4.cloned.1.call-start = ((), (), s32[]{:S(2)}) async-start(), calls=%async_computation.5 | async-start | bytes 1310720 | tf_op jit(solution)/shard_map/all_gather | solution.py:212
  9.0 55.0 %all-gather.6.cloned.1.call-start = ((), (), s32[]{:S(2)}) async-start(), calls=%async_computation.9 | async-start | bytes 1474560 | tf_op jit(solution)/shard_map/all_gather | solution.py:211
  12.1 20.4 %all-to-all-start = ((s32[128,1,128]{2,1,0:T(1,128)}), s32[128,1,128]{2,1,0:T(1,128)S(1)}, u32[]{:S(2)}, u32[]{:S(2)}) async-start(s32[128,1,128]{2,1,0:T(1,128)} %bitcast.30), calls=%async_computation | async-start | bytes 131072 | tf_op jit(solution)/shard_map/all_to_all | solution.py:200
  32.5 0.6 copy-start.4
  64.0 78.7 %all-to-all-start.1 = ((bf16[128,128,128]{2,1,0:T(8,128)(2,1)}), bf16[128,128,128]{2,1,0:T(8,128)(2,1)}, u32[]{:S(2)}, u32[]{:S(2)}) async-start(bf16[128,128,128]{2,1,0:T(8,128)(2,1)} %bitcast.23), calls=%async_computation.1 | async-start | bytes 8388608 | tf_op jit(solution)/shard_map/all_to_all | solution.py:214
  73.3 165.1 %reduce-scatter.3.cloned.1.call-start = ((), (), s32[]{:S(2)}) async-start(), calls=%async_computation.6 | async-start | bytes 2621440 | tf_op jit(solution)/shard_map/reduce_scatter | solution.py:233
  142.7 95.7 %reduce-scatter.5.cloned.1.call-start = ((), (), s32[]{:S(2)}) async-start(), calls=%async_computation.7 | async-start | bytes 2359296 | tf_op jit(solution)/shard_map/reduce_scatter | solution.py:234
  154.2 5.7 %copy-start = (bf16[16384,512]{1,0:T(8,128)(2,1)}, bf16[16384,512]{1,0:T(8,128)(2,1)S(1)}, u32[]{:S(2)}) copy-start(bf16[16384,512]{1,0:T(8,128)(2,1)S(1)} %multiply_convert_fusion) | copy-start | bytes 50331652
  166.0 72.5 %all-to-all-start.2 = ((bf16[128,128,128]{2,1,0:T(8,128)(2,1)}), bf16[128,128,128]{2,1,0:T(8,128)(2,1)}, u32[]{:S(2)}, u32[]{:S(2)}) async-start(bf16[128,128,128]{2,1,0:T(8,128)(2,1)} %bitcast.24), calls=%async_computation.2 | async-start | bytes 8388608 | tf_op jit(solution)/shard_map/all_to_all | solution.py:245
  176.2 82.4 %copy-start.3 = (f32[512,128]{1,0:T(8,128)S(1)}, f32[512,128]{1,0:T(8,128)}, u32[]{:S(2)}) copy-start(f32[512,128]{1,0:T(8,128)} %param.9) | copy-start | bytes 786436
  176.2 82.3 %copy-start.7 = (f32[512,128]{1,0:T(8,128)S(1)}, f32[512,128]{1,0:T(8,128)}, u32[]{:S(2)}) copy-start(f32[512,128]{1,0:T(8,128)} %param.10) | copy-start | bytes 786436
  176.2 84.1 %copy-start.1 = (f32[1024,128]{1,0:T(8,128)S(1)}, f32[1024,128]{1,0:T(8,128)}, u32[]{:S(2)}) copy-start(f32[1024,128]{1,0:T(8,128)} %param.14) | copy-start | bytes 1572868
  176.2 84.1 %copy-start.5 = (f32[1024,128]{1,0:T(8,128)S(1)}, f32[1024,128]{1,0:T(8,128)}, u32[]{:S(2)}) copy-start(f32[1024,128]{1,0:T(8,128)} %param.15) | copy-start | bytes 1572868
  176.3 102.7 %copy-start.2 = (f32[1024,128]{1,0:T(8,128)S(1)}, f32[1024,128]{1,0:T(8,128)}, u32[]{:S(2)}) copy-start(f32[1024,128]{1,0:T(8,128)} %param.12) | copy-start | bytes 1572868
  176.3 102.7 %copy-start.6 = (f32[1024,128]{1,0:T(8,128)S(1)}, f32[1024,128]{1,0:T(8,128)}, u32[]{:S(2)}) copy-start(f32[1024,128]{1,0:T(8,128)} %param.13) | copy-start | bytes 1572868
  176.3 102.7 %all-reduce.2.cloned.1.call-start = ((), (), s32[]{:S(2)}) async-start(), calls=%async_computation.8 | async-start | bytes 1048576 | tf_op jit(solution)/shard_map/psum | solution.py:249
Sparse Core Ops, SparseCore 0:
  10.2 26.9 all-gather.3
  39.5 24.4 all-gather.5
  142.9 30.7 reduce-scatter.2
  175.9 57.5 reduce-scatter.4
  238.6 40.3 all-reduce.1
